TPU v7x, 32 devices: a whole 2x2x4 slice. The times are simulated.
32 devices in a mesh: sub: 2 (over core), row: 4 (over y, x), col: 4 (over z).
Axes of the slice: x: 2, y: 2, z: 4, core: 2. Of those that a mesh axis runs over, the one named last changes fastest.
Arguments:
- child: float32 [2, 6144, 6144], P('sub', 'row', 'col'), may hold values from -1 to 1
- row_map: int32 [2, 48], replicated, may hold values from 0 to 79, as said below
- col_map: int32 [2, 48], replicated, may hold values from 0 to 79, as said below
- own_diagonal: float32 [10240], P(('sub', 'col')), may hold values from 96 to 192
- coupling: float32 [10240, 512], P('row'), may hold values from -24 to 24
Outputs:
- factored: float32 [10240, 10240], P('row', ('sub', 'col'))
Inputs may be any that keep to these rules, and one draw needn't show every extreme that they name: For each child s the entries row_map[s, :] are distinct front blocks, always including block 0 and block 79, and they rise strictly along k = (p % 12) * 4 + p // 12. col_map[s, :] holds the same set of front blocks as row_map[s, :]; they rise strictly along k = (q % 12) * 4 + (q // 12 + 1) % 4.
All inputs are finite; a program needn't handle non-finite values.
Results may differ from a plain program's by a relative error of at most 0.00005.
Values sent between devices are 32-bit elements; how exact they have to be, the bound alone decides.
No kernel may reach another device: no remote copies, remote signals or barrier semaphores. Data moves between devices by JAX's collectives and lax.ppermute only.
A program may use at most 320 MiB of HBM per device.

v0:
```python
import jax
import jax.numpy as jnp
from jax import lax
from jax.sharding import PartitionSpec as P

FRONT = 10240
PANEL = 512
BLOCK = 128


def from_root(value, axis, source):
    kept = jnp.where(lax.axis_index(axis) == source, value, 0).astype(value.dtype)
    return lax.psum(kept, axis)


def block_routes(parent_blocks, per_source, per_target):
    number = parent_blocks.shape[0]
    positions = jnp.arange(number, dtype=jnp.int32)
    source = positions // per_source
    target = parent_blocks // per_target
    earlier = (
        (source[:, None] == source[None, :])
        & (target[:, None] == target[None, :])
        & (positions[None, :] < positions[:, None])
    )
    slot_index = jnp.sum(earlier.astype(jnp.int32), axis=1)
    return (positions, source, target, slot_index, parent_blocks % per_target)


def sending_table(parent_blocks, own_index, per_source, per_target, targets, capacity):
    positions, source, target, slot_index, local_block = block_routes(
        parent_blocks, per_source, per_target
    )
    wanted = jnp.arange(targets * capacity, dtype=jnp.int32)
    matches = (source == own_index)[None, :] & (
        (target * capacity + slot_index)[None, :] == wanted[:, None]
    )
    within = positions % per_source
    return jnp.where(
        jnp.any(matches, axis=1),
        jnp.sum(jnp.where(matches, within[None, :], 0), axis=1),
        per_source,
    )


def receiving_table(parent_blocks, own_index, per_source, per_target, capacity, offset, empty_slot):
    positions, source, target, slot_index, local_block = block_routes(
        parent_blocks, per_source, per_target
    )
    wanted = jnp.arange(per_target, dtype=jnp.int32)
    matches = (target == own_index)[None, :] & (local_block[None, :] == wanted[:, None])
    flat_slot = (source + offset) * capacity + slot_index
    return jnp.where(
        jnp.any(matches, axis=1),
        jnp.sum(jnp.where(matches, flat_slot[None, :], 0), axis=1),
        empty_slot,
    )


def with_zero(blocks, axis):
    shape = list(blocks.shape)
    shape[axis] = 1
    return jnp.concatenate([blocks, jnp.zeros(shape, blocks.dtype)], axis=axis)


def symmetric_of(corner):
    return jnp.tril(corner) + jnp.tril(corner, -1).T


def factor_corner(corner):
    lower = jnp.linalg.cholesky(symmetric_of(corner))
    inverse = jax.scipy.linalg.solve_triangular(
        lower, jnp.eye(PANEL, dtype=jnp.float32), lower=True
    )
    return (lower, inverse)


def apply_inverse(rows, inverse):
    return lax.dot_general(rows, inverse, (((1,), (1,)), ((), ())), precision=lax.Precision.HIGHEST)


def shards(child, row_map, col_map, own_diagonal, coupling):
    n_row = lax.axis_size("row")
    n_col = lax.axis_size("col")
    n_group = lax.axis_size(("sub", "col"))
    my_row = lax.axis_index("row")
    my_col = lax.axis_index("col")
    my_sub = lax.axis_index("sub")
    my_group = lax.axis_index(("sub", "col"))
    child_piece = child[0]
    rows_here, cols_here = child_piece.shape
    front_rows = FRONT // n_row
    front_cols = FRONT // n_group
    row_blocks = rows_here // BLOCK
    col_blocks = cols_here // BLOCK
    front_row_blocks = front_rows // BLOCK
    front_col_blocks = front_cols // BLOCK
    row_cap = min(row_blocks, (front_row_blocks + n_row - 1) // n_row)
    col_cap = min(col_blocks, (front_col_blocks + n_col - 1) // n_col)
    my_rows_map = lax.dynamic_index_in_dim(row_map, my_sub, 0, keepdims=False)
    my_cols_map = lax.dynamic_index_in_dim(col_map, my_sub, 0, keepdims=False)
    padded = with_zero(child_piece.reshape(row_blocks, BLOCK, cols_here), 0)
    chosen = sending_table(my_rows_map, my_row, row_blocks, front_row_blocks, n_row, row_cap)
    outgoing = jnp.take(padded, chosen, axis=0).reshape(n_row, row_cap * BLOCK, cols_here)
    arrived = lax.all_to_all(outgoing, "row", split_axis=0, concat_axis=0, tiled=True)
    arrived = with_zero(arrived.reshape(n_row * row_cap, BLOCK, cols_here), 0)
    placement = receiving_table(
        my_rows_map, my_row, row_blocks, front_row_blocks, row_cap, 0, n_row * row_cap
    )
    front_rows_data = jnp.take(arrived, placement, axis=0).reshape(front_rows, col_blocks, BLOCK)
    padded = with_zero(front_rows_data, 1)
    chosen = sending_table(my_cols_map, my_col, col_blocks, front_col_blocks, n_group, col_cap)
    outgoing = jnp.take(padded, chosen, axis=1).reshape(front_rows, n_group, col_cap * BLOCK)
    arrived = lax.all_to_all(outgoing, ("sub", "col"), split_axis=1, concat_axis=1, tiled=True)
    arrived = with_zero(arrived.reshape(front_rows, n_group * col_cap, BLOCK), 1)
    assembled = jnp.zeros((front_rows, front_col_blocks, BLOCK), jnp.float32)
    for which in range(2):
        placement = receiving_table(
            col_map[which],
            my_group,
            col_blocks,
            front_col_blocks,
            col_cap,
            which * n_col,
            n_group * col_cap,
        )
        assembled = assembled + jnp.take(arrived, placement, axis=1)
    assembled = assembled.reshape(front_rows, front_cols)
    global_row = my_row * front_rows + jnp.arange(front_rows, dtype=jnp.int32)
    global_col = my_group * front_cols + jnp.arange(front_cols, dtype=jnp.int32)
    on_diagonal = global_row[:, None] == global_col[None, :]
    assembled = assembled + jnp.where(on_diagonal, own_diagonal[None, :], 0.0)
    coupling_wide = jnp.concatenate(
        [coupling, jnp.zeros((front_rows, front_cols - PANEL), jnp.float32)], axis=1
    )
    coupling_mask = (global_row[:, None] >= PANEL) & (global_col[None, :] < PANEL)
    front_part = assembled + jnp.where(coupling_mask, coupling_wide, 0.0)
    panel_cols = front_part[:, :PANEL]
    theirs_start = my_group * front_cols % front_rows
    theirs_root = my_group * front_cols // front_rows
    is_root = (my_row == 0) & (my_group == 0)
    corner = jnp.where(is_root, panel_cols[:PANEL], jnp.eye(PANEL, dtype=jnp.float32))
    lower, inverse = factor_corner(corner)
    factors = from_root(jnp.stack([lower, inverse]), "row", 0)
    lower = factors[0]
    inverse = factors[1]
    own_rows = apply_inverse(panel_cols, inverse)
    top_rows = jnp.where(my_row == 0, lower, own_rows[:PANEL])
    own_rows = jnp.concatenate([top_rows, own_rows[PANEL:]], axis=0)
    own_rows = from_root(own_rows, ("sub", "col"), 0)
    theirs = from_root(own_rows, "row", theirs_root)
    theirs = lax.dynamic_slice_in_dim(theirs, theirs_start, front_cols, 0)
    update = lax.dot_general(
        own_rows, theirs, (((1,), (1,)), ((), ())), precision=lax.Precision.HIGHEST
    )
    panel_wide = jnp.concatenate(
        [own_rows, jnp.zeros((front_rows, front_cols - PANEL), jnp.float32)], axis=1
    )
    trailing = front_part - update
    result = jnp.where(
        global_col[None, :] < PANEL,
        panel_wide,
        jnp.where(global_row[:, None] < PANEL, 0.0, trailing),
    )
    return result


def solution(mesh):
    placed = (P("sub", "row", "col"), P(), P(), P(("sub", "col")), P("row", None))
    return jax.shard_map(
        shards, mesh=mesh, in_specs=placed, out_specs=P("row", ("sub", "col")), check_vma=False
    )
```

profile of v0, /device:TPU:0, one launch (start us, length us, event | category | flops | bytes accessed | tf_op | source)
XLA Modules:
  0.0 1695.6 jit_solution(1360508496303780425)
XLA Ops:
  17.5 12.6 gather_fusion
  30.1 11.0 bitcast_select_fusion.1
  48.9 171.6 %all-to-all-done = f32[4,640,1536]{2,1,0:T(8,128)} async-done(((f32[4,640,1536]{2,1,0:T(8,128)}), f32[4,640,1536]{2,1,0:T(8,128)}, u32[]{:S(2)}, u32[]{:S(2)}) %all-to-all-start) | async-done | bytes 15728672 | tf_op jit(solution)/shard_map/all_to_all | solution.py:105
  220.5 11.4 concatenate.33
  231.9 15.2 gather_fusion.1
  247.1 19.2 %reshape.418 = f32[2560,12,128]{2,1,0:T(8,128)} reshape(f32[20,128,1536]{2,1,0:T(8,128)} %gather_fusion.1) | data formatting | bytes 31457280 | tf_op jit(solution)/shard_map/jit(_take)/gather | solution.py:110
  266.2 12.0 copy_select_fusion
  284.6 18.7 %gather_fusion.2 = f32[24,2560,128]{2,1,0:T(8,128)} fusion(f32[2560,13,128]{2,0,1:T(8,128)} %concatenate.34, s32[1024]{0:T(1024)S(1)} %pad_clamp_fusion.2), kind=kCustom, calls=%fused_computation.4 | custom fusion | bytes 62914656 | tf_op jit(solution)/shard_map/jit(_take)/gather | solution.py:113
  303.4 30.9 %copy.26 = f32[2560,24,128]{0,2,1:T(8,128)} copy(f32[2560,24,128]{2,0,1:T(8,128)} %bitcast.146) | data formatting | bytes 62914560 | tf_op jit(solution)/shard_map/jit(_take)/gather | solution.py:113
  334.2 21.8 %bitcast_select_fusion = f32[2560,8,384]{0,2,1:T(8,128)} fusion(pred[8,384]{1,0:T(8,128)(4,1)S(1)} %broadcast_bitcast_fusion.1, f32[2560,8,384]{0,2,1:T(8,128)} %bitcast.147), kind=kLoop, calls=%fused_computation.7 | loop fusion | flops 7864320 | bytes 62917632 | tf_op jit(solution)/shard_map/jit(_take)/select_n | solution.py:113
  364.1 676.6 %all-to-all-done.1 = f32[2560,8,384]{0,2,1:T(8,128)} async-done(((f32[2560,8,384]{0,2,1:T(8,128)}), f32[2560,8,384]{0,2,1:T(8,128)}, u32[]{:S(2)}, u32[]{:S(2)}) %all-to-all-start.1) | async-done | bytes 31457312 | tf_op jit(solution)/shard_map/all_to_all | solution.py:114
  1040.7 30.7 %copy.27 = f32[2560,24,128]{2,0,1:T(8,128)} copy(f32[2560,24,128]{0,2,1:T(8,128)} %bitcast.30) | data formatting | bytes 62914560 | tf_op jit(solution)/shard_map/reshape | solution.py:115
  1071.4 22.3 %concatenate.35 = f32[2560,25,128]{2,0,1:T(8,128)} pad(f32[2560,24,128]{2,0,1:T(8,128)} %copy.27, f32[]{:T(128)} %constant.313.clone.1), padding=0_0x0_1x0_0 | pad | bytes 64225284 | tf_op jit(solution)/shard_map/concatenate | solution.py:63
  1093.8 12.0 gather_fusion.3
  1105.7 11.7 gather_fusion.4
  1117.4 14.5 bitcast_add_fusion
  1131.9 14.0 copy.28
  1145.9 13.9 copy.29
  1175.9 11.7 cholesky.103
  1187.8 9.8 custom-call.31
  1200.1 11.7 cholesky.215
  1213.2 18.5 %custom-call.32 = f32[1,128,128]{1,2,0:T(8,128)S(1)} custom-call(f32[1,128,128]{2,1,0:T(8,128)S(1)} %get-tuple-element.56), custom_call_target="InvertDiagBlocksLowerTriangular" | custom-call | tf_op jit(solution)/shard_map/jit(cholesky)/cholesky | solution.py:71
  1233.3 11.7 cholesky.236
  1245.7 9.8 custom-call.33
  1256.9 11.9 cholesky.253
  1273.4 14.1 while.1
  1287.6 40.1 %custom-call.34 = f32[4,128,128]{1,2,0:T(8,128)S(1)} custom-call(f32[4,128,128]{2,1,0:T(8,128)} %get-tuple-element.13), custom_call_target="InvertDiagBlocksLowerTriangular" | custom-call | tf_op jit(solution)/shard_map/jit(_solve_triangular)/triangular_solve | solution.py:72
  1335.1 67.8 %all-reduce.11.cloned.1.call-done = f32[2,512,512]{2,1,0:T(8,128)} async-done(((f32[2,512,512]{2,1,0:T(8,128)}), f32[2,512,512]{2,1,0:T(8,128)}) %all-reduce.11.cloned.1.call-update) | async-done | bytes 2097168 | tf_op jit(solution)/shard_map/psum | solution.py:13
  1403.0 10.8 fusion.2
  1417.8 116.1 %all-reduce.13.cloned.1.call-done = f32[2560,512]{1,0:T(8,128)} async-done(((f32[2560,512]{1,0:T(8,128)}), f32[2560,512]{1,0:T(8,128)}) %all-reduce.13.cloned.1.call-update) | async-done | bytes 5242896 | tf_op jit(solution)/shard_map/psum | solution.py:13
  1539.5 120.9 %all-reduce.15.cloned.1.call-done = f32[2560,512]{1,0:T(8,128)} async-done(((f32[2560,512]{1,0:T(8,128)}), f32[2560,512]{1,0:T(8,128)}) %all-reduce.15.cloned.1.call-update) | async-done | bytes 5242896 | tf_op jit(solution)/shard_map/psum | solution.py:13
  1660.4 28.3 %fusion.1 = f32[2560,1280]{1,0:T(8,128)} fusion(f32[2560,1280]{1,0:T(8,128)} %copy-done, f32[2560,512]{1,0:T(8,128)} %all-reduce.13.cloned.1.call-done, pred[2560]{0:T(1024)(128)(4,1)S(1)} %fusion.47, pred[1280]{0:T(1024)(128)(4,1)S(1)} %broadcast_compare_fusion, f32[2560,512]{1,0:T(8,128)} %all-reduce.15.cloned.1.call-done, s32[]{:T(128)S(6)} %select_n.412), kind=kOutput, calls=%fused_computation.12 | convolution fusion | flops 20142489600 | bytes 39325444 | tf_op jit(solution)/shard_map/dot_general | solution.py:153
  (131 shorter events, 89.6 us)
Async XLA Ops:
  41.0 7.4 copy-start.4
  41.0 7.4 copy-start.5
  41.0 179.5 %all-to-all-start = ((f32[4,640,1536]{2,1,0:T(8,128)}), f32[4,640,1536]{2,1,0:T(8,128)}, u32[]{:S(2)}, u32[]{:S(2)}) async-start(f32[4,640,1536]{2,1,0:T(8,128)} %bitcast_select_fusion.1), calls=%async_computation | async-start | bytes 31457280 | tf_op jit(solution)/shard_map/all_to_all | solution.py:105
  356.0 684.7 %all-to-all-start.1 = ((f32[2560,8,384]{0,2,1:T(8,128)}), f32[2560,8,384]{0,2,1:T(8,128)}, u32[]{:S(2)}, u32[]{:S(2)}) async-start(f32[2560,8,384]{0,2,1:T(8,128)} %bitcast_select_fusion), calls=%async_computation.1 | async-start | bytes 62914560 | tf_op jit(solution)/shard_map/all_to_all | solution.py:114
  363.0 1040.0 %all-reduce.11.cloned.1.call-start = ((), (), s32[]{:S(2)}) async-start(), calls=%async_computation.2 | async-start | bytes 4194304 | tf_op jit(solution)/shard_map/psum | solution.py:13
  1145.9 13.9 copy-start.3
  1167.4 5.0 copy-start
  1174.9 1.0 copy-start.1
  1335.1 198.9 %all-reduce.13.cloned.1.call-start = ((), (), s32[]{:S(2)}) async-start(), calls=%async_computation.3 | async-start | bytes 10485760 | tf_op jit(solution)/shard_map/psum | solution.py:13
  1403.0 11.3 copy-start.2
  1417.5 242.9 %all-reduce.15.cloned.1.call-start = ((), (), s32[]{:S(2)}) async-start(), calls=%async_computation.4 | async-start | bytes 10485760 | tf_op jit(solution)/shard_map/psum | solution.py:13
Sparse Core Ops, SparseCore 0:
  1335.2 67.7 all-reduce.10
  1417.6 116.2 all-reduce.12
  1539.6 120.7 all-reduce.14
where the time goes:
time: 1710 us; the launch traced here: 1700 us
  waiting for transfers between devices  1150 us (67%)
  local copies, waits for them, and re-layouts  249 us (15%)
  other arithmetic  212 us (12%)
  matrix products  50.3 us (3%)
    all_to_all x1, waiting for transfers between devices, shards(): lax.all_to_all(outgoing, ('sub', 'col'), split_axis=1, concat_axis=1, til...  677 us
    psum x3, waiting for transfers between devices, from_root(): return lax.psum(kept, axis)  305 us
    all_to_all x1, waiting for transfers between devices, shards(): lax.all_to_all(outgoing, 'row', split_axis=0, concat_axis=0, tiled=True)  172 us
    another operation x15, other arithmetic, factor_corner(): lower = jnp.linalg.cholesky(symmetric_of(corner))  88 us
    gather x2, local copies, waits for them, and re-layouts, shards(): jnp.take(padded, chosen, axis=1)  49.6 us
    concatenate x4, local copies, waits for them, and re-layouts, with_zero(): return jnp.concatenate([blocks, jnp.zeros(shape, blocks.dtype)], axis=axis)  48.7 us
    another operation x2, other arithmetic, factor_corner(): jax.scipy.linalg.solve_triangular(lower, jnp.eye(PANEL, dtype=jnp.float32...  40.1 us
    gather x2, local copies, waits for them, and re-layouts, shards(): jnp.take(arrived, placement, axis=0).reshape(front_rows, col_blocks, BLOCK)  34.4 us
  transfers between devices with their start and end apart: 5, of which 5 were waited for; matrix products, arithmetic and copies ran while one was open for 0% of the time, Pallas kernels for 0%

commit v1 on v0

--- a/solution.py
+++ b/solution.py
@@ -77,6 +77,42 @@
 
 def apply_inverse(rows, inverse):
     return lax.dot_general(rows, inverse, (((1,), (1,)), ((), ())), precision=lax.Precision.HIGHEST)
+
+
+def early_corner(child_piece, row_map, col_map, own_diagonal):
+    n_row = lax.axis_size("row")
+    n_col = lax.axis_size("col")
+    n_sub = lax.axis_size("sub")
+    rows_here, cols_here = child_piece.shape
+    row_blocks = rows_here // BLOCK
+    col_blocks = cols_here // BLOCK
+    panel_blocks = PANEL // BLOCK
+    first_rows = min(row_blocks, -(-panel_blocks // n_row))
+    first_cols = min(col_blocks, -(-panel_blocks // n_col))
+    piece = child_piece[: first_rows * BLOCK, : first_cols * BLOCK]
+    pieces = lax.all_gather(piece, ("sub", "row", "col"))
+    pieces = pieces.reshape(n_sub, n_row, n_col, first_rows, BLOCK, first_cols, BLOCK)
+    pieces = pieces.transpose(0, 1, 3, 2, 5, 4, 6).reshape(
+        n_sub, n_row * first_rows, n_col * first_cols, BLOCK, BLOCK
+    )
+    row_pos = (
+        jnp.arange(n_row, dtype=jnp.int32)[:, None] * row_blocks
+        + jnp.arange(first_rows, dtype=jnp.int32)[None, :]
+    ).reshape(-1)
+    col_pos = (
+        jnp.arange(n_col, dtype=jnp.int32)[:, None] * col_blocks
+        + jnp.arange(first_cols, dtype=jnp.int32)[None, :]
+    ).reshape(-1)
+    corner = jnp.zeros((panel_blocks + 1, panel_blocks + 1, BLOCK, BLOCK), jnp.float32)
+    for which in range(n_sub):
+        rb = row_map[which][row_pos]
+        cb = col_map[which][col_pos]
+        rb = jnp.where(rb < panel_blocks, rb, panel_blocks)
+        cb = jnp.where(cb < panel_blocks, cb, panel_blocks)
+        corner = corner.at[rb[:, None], cb[None, :]].add(pieces[which])
+    corner = corner[:panel_blocks, :panel_blocks].transpose(0, 2, 1, 3).reshape(PANEL, PANEL)
+    diagonal = lax.all_gather(own_diagonal, ("sub", "col"), tiled=True)[:PANEL]
+    return corner + jnp.diag(diagonal)
 
 
 def shards(child, row_map, col_map, own_diagonal, coupling):
@@ -97,24 +133,21 @@
     front_col_blocks = front_cols // BLOCK
     row_cap = min(row_blocks, (front_row_blocks + n_row - 1) // n_row)
     col_cap = min(col_blocks, (front_col_blocks + n_col - 1) // n_col)
+    n_children = row_map.shape[0]
     my_rows_map = lax.dynamic_index_in_dim(row_map, my_sub, 0, keepdims=False)
     my_cols_map = lax.dynamic_index_in_dim(col_map, my_sub, 0, keepdims=False)
-    padded = with_zero(child_piece.reshape(row_blocks, BLOCK, cols_here), 0)
-    chosen = sending_table(my_rows_map, my_row, row_blocks, front_row_blocks, n_row, row_cap)
-    outgoing = jnp.take(padded, chosen, axis=0).reshape(n_row, row_cap * BLOCK, cols_here)
-    arrived = lax.all_to_all(outgoing, "row", split_axis=0, concat_axis=0, tiled=True)
-    arrived = with_zero(arrived.reshape(n_row * row_cap, BLOCK, cols_here), 0)
-    placement = receiving_table(
-        my_rows_map, my_row, row_blocks, front_row_blocks, row_cap, 0, n_row * row_cap
-    )
-    front_rows_data = jnp.take(arrived, placement, axis=0).reshape(front_rows, col_blocks, BLOCK)
-    padded = with_zero(front_rows_data, 1)
+
+    corner = early_corner(child_piece, row_map, col_map, own_diagonal)
+    lower, inverse = factor_corner(corner)
+
+    by_col = child_piece.reshape(rows_here, col_blocks, BLOCK).transpose(1, 0, 2)
+    by_col = with_zero(by_col, 0)
     chosen = sending_table(my_cols_map, my_col, col_blocks, front_col_blocks, n_group, col_cap)
-    outgoing = jnp.take(padded, chosen, axis=1).reshape(front_rows, n_group, col_cap * BLOCK)
-    arrived = lax.all_to_all(outgoing, ("sub", "col"), split_axis=1, concat_axis=1, tiled=True)
-    arrived = with_zero(arrived.reshape(front_rows, n_group * col_cap, BLOCK), 1)
-    assembled = jnp.zeros((front_rows, front_col_blocks, BLOCK), jnp.float32)
-    for which in range(2):
+    outgoing = jnp.take(by_col, chosen, axis=0).reshape(n_group, col_cap, rows_here, BLOCK)
+    arrived = lax.all_to_all(outgoing, ("sub", "col"), split_axis=0, concat_axis=0, tiled=True)
+    arrived = with_zero(arrived.reshape(n_group * col_cap, rows_here, BLOCK), 0)
+    per_child = []
+    for which in range(n_children):
         placement = receiving_table(
             col_map[which],
             my_group,
@@ -124,8 +157,32 @@
             which * n_col,
             n_group * col_cap,
         )
-        assembled = assembled + jnp.take(arrived, placement, axis=1)
-    assembled = assembled.reshape(front_rows, front_cols)
+        placed = jnp.take(arrived, placement, axis=0)
+        placed = placed.reshape(front_col_blocks, row_blocks, BLOCK, BLOCK)
+        per_child.append(with_zero(placed, 1))
+
+    sent = []
+    for which in range(n_children):
+        chosen = sending_table(row_map[which], my_row, row_blocks, front_row_blocks, n_row, row_cap)
+        sent.append(jnp.take(per_child[which], chosen, axis=1))
+    outgoing = jnp.stack(sent, axis=0).reshape(
+        n_children, front_col_blocks, n_row, row_cap, BLOCK, BLOCK
+    )
+    outgoing = outgoing.transpose(2, 0, 1, 3, 4, 5)
+    arrived = lax.all_to_all(outgoing, "row", split_axis=0, concat_axis=0, tiled=True)
+    arrived = arrived.reshape(n_row, n_children, front_col_blocks, row_cap, BLOCK, BLOCK)
+    assembled = jnp.zeros((front_col_blocks, front_row_blocks, BLOCK, BLOCK), jnp.float32)
+    for which in range(n_children):
+        from_child = arrived[:, which].transpose(1, 0, 2, 3, 4).reshape(
+            front_col_blocks, n_row * row_cap, BLOCK, BLOCK
+        )
+        from_child = with_zero(from_child, 1)
+        placement = receiving_table(
+            row_map[which], my_row, row_blocks, front_row_blocks, row_cap, 0, n_row * row_cap
+        )
+        assembled = assembled + jnp.take(from_child, placement, axis=1)
+    assembled = assembled.transpose(1, 2, 0, 3).reshape(front_rows, front_cols)
+
     global_row = my_row * front_rows + jnp.arange(front_rows, dtype=jnp.int32)
     global_col = my_group * front_cols + jnp.arange(front_cols, dtype=jnp.int32)
     on_diagonal = global_row[:, None] == global_col[None, :]
@@ -138,12 +195,6 @@
     panel_cols = front_part[:, :PANEL]
     theirs_start = my_group * front_cols % front_rows
     theirs_root = my_group * front_cols // front_rows
-    is_root = (my_row == 0) & (my_group == 0)
-    corner = jnp.where(is_root, panel_cols[:PANEL], jnp.eye(PANEL, dtype=jnp.float32))
-    lower, inverse = factor_corner(corner)
-    factors = from_root(jnp.stack([lower, inverse]), "row", 0)
-    lower = factors[0]
-    inverse = factors[1]
     own_rows = apply_inverse(panel_cols, inverse)
     top_rows = jnp.where(my_row == 0, lower, own_rows[:PANEL])
     own_rows = jnp.concatenate([top_rows, own_rows[PANEL:]], axis=0)

time: 1710 us -> 1520 us (0.89)
  waiting for transfers between devices: 1150 us -> 907 us
  local copies, waits for them, and re-layouts: 249 us -> 287 us
  blocking collectives: 0 us -> 23.9 us
    all_to_all x1, waiting for transfers between devices: 677 us -> 407 us  [shards(): lax.all_to_all(outgoing, ('sub', 'col'), split_axis=0, concat_axis=0, til...]
    all_to_all x1, waiting for transfers between devices: 172 us -> 0.01 us  [shards(): lax.all_to_all(outgoing, 'row', split_axis=0, concat_axis=0, tiled=True)]
    all_gather x0 -> x1, waiting for transfers between devices: none -> 162 us  [early_corner(): pieces = lax.all_gather(piece, ('sub', 'row', 'col'))]
    transpose x0 -> x6, local copies, waits for them, and re-layouts: none -> 50.3 us  [the longest x3 40.6 us: shards(): arrived[:, which].transpose(1, 0, 2, 3, 4)]
    gather x7 -> x11, local copies, waits for them, and re-layouts: 120 us -> 85.4 us  [the longest x2 25.1 us: shards(): assembled = assembled + jnp.take(from_child, placement, axis=1)]
    psum x3 -> x2, waiting for transfers between devices: 305 us -> 338 us  [from_root(): return lax.psum(kept, axis)]
    all_gather x0 -> x1, blocking collectives: none -> 23.9 us  [early_corner(): diagonal = lax.all_gather(own_diagonal, ('sub', 'col'), tiled=True)[:PANEL]]
    select_n x0 -> x2, local copies, waits for them, and re-layouts: none -> 23.5 us  [shards(): sent.append(jnp.take(per_child[which], chosen, axis=1))]
  transfers between devices with their start and end apart: 5 -> 5, of which waited for: 5 -> 4; matrix products, arithmetic and copies ran while one was open for 0% -> 11% of each run, Pallas kernels for 0% -> 0%
where the time goes in v1:
time: 1520 us; the launch traced here: 1510 us
  waiting for transfers between devices  907 us (60%)
  local copies, waits for them, and re-layouts  287 us (19%)
  other arithmetic  211 us (14%)
  matrix products  49.2 us (3%)
  blocking collectives  23.9 us (2%)
  between operations  16.7 us (1%)
  starting transfers between devices  15.4 us (1%)
    all_to_all x1, waiting for transfers between devices, shards(): lax.all_to_all(outgoing, ('sub', 'col'), split_axis=0, concat_axis=0, til...  407 us
    psum x2, waiting for transfers between devices, from_root(): return lax.psum(kept, axis)  338 us
    all_gather x1, waiting for transfers between devices, early_corner(): pieces = lax.all_gather(piece, ('sub', 'row', 'col'))  162 us
    another operation x15, other arithmetic, factor_corner(): lower = jnp.linalg.cholesky(symmetric_of(corner))  79.6 us
    concatenate x6, local copies, waits for them, and re-layouts, with_zero(): return jnp.concatenate([blocks, jnp.zeros(shape, blocks.dtype)], axis=axis)  56.1 us
    another operation x3, other arithmetic, factor_corner(): jax.scipy.linalg.solve_triangular(lower, jnp.eye(PANEL, dtype=jnp.float32...  41.2 us
    transpose x3, local copies, waits for them, and re-layouts, shards(): arrived[:, which].transpose(1, 0, 2, 3, 4)  40.6 us
  transfers between devices with their start and end apart: 5, of which 4 were waited for; matrix products, arithmetic and copies ran while one was open for 11% of the time, Pallas kernels for 0%

profile of v1, /device:TPU:0, one launch (start us, length us, event | category | flops | bytes accessed | tf_op | source)
XLA Modules:
  0.0 1510.1 jit_solution(17915247903720305442)
XLA Ops:
  35.7 13.5 gather_fusion.4
  49.2 12.7 broadcast_select_fusion
  69.3 406.9 %all-to-all-done = f32[8,3,1536,128]{3,2,1,0:T(8,128)} async-done(((f32[8,3,1536,128]{3,2,1,0:T(8,128)}), f32[8,3,1536,128]{3,2,1,0:T(8,128)}, u32[]{:S(2)}, u32[]{:S(2)}) %all-to-all-start) | async-done | bytes 18874400 | tf_op jit(solution)/shard_map/all_to_all | solution.py:147
  476.2 14.5 concatenate.48
  490.7 10.9 gather_fusion.7
  510.0 11.1 gather_fusion.8
  521.1 12.8 select_bitcast_fusion
  533.9 11.8 copy.62
  545.6 10.9 gather_fusion.5
  564.8 11.3 gather_fusion.6
  576.1 12.8 select_bitcast_fusion.1
  588.8 11.7 copy.61
  632.1 23.9 %all-gather.1 = f32[8,1,1280]{2,1,0:T(1,128)S(1)} all-gather(f32[1,1,1280]{2,1,0:T(1,128)S(1)} %reshape.507), channel_id=1, replica_groups=mesh['sub'=2,'row'=4,'col'=4] {'sub','col'}, dimensions={0}, use_global_device_ids=true | all-gather | bytes 46080 | tf_op jit(solution)/shard_map/all_gather | solution.py:114
  658.4 161.6 %all-gather.4.cloned.1.call-done = f32[4096,128]{1,0:T(8,128)} async-done(((f32[128,128]{1,0:T(8,128)}), f32[4096,128]{1,0:T(8,128)}) %all-gather.4.cloned.1.call-update) | async-done | bytes 2097168 | tf_op jit(solution)/shard_map/all_gather | solution.py:93
  831.0 11.7 cholesky.103
  855.2 11.9 cholesky.215
  867.1 9.8 custom-call.32
  878.5 11.7 cholesky.236
  901.5 12.1 cholesky.253
  920.0 14.2 while.1
  934.1 40.1 %custom-call.34 = f32[4,128,128]{1,2,0:T(8,128)S(1)} custom-call(f32[4,128,128]{2,1,0:T(8,128)} %get-tuple-element.15), custom_call_target="InvertDiagBlocksLowerTriangular" | custom-call | tf_op jit(solution)/shard_map/jit(_solve_triangular)/triangular_solve | solution.py:72
  980.9 17.1 %slice_bitcast_fusion.1 = (f32[10,4,5,128,128]{4,3,2,0,1:T(8,128)}, f32[10,4,5,128,128]{4,3,2,0,1:T(8,128)}) fusion(f32[4,2,10,5,128,128]{5,4,3,2,1,0:T(8,128)} %all-to-all-done.1), kind=kLoop, calls=%fused_computation.22 | loop fusion | bytes 52428800 | tf_op jit(solution)/shard_map/transpose | solution.py:176
  998.0 11.8 copy.65
  1009.8 12.0 concatenate.52
  1021.8 11.7 copy.64
  1033.5 12.0 concatenate.51
  1045.5 12.7 gather_fusion.10
  1058.2 12.4 gather_fusion.9
  1080.2 26.6 %copy.68 = f32[20,128,10,128]{3,2,1,0:T(8,128)S(1)} copy(f32[20,128,10,128]{3,1,2,0:T(8,128)S(1)} %fusion.3) | data formatting | bytes 26214400 | tf_op jit(solution)/shard_map/reshape | solution.py:184
  1131.1 217.3 %all-reduce.12.cloned.1.call-done = f32[2560,512]{1,0:T(8,128)} async-done(((f32[2560,512]{1,0:T(8,128)}), f32[2560,512]{1,0:T(8,128)}) %all-reduce.12.cloned.1.call-update) | async-done | bytes 5242896 | tf_op jit(solution)/shard_map/psum | solution.py:13
  1353.9 120.9 %all-reduce.14.cloned.1.call-done = f32[2560,512]{1,0:T(8,128)} async-done(((f32[2560,512]{1,0:T(8,128)}), f32[2560,512]{1,0:T(8,128)}) %all-reduce.14.cloned.1.call-update) | async-done | bytes 5242896 | tf_op jit(solution)/shard_map/psum | solution.py:13
  1474.8 28.6 %fusion.1 = f32[2560,1280]{1,0:T(8,128)} fusion(f32[2560,1280]{1,0:T(8,128)} %copy-done, f32[2560,512]{1,0:T(8,128)} %all-reduce.12.cloned.1.call-done, pred[2560]{0:T(1024)(128)(4,1)S(1)} %fusion.60, pred[1280]{0:T(1024)(128)(4,1)S(1)} %broadcast_compare_fusion, f32[2560,512]{1,0:T(8,128)} %all-reduce.14.cloned.1.call-done, s32[]{:T(128)S(6)} %select_n.468), kind=kOutput, calls=%fused_computation.18 | convolution fusion | flops 20142489600 | bytes 39325444 | tf_op jit(solution)/shard_map/dot_general | solution.py:204
  (169 shorter events, 186.9 us)
Async XLA Ops:
  16.1 9.7 copy-start.6
  16.1 9.7 copy-start.7
  61.9 414.3 %all-to-all-start = ((f32[8,3,1536,128]{3,2,1,0:T(8,128)}), f32[8,3,1536,128]{3,2,1,0:T(8,128)}, u32[]{:S(2)}, u32[]{:S(2)}) async-start(f32[8,3,1536,128]{3,2,1,0:T(8,128)} %broadcast_select_fusion), calls=%async_computation | async-start | bytes 37748736 | tf_op jit(solution)/shard_map/all_to_all | solution.py:147
  618.7 11.0 copy-start.8
  618.7 13.4 copy-start.5
  618.7 37.3 %copy-start.10 = (pred[48]{0:T(512)(128)(4,1)S(1)}, pred[48]{0:T(512)(128)(4,1)}, u32[]{:S(2)}) copy-start(pred[48]{0:T(512)(128)(4,1)} %get-tuple-element.39) | copy-start | bytes 148
  618.7 37.5 %copy-start.9 = (pred[48]{0:T(512)(128)(4,1)S(1)}, pred[48]{0:T(512)(128)(4,1)}, u32[]{:S(2)}) copy-start(pred[48]{0:T(512)(128)(4,1)} %get-tuple-element.84) | copy-start | bytes 148
  618.7 362.2 %all-to-all-start.1 = ((f32[4,2,10,5,128,128]{5,4,3,2,1,0:T(8,128)}), f32[4,2,10,5,128,128]{5,4,3,2,1,0:T(8,128)}, u32[]{:S(2)}, u32[]{:S(2)}) async-start(f32[4,2,10,5,128,128]{5,4,3,2,1,0:T(8,128)} %copy.63), calls=%async_computation.1 | async-start | bytes 52428800 | tf_op jit(solution)/shard_map/all_to_all | solution.py:172
  627.5 192.6 %all-gather.4.cloned.1.call-start = ((), (), s32[]{:S(2)}) async-start(), calls=%async_computation.4 | async-start | bytes 2162688 | tf_op jit(solution)/shard_map/all_gather | solution.py:93
  629.0 719.3 %all-reduce.12.cloned.1.call-start = ((), (), s32[]{:S(2)}) async-start(), calls=%async_computation.2 | async-start | bytes 10485760 | tf_op jit(solution)/shard_map/psum | solution.py:13
  829.4 145.9 %copy-start.1 = (f32[512,512]{1,0:T(8,128)S(1)}, f32[512,512]{1,0:T(8,128)}, u32[]{:S(2)}) copy-start(f32[512,512]{1,0:T(8,128)} %fusion.22) | copy-start | bytes 3145732
  830.0 1.0 copy-start.2
  978.8 1.7 copy-start.3
  1106.7 12.0 copy-start.4
  1113.8 5.0 copy-start
  1131.0 343.8 %all-reduce.14.cloned.1.call-start = ((), (), s32[]{:S(2)}) async-start(), calls=%async_computation.3 | async-start | bytes 10485760 | tf_op jit(solution)/shard_map/psum | solution.py:13
Sparse Core Ops, SparseCore 0:
  631.3 188.6 all-gather.3
  1131.1 217.1 all-reduce.11
  1354.0 120.7 all-reduce.13

commit v2 on v1

--- a/solution.py
+++ b/solution.py
@@ -138,50 +138,52 @@
     my_cols_map = lax.dynamic_index_in_dim(col_map, my_sub, 0, keepdims=False)
 
     corner = early_corner(child_piece, row_map, col_map, own_diagonal)
+
+    by_col = child_piece.reshape(rows_here, col_blocks, BLOCK)
+    chosen = sending_table(my_cols_map, my_col, col_blocks, front_col_blocks, n_group, col_cap)
+    outgoing = jnp.take(by_col, chosen, axis=1, mode="fill", fill_value=0.0)
+    outgoing = outgoing.transpose(1, 0, 2).reshape(n_group, col_cap, rows_here, BLOCK)
+    outgoing, corner = lax.optimization_barrier((outgoing, corner))
     lower, inverse = factor_corner(corner)
-
-    by_col = child_piece.reshape(rows_here, col_blocks, BLOCK).transpose(1, 0, 2)
-    by_col = with_zero(by_col, 0)
-    chosen = sending_table(my_cols_map, my_col, col_blocks, front_col_blocks, n_group, col_cap)
-    outgoing = jnp.take(by_col, chosen, axis=0).reshape(n_group, col_cap, rows_here, BLOCK)
     arrived = lax.all_to_all(outgoing, ("sub", "col"), split_axis=0, concat_axis=0, tiled=True)
-    arrived = with_zero(arrived.reshape(n_group * col_cap, rows_here, BLOCK), 0)
-    per_child = []
+    arrived, lower, inverse = lax.optimization_barrier((arrived, lower, inverse))
+    arrived = arrived.reshape(n_group * col_cap, row_blocks, BLOCK, BLOCK)
+
+    col_index = jnp.stack(
+        [
+            receiving_table(
+                col_map[which],
+                my_group,
+                col_blocks,
+                front_col_blocks,
+                col_cap,
+                which * n_col,
+                n_group * col_cap,
+            )
+            for which in range(n_children)
+        ]
+    )
+    row_index = jnp.stack(
+        [
+            sending_table(row_map[which], my_row, row_blocks, front_row_blocks, n_row, row_cap)
+            for which in range(n_children)
+        ]
+    ).reshape(n_children, n_row, row_cap)
+    outgoing = arrived.at[
+        col_index[None, :, None, :], row_index.transpose(1, 0, 2)[:, :, :, None]
+    ].get(mode="fill", fill_value=0.0)
+    arrived = lax.all_to_all(outgoing, "row", split_axis=0, concat_axis=0, tiled=True)
+    arrived = arrived.transpose(1, 0, 2, 3, 4, 5).reshape(
+        n_children, n_row * row_cap, front_col_blocks, BLOCK, BLOCK
+    )
+    assembled = None
     for which in range(n_children):
-        placement = receiving_table(
-            col_map[which],
-            my_group,
-            col_blocks,
-            front_col_blocks,
-            col_cap,
-            which * n_col,
-            n_group * col_cap,
-        )
-        placed = jnp.take(arrived, placement, axis=0)
-        placed = placed.reshape(front_col_blocks, row_blocks, BLOCK, BLOCK)
-        per_child.append(with_zero(placed, 1))
-
-    sent = []
-    for which in range(n_children):
-        chosen = sending_table(row_map[which], my_row, row_blocks, front_row_blocks, n_row, row_cap)
-        sent.append(jnp.take(per_child[which], chosen, axis=1))
-    outgoing = jnp.stack(sent, axis=0).reshape(
-        n_children, front_col_blocks, n_row, row_cap, BLOCK, BLOCK
-    )
-    outgoing = outgoing.transpose(2, 0, 1, 3, 4, 5)
-    arrived = lax.all_to_all(outgoing, "row", split_axis=0, concat_axis=0, tiled=True)
-    arrived = arrived.reshape(n_row, n_children, front_col_blocks, row_cap, BLOCK, BLOCK)
-    assembled = jnp.zeros((front_col_blocks, front_row_blocks, BLOCK, BLOCK), jnp.float32)
-    for which in range(n_children):
-        from_child = arrived[:, which].transpose(1, 0, 2, 3, 4).reshape(
-            front_col_blocks, n_row * row_cap, BLOCK, BLOCK
-        )
-        from_child = with_zero(from_child, 1)
         placement = receiving_table(
             row_map[which], my_row, row_blocks, front_row_blocks, row_cap, 0, n_row * row_cap
         )
-        assembled = assembled + jnp.take(from_child, placement, axis=1)
-    assembled = assembled.transpose(1, 2, 0, 3).reshape(front_rows, front_cols)
+        part = arrived[which].at[placement].get(mode="fill", fill_value=0.0)
+        assembled = part if assembled is None else assembled + part
+    assembled = assembled.transpose(0, 2, 1, 3).reshape(front_rows, front_cols)
 
     global_row = my_row * front_rows + jnp.arange(front_rows, dtype=jnp.int32)
     global_col = my_group * front_cols + jnp.arange(front_cols, dtype=jnp.int32)

time: 1520 us -> 1230 us (0.81)
  waiting for transfers between devices: 907 us -> 777 us
  local copies, waits for them, and re-layouts: 287 us -> 158 us
  other arithmetic: 211 us -> 188 us
    all_to_all x1, waiting for transfers between devices: 0.01 us -> 283 us  [shards(): lax.all_to_all(outgoing, 'row', split_axis=0, concat_axis=0, tiled=True)]
    all_gather x1, waiting for transfers between devices: 162 us -> 0.01 us  [early_corner(): pieces = lax.all_gather(piece, ('sub', 'row', 'col'))]
    all_to_all x1, waiting for transfers between devices: 407 us -> 259 us  [shards(): lax.all_to_all(outgoing, ('sub', 'col'), split_axis=0, concat_axis=0, til...]
    psum x2, waiting for transfers between devices: 338 us -> 235 us  [from_root(): return lax.psum(kept, axis)]
    concatenate x6 -> x2, local copies, waits for them, and re-layouts: 56.1 us -> 0.12 us  [shards(): outgoing = arrived.at[col_index[None, :, None, :], row_index.transpose(1,...]
    transpose x4 -> x0, local copies, waits for them, and re-layouts: 49.5 us -> none  [the longest x3 40.6 us: shards(): arrived[:, which].transpose(1, 0, 2, 3, 4)]
    select_n x2 -> x1, local copies, waits for them, and re-layouts: 23.5 us -> 0.1 us  [shards(): outgoing = arrived.at[col_index[None, :, None, :], row_index.transpose(1,...]
    transpose x2 -> x0, other arithmetic: 18.8 us -> none  [the longest x1 9.51 us: shards(): assembled = assembled.transpose(1, 2, 0, 3).reshape(front_rows, front_cols)]
  transfers between devices with their start and end apart: 5 -> 5, of which waited for: 4 -> 4; matrix products, arithmetic and copies ran while one was open for 11% -> 16% of each run, Pallas kernels for 0% -> 0%
where the time goes in v2:
time: 1230 us
  waiting for transfers between devices  777 us (63%)
  other arithmetic  188 us (15%)
  local copies, waits for them, and re-layouts  158 us (13%)
  matrix products  46.1 us (4%)
  blocking collectives  25.2 us (2%)
  between operations  16.8 us (1%)
  starting transfers between devices  14.8 us (1%)
    all_to_all x1, waiting for transfers between devices, shards(): lax.all_to_all(outgoing, 'row', split_axis=0, concat_axis=0, tiled=True)  283 us
    all_to_all x1, waiting for transfers between devices, shards(): lax.all_to_all(outgoing, ('sub', 'col'), split_axis=0, concat_axis=0, til...  259 us
    psum x2, waiting for transfers between devices, from_root(): return lax.psum(kept, axis)  235 us
    another operation x15, other arithmetic, factor_corner(): lower = jnp.linalg.cholesky(symmetric_of(corner))  79.5 us
    another operation x4, other arithmetic, factor_corner(): jax.scipy.linalg.solve_triangular(lower, jnp.eye(PANEL, dtype=jnp.float32...  41.3 us
    gather x1, local copies, waits for them, and re-layouts, shards(): outgoing = arrived.at[col_index[None, :, None, :], row_index.transpose(1,...  33.9 us
    dot_general x1, matrix products, shards(): lax.dot_general(own_rows, theirs, (((1,), (1,)), ((), ())), precision=lax...  28.8 us
    reshape x1, local copies, waits for them, and re-layouts, shards(): assembled = assembled.transpose(0, 2, 1, 3).reshape(front_rows, front_cols)  26.6 us
  transfers between devices with their start and end apart: 5, of which 4 were waited for; matrix products, arithmetic and copies ran while one was open for 16% of the time, Pallas kernels for 0%

profile of v2, /device:TPU:0, one launch (start us, length us, event | category | flops | bytes accessed | tf_op | source)
XLA Modules:
  0.0 1226.0 jit_solution(15242075423732847923)
XLA Ops:
  12.3 9.6 copy.48
  21.9 9.7 copy.49
  31.8 25.2 %all-gather.1 = f32[8,1,1280]{2,1,0:T(1,128)S(1)} all-gather(f32[1,1,1280]{2,1,0:T(1,128)S(1)} %reshape.589), channel_id=1, replica_groups=mesh['sub'=2,'row'=4,'col'=4] {'sub','col'}, dimensions={0}, use_global_device_ids=true | all-gather | bytes 46080 | tf_op jit(solution)/shard_map/all_gather | solution.py:114
  57.7 13.4 %gather_fusion = f32[24,1536,128]{2,1,0:T(8,128)} fusion(f32[1536,12,128]{2,0,1:T(8,128)} %copy.49, s32[1024]{0:T(1024)S(1)} %pad_clamp_fusion.3), kind=kCustom, calls=%fused_computation | custom fusion | bytes 37748832 | tf_op jit(solution)/shard_map/jit(_take)/gather | solution.py:144
  71.2 12.7 %broadcast_select_fusion.1 = f32[24,1536,128]{2,1,0:T(8,128)} fusion(f32[24,1536,128]{2,1,0:T(8,128)} %gather_fusion, pred[24]{0:T(512)(128)(4,1)S(1)} %compare_and_fusion.7), kind=kLoop, calls=%fused_computation.19 | loop fusion | flops 4718592 | bytes 37748760 | tf_op jit(solution)/shard_map/jit(_take)/select_n | solution.py:144
  92.3 6.1 all-to-all-start
  102.4 11.7 cholesky.103
  114.2 9.8 custom-call.31
  124.7 11.7 cholesky.215
  136.9 9.8 custom-call.32
  147.4 11.7 cholesky.236
  159.1 9.8 custom-call.33
  169.5 11.9 cholesky.253
  187.6 13.8 %while.1 = (s32[]{:T(128)}, f32[512,512]{1,0:T(8,128)}, s32[4,2]{0,1:T(2,128)S(1)}, f32[4,128,128]{2,1,0:T(8,128)}, s32[]{:T(128)}) while((s32[]{:T(128)}, f32[512,512]{1,0:T(8,128)}, s32[4,2]{0,1:T(2,128)S(1)}, f32[4,128,128]{2,1,0:T(8,128)}, s32[]{:T(128)}) %tuple.72), condition=%wide.while_cond, body=%wide.while_body.sunk | while | flops 2 | bytes 132705 | solution.py:72
  201.4 40.1 %custom-call.34 = f32[4,128,128]{1,2,0:T(8,128)S(1)} custom-call(f32[4,128,128]{2,1,0:T(8,128)} %get-tuple-element.22), custom_call_target="InvertDiagBlocksLowerTriangular" | custom-call | tf_op jit(solution)/shard_map/jit(_solve_triangular)/triangular_solve | solution.py:72
  247.8 258.6 %all-to-all-done = f32[8,3,1536,128]{3,2,1,0:T(8,128)} async-done(((f32[8,3,1536,128]{3,2,1,0:T(8,128)}), f32[8,3,1536,128]{3,2,1,0:T(8,128)}, u32[]{:S(2)}, u32[]{:S(2)}) %all-to-all-start) | async-done | bytes 18874400 | tf_op jit(solution)/shard_map/all_to_all | solution.py:148
  506.3 33.9 %gather_fusion.5 = f32[400,128,128]{2,1,0:T(8,128)} fusion(f32[24,12,128,128]{3,2,1,0:T(8,128)} %bitcast.48, s32[400]{0:T(512)S(1)} %reshape.548), kind=kCustom, calls=%fused_computation.5 | custom fusion | bytes 52432000 | tf_op jit(solution)/shard_map/gather | solution.py:174
  540.2 19.0 %broadcast_select_fusion = f32[4,2,5,10,128,128]{5,4,3,2,1,0:T(8,128)} fusion(f32[4,2,5,10,128,128]{5,4,3,2,1,0:T(8,128)} %bitcast.167, pred[4,2,5,10]{3,2,1,0:T(8,128)(4,1)S(1)} %copy.54), kind=kLoop, calls=%fused_computation.18 | loop fusion | flops 6553600 | bytes 52429200 | tf_op jit(solution)/shard_map/select_n | solution.py:174
  559.2 8.6 all-to-all-start.1
  568.5 283.4 %all-to-all-done.1 = f32[4,2,5,10,128,128]{5,4,3,2,1,0:T(8,128)} async-done(((f32[4,2,5,10,128,128]{5,4,3,2,1,0:T(8,128)}), f32[4,2,5,10,128,128]{5,4,3,2,1,0:T(8,128)}, u32[]{:S(2)}, u32[]{:S(2)}) %all-to-all-start.1) | async-done | bytes 26214432 | tf_op jit(solution)/shard_map/all_to_all | solution.py:175
  851.9 17.3 %fusion.78 = (f32[1,4,5,10,128,128]{5,4,3,2,0,1:T(8,128)}, f32[1,4,5,10,128,128]{5,4,3,2,0,1:T(8,128)}) fusion(f32[2,4,5,10,128,128]{5,4,3,2,0,1:T(8,128)} %bitcast.50), kind=kLoop, calls=%fused_computation.251 | loop fusion | bytes 52428800 | tf_op jit(solution)/shard_map/slice | solution.py:184
  869.2 12.2 gather_fusion.6
  881.4 12.5 %gather_fusion.7 = f32[20,10,128,128]{3,2,1,0:T(8,128)} fusion(f32[20,10,128,128]{3,2,1,0:T(8,128)} %bitcast.170, s32[1024]{0:T(1024)S(1)} %pad_clamp_fusion), kind=kCustom, calls=%fused_computation.7 | custom fusion | bytes 26214480 | tf_op jit(solution)/shard_map/gather | solution.py:184
  893.8 9.5 add_bitcast_fusion
  903.4 26.6 %copy.58 = f32[20,128,10,128]{3,2,1,0:T(8,128)S(1)} copy(f32[20,128,10,128]{3,1,2,0:T(8,128)S(1)} %add_bitcast_fusion) | data formatting | bytes 26214400 | tf_op jit(solution)/shard_map/reshape | solution.py:186
  929.9 7.0 fusion.2
  936.9 9.4 fusion.3
  947.0 3.0 maximum_select_fusion
  950.1 113.7 %all-reduce.6.cloned.1.call-done = f32[2560,512]{1,0:T(8,128)} async-done(((f32[2560,512]{1,0:T(8,128)}), f32[2560,512]{1,0:T(8,128)}) %all-reduce.6.cloned.1.call-update) | async-done | bytes 5242896 | tf_op jit(solution)/shard_map/psum | solution.py:13
  1063.8 5.5 broadcast_select_fusion.2
  1069.3 120.9 %all-reduce.8.cloned.1.call-done = f32[2560,512]{1,0:T(8,128)} async-done(((f32[2560,512]{1,0:T(8,128)}), f32[2560,512]{1,0:T(8,128)}) %all-reduce.8.cloned.1.call-update) | async-done | bytes 5242896 | tf_op jit(solution)/shard_map/psum | solution.py:13
  1190.3 28.8 %fusion.1 = f32[2560,1280]{1,0:T(8,128)} fusion(f32[2560,1280]{1,0:T(8,128)} %copy-done, f32[2560,512]{1,0:T(8,128)} %all-reduce.6.cloned.1.call-done, pred[2560]{0:T(1024)(128)(4,1)S(1)} %fusion.56, pred[1280]{0:T(1024)(128)(4,1)S(1)} %broadcast_compare_fusion, f32[2560,512]{1,0:T(8,128)} %all-reduce.8.cloned.1.call-done, s32[]{:T(128)S(6)} %select_n.579), kind=kOutput, calls=%fused_computation.14 | convolution fusion | flops 20142489600 | bytes 39325444 | tf_op jit(solution)/shard_map/dot_general | solution.py:206
  (150 shorter events, 46.3 us)
Async XLA Ops:
  6.5 77.3 %all-gather.4.cloned.1.call-start = ((), (), s32[]{:S(2)}) async-start(), calls=%async_computation.4 | async-start | bytes 2162688 | tf_op jit(solution)/shard_map/all_gather | solution.py:93
  21.9 10.0 copy-start.1
  21.9 35.2 %copy-start.2 = (s32[2,48]{1,0:T(2,128)S(1)}, s32[2,48]{1,0:T(2,128)}, u32[]{:S(2)}) copy-start(s32[2,48]{1,0:T(2,128)} %param.7) | copy-start | bytes 1156
  21.9 35.2 %copy-start.3 = (s32[2,48]{1,0:T(2,128)S(1)}, s32[2,48]{1,0:T(2,128)}, u32[]{:S(2)}) copy-start(s32[2,48]{1,0:T(2,128)} %param.6) | copy-start | bytes 1156
  92.3 7.5 copy-start.4
  92.3 414.0 %all-to-all-start = ((f32[8,3,1536,128]{3,2,1,0:T(8,128)}), f32[8,3,1536,128]{3,2,1,0:T(8,128)}, u32[]{:S(2)}, u32[]{:S(2)}) async-start(f32[8,3,1536,128]{3,2,1,0:T(8,128)} %bitcast.169), calls=%async_computation | async-start | bytes 37748736 | tf_op jit(solution)/shard_map/all_to_all | solution.py:148
  559.2 292.7 %all-to-all-start.1 = ((f32[4,2,5,10,128,128]{5,4,3,2,1,0:T(8,128)}), f32[4,2,5,10,128,128]{5,4,3,2,1,0:T(8,128)}, u32[]{:S(2)}, u32[]{:S(2)}) async-start(f32[4,2,5,10,128,128]{5,4,3,2,1,0:T(8,128)} %broadcast_select_fusion), calls=%async_computation.1 | async-start | bytes 52428800 | tf_op jit(solution)/shard_map/all_to_all | solution.py:175
  567.8 496.0 %all-reduce.6.cloned.1.call-start = ((), (), s32[]{:S(2)}) async-start(), calls=%async_computation.2 | async-start | bytes 10485760 | tf_op jit(solution)/shard_map/psum | solution.py:13
  936.9 9.9 copy-start
  950.1 240.2 %all-reduce.8.cloned.1.call-start = ((), (), s32[]{:S(2)}) async-start(), calls=%async_computation.3 | async-start | bytes 10485760 | tf_op jit(solution)/shard_map/psum | solution.py:13
Sparse Core Ops, SparseCore 0:
  10.3 59.2 all-gather.3
  950.2 113.5 all-reduce.5
  1069.4 120.7 all-reduce.7

commit v3 on v2

--- a/solution.py
+++ b/solution.py
@@ -201,8 +201,8 @@
     top_rows = jnp.where(my_row == 0, lower, own_rows[:PANEL])
     own_rows = jnp.concatenate([top_rows, own_rows[PANEL:]], axis=0)
     own_rows = from_root(own_rows, ("sub", "col"), 0)
-    theirs = from_root(own_rows, "row", theirs_root)
-    theirs = lax.dynamic_slice_in_dim(theirs, theirs_start, front_cols, 0)
+    theirs = lax.dynamic_slice_in_dim(own_rows, theirs_start, front_cols, 0)
+    theirs = from_root(theirs, "row", theirs_root)
     update = lax.dot_general(
         own_rows, theirs, (((1,), (1,)), ((), ())), precision=lax.Precision.HIGHEST
     )

time: 1230 us -> 1190 us (0.967)
  waiting for transfers between devices: 777 us -> 735 us
    psum x2, waiting for transfers between devices: 235 us -> 193 us  [from_root(): return lax.psum(kept, axis)]
  transfers between devices with their start and end apart: 5 -> 5, of which waited for: 4 -> 4; matrix products, arithmetic and copies ran while one was open for 16% -> 17% of each run, Pallas kernels for 0% -> 0%
where the time goes in v3:
time: 1190 us; the launch traced here: 1180 us
  waiting for transfers between devices  735 us (62%)
  other arithmetic  186 us (16%)
  local copies, waits for them, and re-layouts  158 us (13%)
  matrix products  46 us (4%)
  blocking collectives  25.2 us (2%)
  between operations  16.8 us (1%)
  starting transfers between devices  14.8 us (1%)
    all_to_all x1, waiting for transfers between devices, shards(): lax.all_to_all(outgoing, 'row', split_axis=0, concat_axis=0, tiled=True)  283 us
    all_to_all x1, waiting for transfers between devices, shards(): lax.all_to_all(outgoing, ('sub', 'col'), split_axis=0, concat_axis=0, til...  259 us
    psum x2, waiting for transfers between devices, from_root(): return lax.psum(kept, axis)  193 us
    another operation x15, other arithmetic, factor_corner(): lower = jnp.linalg.cholesky(symmetric_of(corner))  79.5 us
    another operation x4, other arithmetic, factor_corner(): jax.scipy.linalg.solve_triangular(lower, jnp.eye(PANEL, dtype=jnp.float32...  41.3 us
    gather x1, local copies, waits for them, and re-layouts, shards(): outgoing = arrived.at[col_index[None, :, None, :], row_index.transpose(1,...  33.9 us
    dot_general x1, matrix products, shards(): lax.dot_general(own_rows, theirs, (((1,), (1,)), ((), ())), precision=lax...  28.6 us
    reshape x1, local copies, waits for them, and re-layouts, shards(): assembled = assembled.transpose(0, 2, 1, 3).reshape(front_rows, front_cols)  26.6 us
  transfers between devices with their start and end apart: 5, of which 4 were waited for; matrix products, arithmetic and copies ran while one was open for 17% of the time, Pallas kernels for 0%

profile of v3, /device:TPU:0, one launch (start us, length us, event | category | flops | bytes accessed | tf_op | source)
XLA Modules:
  0.0 1182.0 jit_solution(10320608231453694730)
XLA Ops:
  12.3 9.6 copy.48
  21.9 9.7 copy.49
  31.8 25.2 %all-gather.1 = f32[8,1,1280]{2,1,0:T(1,128)S(1)} all-gather(f32[1,1,1280]{2,1,0:T(1,128)S(1)} %reshape.589), channel_id=1, replica_groups=mesh['sub'=2,'row'=4,'col'=4] {'sub','col'}, dimensions={0}, use_global_device_ids=true | all-gather | bytes 46080 | tf_op jit(solution)/shard_map/all_gather | solution.py:114
  57.7 13.5 %gather_fusion = f32[24,1536,128]{2,1,0:T(8,128)} fusion(f32[1536,12,128]{2,0,1:T(8,128)} %copy.49, s32[1024]{0:T(1024)S(1)} %pad_clamp_fusion.3), kind=kCustom, calls=%fused_computation | custom fusion | bytes 37748832 | tf_op jit(solution)/shard_map/jit(_take)/gather | solution.py:144
  71.2 12.7 %broadcast_select_fusion.1 = f32[24,1536,128]{2,1,0:T(8,128)} fusion(f32[24,1536,128]{2,1,0:T(8,128)} %gather_fusion, pred[24]{0:T(512)(128)(4,1)S(1)} %compare_and_fusion.7), kind=kLoop, calls=%fused_computation.19 | loop fusion | flops 4718592 | bytes 37748760 | tf_op jit(solution)/shard_map/jit(_take)/select_n | solution.py:144
  92.3 6.1 all-to-all-start
  102.4 11.7 cholesky.103
  114.3 9.8 custom-call.31
  124.8 11.7 cholesky.215
  136.9 9.8 custom-call.32
  147.4 11.7 cholesky.236
  159.2 9.8 custom-call.33
  169.6 11.9 %cholesky.253 = f32[128,128]{1,0:T(8,128)S(1)} custom-call(f32[128,128]{1,0:T(8,128)S(1)} %convolution_subtract_fusion.6), custom_call_target="Cholesky" | custom-call | tf_op jit(solution)/shard_map/jit(cholesky)/cholesky | solution.py:71
  187.7 13.8 %while.1 = (s32[]{:T(128)}, f32[512,512]{1,0:T(8,128)}, s32[4,2]{0,1:T(2,128)S(1)}, f32[4,128,128]{2,1,0:T(8,128)}, s32[]{:T(128)}) while((s32[]{:T(128)}, f32[512,512]{1,0:T(8,128)}, s32[4,2]{0,1:T(2,128)S(1)}, f32[4,128,128]{2,1,0:T(8,128)}, s32[]{:T(128)}) %tuple.72), condition=%wide.while_cond, body=%wide.while_body.sunk | while | flops 2 | bytes 132705 | solution.py:72
  201.4 40.1 %custom-call.34 = f32[4,128,128]{1,2,0:T(8,128)S(1)} custom-call(f32[4,128,128]{2,1,0:T(8,128)} %get-tuple-element.22), custom_call_target="InvertDiagBlocksLowerTriangular" | custom-call | tf_op jit(solution)/shard_map/jit(_solve_triangular)/triangular_solve | solution.py:72
  247.8 258.6 %all-to-all-done = f32[8,3,1536,128]{3,2,1,0:T(8,128)} async-done(((f32[8,3,1536,128]{3,2,1,0:T(8,128)}), f32[8,3,1536,128]{3,2,1,0:T(8,128)}, u32[]{:S(2)}, u32[]{:S(2)}) %all-to-all-start) | async-done | bytes 18874400 | tf_op jit(solution)/shard_map/all_to_all | solution.py:148
  506.3 33.9 %gather_fusion.5 = f32[400,128,128]{2,1,0:T(8,128)} fusion(f32[24,12,128,128]{3,2,1,0:T(8,128)} %bitcast.48, s32[400]{0:T(512)S(1)} %reshape.548), kind=kCustom, calls=%fused_computation.5 | custom fusion | bytes 52432000 | tf_op jit(solution)/shard_map/gather | solution.py:174
  540.2 19.0 %broadcast_select_fusion = f32[4,2,5,10,128,128]{5,4,3,2,1,0:T(8,128)} fusion(f32[4,2,5,10,128,128]{5,4,3,2,1,0:T(8,128)} %bitcast.168, pred[4,2,5,10]{3,2,1,0:T(8,128)(4,1)S(1)} %copy.54), kind=kLoop, calls=%fused_computation.18 | loop fusion | flops 6553600 | bytes 52429200 | tf_op jit(solution)/shard_map/select_n | solution.py:174
  559.2 8.6 all-to-all-start.1
  568.5 283.4 %all-to-all-done.1 = f32[4,2,5,10,128,128]{5,4,3,2,1,0:T(8,128)} async-done(((f32[4,2,5,10,128,128]{5,4,3,2,1,0:T(8,128)}), f32[4,2,5,10,128,128]{5,4,3,2,1,0:T(8,128)}, u32[]{:S(2)}, u32[]{:S(2)}) %all-to-all-start.1) | async-done | bytes 26214432 | tf_op jit(solution)/shard_map/all_to_all | solution.py:175
  851.9 17.3 %fusion.76 = (f32[1,4,5,10,128,128]{5,4,3,2,0,1:T(8,128)}, f32[1,4,5,10,128,128]{5,4,3,2,0,1:T(8,128)}) fusion(f32[2,4,5,10,128,128]{5,4,3,2,0,1:T(8,128)} %bitcast.50), kind=kLoop, calls=%fused_computation.249 | loop fusion | bytes 52428800 | tf_op jit(solution)/shard_map/slice | solution.py:184
  869.2 12.2 %gather_fusion.6 = f32[20,10,128,128]{3,2,1,0:T(8,128)} fusion(f32[20,10,128,128]{3,2,1,0:T(8,128)} %bitcast.172, s32[1024]{0:T(1024)S(1)} %pad_clamp_fusion.1), kind=kCustom, calls=%fused_computation.6 | custom fusion | bytes 26214480 | tf_op jit(solution)/shard_map/gather | solution.py:184
  881.4 12.4 %gather_fusion.7 = f32[20,10,128,128]{3,2,1,0:T(8,128)} fusion(f32[20,10,128,128]{3,2,1,0:T(8,128)} %bitcast.171, s32[1024]{0:T(1024)S(1)} %pad_clamp_fusion), kind=kCustom, calls=%fused_computation.7 | custom fusion | bytes 26214480 | tf_op jit(solution)/shard_map/gather | solution.py:184
  893.8 9.5 add_bitcast_fusion
  903.3 26.6 %copy.58 = f32[20,128,10,128]{3,2,1,0:T(8,128)S(1)} copy(f32[20,128,10,128]{3,1,2,0:T(8,128)S(1)} %add_bitcast_fusion) | data formatting | bytes 26214400 | tf_op jit(solution)/shard_map/reshape | solution.py:186
  929.9 7.0 fusion.2
  936.9 9.4 fusion.3
  947.0 3.0 maximum_select_fusion
  950.1 113.9 %all-reduce.6.cloned.1.call-done = f32[2560,512]{1,0:T(8,128)} async-done(((f32[2560,512]{1,0:T(8,128)}), f32[2560,512]{1,0:T(8,128)}) %all-reduce.6.cloned.1.call-update) | async-done | bytes 5242896 | tf_op jit(solution)/shard_map/psum | solution.py:13
  1064.0 3.7 dynamic-slice_select_fusion
  1067.7 78.6 %all-reduce.8.cloned.1.call-done = f32[1280,512]{1,0:T(8,128)} async-done(((f32[1280,512]{1,0:T(8,128)}), f32[1280,512]{1,0:T(8,128)}) %all-reduce.8.cloned.1.call-update) | async-done | bytes 2621456 | tf_op jit(solution)/shard_map/psum | solution.py:13
  1146.4 28.6 %fusion.1 = f32[2560,1280]{1,0:T(8,128)} fusion(f32[2560,1280]{1,0:T(8,128)} %copy-done, f32[2560,512]{1,0:T(8,128)} %all-reduce.6.cloned.1.call-done, f32[1280,512]{1,0:T(8,128)} %all-reduce.8.cloned.1.call-done, pred[2560]{0:T(1024)(128)(4,1)S(1)} %fusion.55, pred[1280]{0:T(1024)(128)(4,1)S(1)} %broadcast_compare_fusion), kind=kOutput, calls=%fused_computation.14 | convolution fusion | flops 20142489600 | bytes 34082560 | tf_op jit(solution)/shard_map/dot_general | solution.py:206
  (150 shorter events, 46.3 us)
Async XLA Ops:
  6.5 77.4 %all-gather.4.cloned.1.call-start = ((), (), s32[]{:S(2)}) async-start(), calls=%async_computation.4 | async-start | bytes 2162688 | tf_op jit(solution)/shard_map/all_gather | solution.py:93
  21.9 10.0 copy-start.1
  21.9 35.2 %copy-start.2 = (s32[2,48]{1,0:T(2,128)S(1)}, s32[2,48]{1,0:T(2,128)}, u32[]{:S(2)}) copy-start(s32[2,48]{1,0:T(2,128)} %param.7) | copy-start | bytes 1156
  21.9 35.2 %copy-start.3 = (s32[2,48]{1,0:T(2,128)S(1)}, s32[2,48]{1,0:T(2,128)}, u32[]{:S(2)}) copy-start(s32[2,48]{1,0:T(2,128)} %param.6) | copy-start | bytes 1156
  92.3 7.5 copy-start.4
  92.3 414.0 %all-to-all-start = ((f32[8,3,1536,128]{3,2,1,0:T(8,128)}), f32[8,3,1536,128]{3,2,1,0:T(8,128)}, u32[]{:S(2)}, u32[]{:S(2)}) async-start(f32[8,3,1536,128]{3,2,1,0:T(8,128)} %bitcast.170), calls=%async_computation | async-start | bytes 37748736 | tf_op jit(solution)/shard_map/all_to_all | solution.py:148
  559.2 292.7 %all-to-all-start.1 = ((f32[4,2,5,10,128,128]{5,4,3,2,1,0:T(8,128)}), f32[4,2,5,10,128,128]{5,4,3,2,1,0:T(8,128)}, u32[]{:S(2)}, u32[]{:S(2)}) async-start(f32[4,2,5,10,128,128]{5,4,3,2,1,0:T(8,128)} %broadcast_select_fusion), calls=%async_computation.1 | async-start | bytes 52428800 | tf_op jit(solution)/shard_map/all_to_all | solution.py:175
  567.8 496.2 %all-reduce.6.cloned.1.call-start = ((), (), s32[]{:S(2)}) async-start(), calls=%async_computation.2 | async-start | bytes 10485760 | tf_op jit(solution)/shard_map/psum | solution.py:13
  936.9 9.9 copy-start
  950.0 196.4 %all-reduce.8.cloned.1.call-start = ((), (), s32[]{:S(2)}) async-start(), calls=%async_computation.3 | async-start | bytes 5242880 | tf_op jit(solution)/shard_map/psum | solution.py:13
Sparse Core Ops, SparseCore 0:
  10.3 59.2 all-gather.3
  950.1 113.8 all-reduce.5
  1067.8 78.4 all-reduce.7

commit v4 on v3

--- a/solution.py
+++ b/solution.py
@@ -133,7 +133,7 @@
     front_col_blocks = front_cols // BLOCK
     row_cap = min(row_blocks, (front_row_blocks + n_row - 1) // n_row)
     col_cap = min(col_blocks, (front_col_blocks + n_col - 1) // n_col)
-    n_children = row_map.shape[0]
+    n_sub = lax.axis_size("sub")
     my_rows_map = lax.dynamic_index_in_dim(row_map, my_sub, 0, keepdims=False)
     my_cols_map = lax.dynamic_index_in_dim(col_map, my_sub, 0, keepdims=False)
 
@@ -141,48 +141,59 @@
 
     by_col = child_piece.reshape(rows_here, col_blocks, BLOCK)
     chosen = sending_table(my_cols_map, my_col, col_blocks, front_col_blocks, n_group, col_cap)
-    outgoing = jnp.take(by_col, chosen, axis=1, mode="fill", fill_value=0.0)
-    outgoing = outgoing.transpose(1, 0, 2).reshape(n_group, col_cap, rows_here, BLOCK)
+    chosen = jnp.minimum(chosen, col_blocks - 1).reshape(n_sub, n_col * col_cap)
+    chosen = jnp.stack([chosen[1 - my_sub], chosen[my_sub]]).reshape(-1)
+    outgoing = by_col.at[:, chosen].get(mode="promise_in_bounds")
+    outgoing = outgoing.transpose(1, 0, 2).reshape(2, n_col, col_cap, rows_here, BLOCK)
     outgoing, corner = lax.optimization_barrier((outgoing, corner))
     lower, inverse = factor_corner(corner)
-    arrived = lax.all_to_all(outgoing, ("sub", "col"), split_axis=0, concat_axis=0, tiled=True)
-    arrived, lower, inverse = lax.optimization_barrier((arrived, lower, inverse))
-    arrived = arrived.reshape(n_group * col_cap, row_blocks, BLOCK, BLOCK)
-
-    col_index = jnp.stack(
-        [
-            receiving_table(
-                col_map[which],
-                my_group,
-                col_blocks,
-                front_col_blocks,
-                col_cap,
-                which * n_col,
-                n_group * col_cap,
-            )
-            for which in range(n_children)
-        ]
-    )
-    row_index = jnp.stack(
-        [
-            sending_table(row_map[which], my_row, row_blocks, front_row_blocks, n_row, row_cap)
-            for which in range(n_children)
-        ]
-    ).reshape(n_children, n_row, row_cap)
-    outgoing = arrived.at[
-        col_index[None, :, None, :], row_index.transpose(1, 0, 2)[:, :, :, None]
-    ].get(mode="fill", fill_value=0.0)
-    arrived = lax.all_to_all(outgoing, "row", split_axis=0, concat_axis=0, tiled=True)
-    arrived = arrived.transpose(1, 0, 2, 3, 4, 5).reshape(
-        n_children, n_row * row_cap, front_col_blocks, BLOCK, BLOCK
-    )
-    assembled = None
-    for which in range(n_children):
+    other_half = lax.all_to_all(outgoing[0], "col", split_axis=0, concat_axis=0, tiled=True)
+    other_half = lax.ppermute(other_half, "sub", [(0, 1), (1, 0)])
+
+    def row_sending(half, which):
+        cols_of = lax.dynamic_index_in_dim(col_map, which, 0, keepdims=False)
+        rows_of = lax.dynamic_index_in_dim(row_map, which, 0, keepdims=False)
+        col_index = receiving_table(
+            cols_of, my_group, col_blocks, front_col_blocks, col_cap, 0, n_col * col_cap
+        )
+        col_valid = col_index < n_col * col_cap
+        col_index = jnp.minimum(col_index, n_col * col_cap - 1)
+        row_index = sending_table(rows_of, my_row, row_blocks, front_row_blocks, n_row, row_cap)
+        row_index = jnp.minimum(row_index, row_blocks - 1).reshape(n_row, row_cap)
+        half = half.reshape(n_col * col_cap, row_blocks, BLOCK, BLOCK)
+        sending = half.at[col_index[None, None, :], row_index[:, :, None]].get(
+            mode="promise_in_bounds"
+        )
+        return sending, col_valid, rows_of
+
+    def row_receiving(sending, col_valid, rows_of):
+        pieces = [lax.dynamic_index_in_dim(sending, my_row, 0, keepdims=False)]
+        for shift in range(1, n_row):
+            piece = lax.dynamic_index_in_dim(sending, (my_row + shift) % n_row, 0, keepdims=False)
+            pairs = [(i, (i + shift) % n_row) for i in range(n_row)]
+            pieces.append(lax.ppermute(piece, "row", pairs))
+        received = jnp.stack(pieces).reshape(n_row * row_cap, front_col_blocks, BLOCK, BLOCK)
         placement = receiving_table(
-            row_map[which], my_row, row_blocks, front_row_blocks, row_cap, 0, n_row * row_cap
+            rows_of, my_row, row_blocks, front_row_blocks, row_cap, 0, n_row * row_cap
         )
-        part = arrived[which].at[placement].get(mode="fill", fill_value=0.0)
-        assembled = part if assembled is None else assembled + part
+        row_valid = placement < n_row * row_cap
+        source = jnp.minimum(placement, n_row * row_cap - 1) // row_cap
+        slot = placement % row_cap
+        placement = ((my_row - source) % n_row) * row_cap + slot
+        part = received.at[placement].get(mode="promise_in_bounds")
+        keep = row_valid[:, None] & col_valid[None, :]
+        return part, keep
+
+    sending_other, col_valid_other, rows_other = row_sending(other_half, 1 - my_sub)
+    sending_other, own_outgoing = lax.optimization_barrier((sending_other, outgoing[1]))
+    part_other, keep_other = row_receiving(sending_other, col_valid_other, rows_other)
+    own_half = lax.all_to_all(own_outgoing, "col", split_axis=0, concat_axis=0, tiled=True)
+    own_half, lower, inverse = lax.optimization_barrier((own_half, lower, inverse))
+    sending_own, col_valid_own, rows_own = row_sending(own_half, my_sub)
+    part_own, keep_own = row_receiving(sending_own, col_valid_own, rows_own)
+    assembled = jnp.where(keep_other[:, :, None, None], part_other, 0.0) + jnp.where(
+        keep_own[:, :, None, None], part_own, 0.0
+    )
     assembled = assembled.transpose(0, 2, 1, 3).reshape(front_rows, front_cols)
 
     global_row = my_row * front_rows + jnp.arange(front_rows, dtype=jnp.int32)

time: 1190 us -> 1110 us (0.933)
  waiting for transfers between devices: 735 us -> 430 us
  blocking collectives: 25.2 us -> 236 us
  local copies, waits for them, and re-layouts: 158 us -> 174 us
    all_to_all x2 -> x1, waiting for transfers between devices: 542 us -> 34.6 us  [shards(): lax.all_to_all(own_outgoing, 'col', split_axis=0, concat_axis=0, tiled=True)]
    all_to_all x0 -> x1, blocking collectives: none -> 211 us  [shards(): lax.all_to_all(outgoing[0], 'col', split_axis=0, concat_axis=0, tiled=True)]
    ppermute x0 -> x7, waiting for transfers between devices: none -> 138 us  [the longest x6 125 us: row_receiving(): pieces.append(lax.ppermute(piece, 'row', pairs))]
    psum x2, waiting for transfers between devices: 193 us -> 257 us  [from_root(): return lax.psum(kept, axis)]
    select_n x10 -> x4, other arithmetic: 31.8 us -> 0.07 us  [the longest x2 0.05 us: row_receiving(): part = received.at[placement].get(mode='promise_in_bounds')]
    dynamic_slice x0 -> x3, local copies, waits for them, and re-layouts: none -> 19.5 us  [the longest x2 19.4 us: row_receiving(): pieces = [lax.dynamic_index_in_dim(sending, my_row, 0, keepdims=False)]]
    another operation x0 -> x3, other arithmetic: none -> 17.9 us  [the longest x2 17.9 us: row_receiving(): jnp.stack(pieces).reshape(n_row * row_cap, front_col_blocks, BLOCK, BLOCK)]
    slice x1 -> x0, local copies, waits for them, and re-layouts: 17.3 us -> none  [shards(): part = arrived[which].at[placement].get(mode='fill', fill_value=0.0)]
  transfers between devices with their start and end apart: 5 -> 11, of which waited for: 4 -> 9; matrix products, arithmetic and copies ran while one was open for 17% -> 23% of each run, Pallas kernels for 0% -> 0%
where the time goes in v4:
time: 1110 us; the launch traced here: 1100 us
  waiting for transfers between devices  430 us (39%)
  blocking collectives  236 us (21%)
  other arithmetic  177 us (16%)
  local copies, waits for them, and re-layouts  174 us (16%)
  matrix products  48.5 us (4%)
  between operations  16.8 us (2%)
  starting transfers between devices  16.1 us (1%)
    psum x2, waiting for transfers between devices, from_root(): return lax.psum(kept, axis)  257 us
    all_to_all x1, blocking collectives, shards(): lax.all_to_all(outgoing[0], 'col', split_axis=0, concat_axis=0, tiled=True)  211 us
    ppermute x6, waiting for transfers between devices, row_receiving(): pieces.append(lax.ppermute(piece, 'row', pairs))  125 us
    another operation x15, other arithmetic, factor_corner(): lower = jnp.linalg.cholesky(symmetric_of(corner))  79.5 us
    another operation x4, other arithmetic, factor_corner(): jax.scipy.linalg.solve_triangular(lower, jnp.eye(PANEL, dtype=jnp.float32...  43.9 us
    gather x2, local copies, waits for them, and re-layouts, row_sending(): half.at[col_index[None, None, :], row_index[:, :, None]]  35.5 us
    all_to_all x1, waiting for transfers between devices, shards(): lax.all_to_all(own_outgoing, 'col', split_axis=0, concat_axis=0, tiled=True)  34.6 us
    dot_general x1, matrix products, shards(): lax.dot_general(own_rows, theirs, (((1,), (1,)), ((), ())), precision=lax...  28.6 us
  transfers between devices with their start and end apart: 11, of which 9 were waited for; matrix products, arithmetic and copies ran while one was open for 23% of the time, Pallas kernels for 0%

profile of v4, /device:TPU:0, one launch (start us, length us, event | category | flops | bytes accessed | tf_op | source)
XLA Modules:
  0.0 1099.4 jit_solution(7284549305836817544)
XLA Ops:
  9.7 9.6 copy.30
  20.0 9.7 copy.31
  32.8 25.2 %all-gather.1 = f32[8,1,1280]{2,1,0:T(1,128)S(1)} all-gather(f32[1,1,1280]{2,1,0:T(1,128)S(1)} %reshape.889), channel_id=1, replica_groups=mesh['sub'=2,'row'=4,'col'=4] {'sub','col'}, dimensions={0}, use_global_device_ids=true | all-gather | bytes 46080 | tf_op jit(solution)/shard_map/all_gather | solution.py:114
  58.1 13.4 %gather_fusion = f32[24,1536,128]{2,1,0:T(8,128)} fusion(f32[1536,12,128]{2,0,1:T(8,128)} %copy.31, s32[1024]{0:T(1024)S(1)} %pad_clamp_fusion.3), kind=kCustom, calls=%fused_computation | custom fusion | bytes 37748832 | tf_op jit(solution)/shard_map/gather | solution.py:146
  79.9 11.0 %slice_bitcast_fusion = (f32[4,3,1536,128]{3,2,1,0:T(8,128)}, f32[4,3,1536,128]{3,2,1,0:T(8,128)S(1)}) fusion(f32[2,4,3,1536,128]{4,3,2,1,0:T(8,128)} %bitcast.216), kind=kLoop, calls=%fused_computation.21 | loop fusion | bytes 37748736 | tf_op jit(solution)/shard_map/squeeze | solution.py:188
  90.9 210.7 %all_to_all.10 = f32[4,3,1536,128]{3,2,1,0:T(8,128)} all-to-all(f32[4,3,1536,128]{3,2,1,0:T(8,128)S(1)} %get-tuple-element.60), channel_id=1, replica_groups=mesh['sub'=2,'row'=4,'col'=4] {'col'}, dimensions={0} | all-to-all | bytes 18874368 | tf_op jit(solution)/shard_map/all_to_all | solution.py:150
  302.9 13.8 %collective-permute-done = f32[4,3,1536,128]{3,2,1,0:T(8,128)} collective-permute-done((f32[4,3,1536,128]{3,2,1,0:T(8,128)}, f32[4,3,1536,128]{3,2,1,0:T(8,128)}, u32[]{:S(2)}, u32[]{:S(2)}) %collective-permute-start) | collective-permute-done | bytes 9437216 | tf_op jit(solution)/shard_map/ppermute | solution.py:151
  316.7 17.7 %gather_fusion.5 = f32[200,128,128]{2,1,0:T(8,128)} fusion(f32[12,12,128,128]{3,2,1,0:T(8,128)} %bitcast.19, s32[200]{0:T(256)S(1)} %reshape.842), kind=kCustom, calls=%fused_computation.5 | custom fusion | bytes 26216000 | tf_op jit(solution)/shard_map/gather | solution.py:164
  346.4 11.7 %cholesky.103 = f32[128,128]{1,0:T(8,128)S(1)} custom-call(f32[128,128]{1,0:T(8,128)S(1)} %cholesky.263), custom_call_target="Cholesky" | custom-call | tf_op jit(solution)/shard_map/jit(cholesky)/cholesky | solution.py:71
  358.3 9.8 custom-call.31
  368.7 11.7 %cholesky.215 = f32[128,128]{1,0:T(8,128)S(1)} custom-call(f32[128,128]{1,0:T(8,128)S(1)} %cholesky.267), custom_call_target="Cholesky" | custom-call | tf_op jit(solution)/shard_map/jit(cholesky)/cholesky | solution.py:71
  380.5 10.0 custom-call.32
  391.1 11.7 %cholesky.236 = f32[128,128]{1,0:T(8,128)S(1)} custom-call(f32[128,128]{1,0:T(8,128)S(1)} %cholesky.272), custom_call_target="Cholesky" | custom-call | tf_op jit(solution)/shard_map/jit(cholesky)/cholesky | solution.py:71
  402.9 9.8 custom-call.33
  413.3 11.9 %cholesky.253 = f32[128,128]{1,0:T(8,128)S(1)} custom-call(f32[128,128]{1,0:T(8,128)S(1)} %convolution_subtract_fusion.6), custom_call_target="Cholesky" | custom-call | tf_op jit(solution)/shard_map/jit(cholesky)/cholesky | solution.py:71
  432.1 9.1 constant_dynamic-slice_fusion.3
  443.3 13.9 %while.1 = (s32[]{:T(128)}, f32[512,512]{1,0:T(8,128)}, s32[4,2]{0,1:T(2,128)S(1)}, f32[4,128,128]{2,1,0:T(8,128)}, s32[]{:T(128)}) while((s32[]{:T(128)}, f32[512,512]{1,0:T(8,128)}, s32[4,2]{0,1:T(2,128)S(1)}, f32[4,128,128]{2,1,0:T(8,128)}, s32[]{:T(128)}) %tuple.75), condition=%wide.while_cond, body=%wide.while_body.sunk | while | flops 2 | bytes 132705 | solution.py:72
  457.2 40.8 %custom-call.34 = f32[4,128,128]{1,2,0:T(8,128)} custom-call(f32[4,128,128]{2,1,0:T(8,128)} %get-tuple-element.26), custom_call_target="InvertDiagBlocksLowerTriangular" | custom-call | tf_op jit(solution)/shard_map/jit(_solve_triangular)/triangular_solve | solution.py:72
  511.8 34.6 %all-to-all-done.1 = f32[4,3,1536,128]{3,2,1,0:T(8,128)} async-done(((f32[4,3,1536,128]{3,2,1,0:T(8,128)}), f32[4,3,1536,128]{3,2,1,0:T(8,128)}, u32[]{:S(2)}, u32[]{:S(2)}) %all-to-all-start.1) | async-done | bytes 9437216 | tf_op jit(solution)/shard_map/all_to_all | solution.py:190
  546.4 17.7 %gather_fusion.7 = f32[200,128,128]{2,1,0:T(8,128)} fusion(f32[12,12,128,128]{3,2,1,0:T(8,128)} %bitcast.64, s32[200]{0:T(256)S(1)} %reshape.856), kind=kCustom, calls=%fused_computation.7 | custom fusion | bytes 26216000 | tf_op jit(solution)/shard_map/gather | solution.py:164
  564.2 10.4 constant_dynamic-slice_fusion.1
  586.6 9.0 pad_maximum_fusion
  595.5 12.5 %gather_fusion.6 = f32[20,10,128,128]{3,2,1,0:T(8,128)} fusion(f32[20,10,128,128]{3,2,1,0:T(8,128)} %bitcast.219, s32[1024]{0:T(1024)S(1)} %pad_clamp_fusion.1), kind=kCustom, calls=%fused_computation.6 | custom fusion | bytes 26214480 | tf_op jit(solution)/shard_map/gather | solution.py:183
  608.0 48.6 %collective-permute-done.4 = f32[5,10,128,128]{3,2,1,0:T(8,128)} collective-permute-done((f32[5,10,128,128]{3,2,1,0:T(8,128)}, f32[5,10,128,128]{3,2,1,0:T(8,128)}, u32[]{:S(2)}, u32[]{:S(2)}) %collective-permute-start.4) | collective-permute-done | bytes 3276832 | tf_op jit(solution)/shard_map/ppermute | solution.py:174
  656.7 69.3 %collective-permute-done.5 = f32[5,10,128,128]{3,2,1,0:T(8,128)} collective-permute-done((f32[5,10,128,128]{3,2,1,0:T(8,128)}, f32[5,10,128,128]{3,2,1,0:T(8,128)}, u32[]{:S(2)}, u32[]{:S(2)}) %collective-permute-start.5) | collective-permute-done | bytes 3276832 | tf_op jit(solution)/shard_map/ppermute | solution.py:174
  726.2 8.9 pad_maximum_fusion.1
  735.2 12.5 %gather_fusion.8 = f32[20,10,128,128]{3,2,1,0:T(8,128)} fusion(f32[20,10,128,128]{3,2,1,0:T(8,128)} %bitcast.220, s32[1024]{0:T(1024)S(1)} %pad_clamp_fusion), kind=kCustom, calls=%fused_computation.8 | custom fusion | bytes 26214480 | tf_op jit(solution)/shard_map/gather | solution.py:183
  747.6 9.3 add_bitcast_fusion
  756.9 26.6 %copy.37 = f32[20,128,10,128]{3,2,1,0:T(8,128)S(1)} copy(f32[20,128,10,128]{3,1,2,0:T(8,128)S(1)} %add_bitcast_fusion) | data formatting | bytes 26214400 | tf_op jit(solution)/shard_map/reshape | solution.py:197
  803.1 178.5 %all-reduce.6.cloned.1.call-done = f32[2560,512]{1,0:T(8,128)} async-done(((f32[2560,512]{1,0:T(8,128)}), f32[2560,512]{1,0:T(8,128)}) %all-reduce.6.cloned.1.call-update) | async-done | bytes 5242896 | tf_op jit(solution)/shard_map/psum | solution.py:13
  985.4 78.6 %all-reduce.8.cloned.1.call-done = f32[1280,512]{1,0:T(8,128)} async-done(((f32[1280,512]{1,0:T(8,128)}), f32[1280,512]{1,0:T(8,128)}) %all-reduce.8.cloned.1.call-update) | async-done | bytes 2621456 | tf_op jit(solution)/shard_map/psum | solution.py:13
  1064.0 28.6 %fusion.1 = f32[2560,1280]{1,0:T(8,128)} fusion(f32[2560,1280]{1,0:T(8,128)} %copy-done, f32[2560,512]{1,0:T(8,128)} %all-reduce.6.cloned.1.call-done, f32[1280,512]{1,0:T(8,128)} %all-reduce.8.cloned.1.call-done, pred[2560]{0:T(1024)(128)(4,1)S(1)} %fusion.50, pred[1280]{0:T(1024)(128)(4,1)S(1)} %broadcast_compare_fusion), kind=kOutput, calls=%fused_computation.15 | convolution fusion | flops 20142489600 | bytes 34082560 | tf_op jit(solution)/shard_map/dot_general | solution.py:217
  (213 shorter events, 99.8 us)
Async XLA Ops:
  6.5 65.0 %all-gather.4.cloned.1.call-start = ((), (), s32[]{:S(2)}) async-start(), calls=%async_computation.4 | async-start | bytes 2162688 | tf_op jit(solution)/shard_map/all_gather | solution.py:93
  8.8 334.5 %copy-start.10 = (pred[48]{0:T(512)(128)(4,1)}, pred[48]{0:T(512)(128)(4,1)S(1)}, u32[]{:S(2)}) copy-start(pred[48]{0:T(512)(128)(4,1)S(1)} %get-tuple-element.94) | copy-start | bytes 148
  20.0 9.8 copy-start.6
  20.0 10.4 copy-start.7
  20.0 12.8 %copy-start.4 = (f32[1280]{0:T(1024)S(1)}, f32[1280]{0:T(1024)}, u32[]{:S(2)}) copy-start(f32[1280]{0:T(1024)} %param.8) | copy-start | bytes 15364
  29.8 313.5 %copy-start.8 = (s32[48]{0:T(128)}, s32[48]{0:T(128)S(1)}, u32[]{:S(2)}) copy-start(s32[48]{0:T(128)S(1)} %get-tuple-element.84) | copy-start | bytes 580
  301.7 15.0 %collective-permute-start = (f32[4,3,1536,128]{3,2,1,0:T(8,128)}, f32[4,3,1536,128]{3,2,1,0:T(8,128)}, u32[]{:S(2)}, u32[]{:S(2)}) collective-permute-start(f32[4,3,1536,128]{3,2,1,0:T(8,128)} %all_to_all.10), channel_id=1, source_target_pairs={{0,16},{16,0},{1,17},{17,1},{2,18},{18,2},{3,19},{19,3},{4,20},{20... | collective-permute-start | bytes 28311560 | tf_op jit(solution)/shard_map/ppermute | solution.py:151
  302.3 32.2 %copy-start.20 = (pred[10]{0:T(512)(128)(4,1)}, pred[10]{0:T(512)(128)(4,1)S(1)}, u32[]{:S(2)}) copy-start(pred[10]{0:T(512)(128)(4,1)S(1)} %fusion.53) | copy-start | bytes 34
  302.4 32.0 %copy-start.22 = (pred[10]{0:T(512)(128)(4,1)}, pred[10]{0:T(512)(128)(4,1)S(1)}, u32[]{:S(2)}) copy-start(pred[10]{0:T(512)(128)(4,1)S(1)} %fusion.55) | copy-start | bytes 34
  302.5 31.9 %copy-start.12 = (s32[10]{0:T(128)}, s32[10]{0:T(128)S(1)}, u32[]{:S(2)}) copy-start(s32[10]{0:T(128)S(1)} %select_reduce_fusion.10) | copy-start | bytes 124
  302.7 31.8 %copy-start.14 = (s32[10]{0:T(128)}, s32[10]{0:T(128)S(1)}, u32[]{:S(2)}) copy-start(s32[10]{0:T(128)S(1)} %select_reduce_fusion.9) | copy-start | bytes 124
  334.4 211.9 %all-to-all-start.1 = ((f32[4,3,1536,128]{3,2,1,0:T(8,128)}), f32[4,3,1536,128]{3,2,1,0:T(8,128)}, u32[]{:S(2)}, u32[]{:S(2)}) async-start(f32[4,3,1536,128]{3,2,1,0:T(8,128)} %get-tuple-element.13), calls=%async_computation.1 | async-start | bytes 18874368 | tf_op jit(solution)/shard_map/all_to_all | solution.py:190
  340.3 641.4 %all-reduce.6.cloned.1.call-start = ((), (), s32[]{:S(2)}) async-start(), calls=%async_computation.2 | async-start | bytes 10485760 | tf_op jit(solution)/shard_map/psum | solution.py:13
  441.2 136.4 %collective-permute-start.1 = (f32[5,10,128,128]{3,2,1,0:T(8,128)}, f32[5,10,128,128]{3,2,1,0:T(8,128)}, u32[]{:S(2)}, u32[]{:S(2)}) collective-permute-start(f32[5,10,128,128]{3,2,1,0:T(8,128)} %get-tuple-element.64), channel_id=1, source_target_pairs={{0,4},{4,8},{8,12},{12,0},{1,5},{5,9},{9,13},{13,1},{2,6},{6,10},{... | collective-permute-start | bytes 9830408 | tf_op jit(solution)/shard_map/ppermute | solution.py:174
  504.5 82.0 %collective-permute-start.2 = (f32[5,10,128,128]{3,2,1,0:T(8,128)}, f32[5,10,128,128]{3,2,1,0:T(8,128)}, u32[]{:S(2)}, u32[]{:S(2)}) collective-permute-start(f32[5,10,128,128]{3,2,1,0:T(8,128)} %get-tuple-element.63), channel_id=1, source_target_pairs={{0,8},{4,12},{8,0},{12,4},{1,9},{5,13},{9,1},{13,5},{2,10},{6,14},... | collective-permute-start | bytes 9830408 | tf_op jit(solution)/shard_map/ppermute | solution.py:174
  506.0 80.5 %collective-permute-start.3 = (f32[5,10,128,128]{3,2,1,0:T(8,128)}, f32[5,10,128,128]{3,2,1,0:T(8,128)}, u32[]{:S(2)}, u32[]{:S(2)}) collective-permute-start(f32[5,10,128,128]{3,2,1,0:T(8,128)} %get-tuple-element.62), channel_id=1, source_target_pairs={{0,12},{4,0},{8,4},{12,8},{1,13},{5,1},{9,5},{13,9},{2,14},{6,2},{... | collective-permute-start | bytes 9830408 | tf_op jit(solution)/shard_map/ppermute | solution.py:174
  564.1 15.4 %copy-start.16 = (s32[20]{0:T(128)S(1)}, s32[20]{0:T(128)}, u32[]{:S(2)}) copy-start(s32[20]{0:T(128)} %select_reduce_fusion.6) | copy-start | bytes 244
  564.1 15.4 %copy-start.17 = (pred[20]{0:T(512)(128)(4,1)S(1)}, pred[20]{0:T(512)(128)(4,1)}, u32[]{:S(2)}) copy-start(pred[20]{0:T(512)(128)(4,1)} %get-tuple-element.113) | copy-start | bytes 64
  564.1 15.5 %copy-start.9 = (s32[48]{0:T(128)S(1)}, s32[48]{0:T(128)}, u32[]{:S(2)}) copy-start(s32[48]{0:T(128)} %copy-done.8) | copy-start | bytes 580
  564.1 15.5 %copy-start.11 = (pred[48]{0:T(512)(128)(4,1)S(1)}, pred[48]{0:T(512)(128)(4,1)}, u32[]{:S(2)}) copy-start(pred[48]{0:T(512)(128)(4,1)} %copy-done.10) | copy-start | bytes 148
  564.1 15.5 %copy-start.18 = (s32[48]{0:T(128)S(1)}, s32[48]{0:T(128)}, u32[]{:S(2)}) copy-start(s32[48]{0:T(128)} %get-tuple-element.111) | copy-start | bytes 580
  564.1 15.6 %copy-start.19 = (pred[20]{0:T(512)(128)(4,1)S(1)}, pred[20]{0:T(512)(128)(4,1)}, u32[]{:S(2)}) copy-start(pred[20]{0:T(512)(128)(4,1)} %get-tuple-element.114) | copy-start | bytes 64
  564.1 15.7 %copy-start.15 = (s32[10]{0:T(128)S(1)}, s32[10]{0:T(128)}, u32[]{:S(2)}) copy-start(s32[10]{0:T(128)} %copy-done.14) | copy-start | bytes 124
  564.1 15.7 %copy-start.23 = (pred[10]{0:T(512)(128)(4,1)S(1)}, pred[10]{0:T(512)(128)(4,1)}, u32[]{:S(2)}) copy-start(pred[10]{0:T(512)(128)(4,1)} %copy-done.22) | copy-start | bytes 34
  564.1 15.7 %copy-start.13 = (s32[10]{0:T(128)S(1)}, s32[10]{0:T(128)}, u32[]{:S(2)}) copy-start(s32[10]{0:T(128)} %copy-done.12) | copy-start | bytes 124
  564.1 15.7 %copy-start.21 = (pred[10]{0:T(512)(128)(4,1)S(1)}, pred[10]{0:T(512)(128)(4,1)}, u32[]{:S(2)}) copy-start(pred[10]{0:T(512)(128)(4,1)} %copy-done.20) | copy-start | bytes 34
  574.5 82.1 %collective-permute-start.4 = (f32[5,10,128,128]{3,2,1,0:T(8,128)}, f32[5,10,128,128]{3,2,1,0:T(8,128)}, u32[]{:S(2)}, u32[]{:S(2)}) collective-permute-start(f32[5,10,128,128]{3,2,1,0:T(8,128)} %get-tuple-element.67), channel_id=1, source_target_pairs={{0,4},{4,8},{8,12},{12,0},{1,5},{5,9},{9,13},{13,1},{2,6},{6,10},{... | collective-permute-start | bytes 9830408 | tf_op jit(solution)/shard_map/ppermute | solution.py:174
  576.0 149.9 %collective-permute-start.5 = (f32[5,10,128,128]{3,2,1,0:T(8,128)}, f32[5,10,128,128]{3,2,1,0:T(8,128)}, u32[]{:S(2)}, u32[]{:S(2)}) collective-permute-start(f32[5,10,128,128]{3,2,1,0:T(8,128)} %get-tuple-element.66), channel_id=1, source_target_pairs={{0,8},{4,12},{8,0},{12,4},{1,9},{5,13},{9,1},{13,5},{2,10},{6,14},... | collective-permute-start | bytes 9830408 | tf_op jit(solution)/shard_map/ppermute | solution.py:174
  577.5 148.7 %collective-permute-start.6 = (f32[5,10,128,128]{3,2,1,0:T(8,128)}, f32[5,10,128,128]{3,2,1,0:T(8,128)}, u32[]{:S(2)}, u32[]{:S(2)}) collective-permute-start(f32[5,10,128,128]{3,2,1,0:T(8,128)} %get-tuple-element.68), channel_id=1, source_target_pairs={{0,12},{4,0},{8,4},{12,8},{1,13},{5,1},{9,5},{13,9},{2,14},{6,2},{... | collective-permute-start | bytes 9830408 | tf_op jit(solution)/shard_map/ppermute | solution.py:174
  595.5 130.7 %copy-start.1 = (f32[1,5,10,128,128]{4,3,2,1,0:T(8,128)S(1)}, f32[1,5,10,128,128]{4,3,2,1,0:T(8,128)}, u32[]{:S(2)}) copy-start(f32[1,5,10,128,128]{4,3,2,1,0:T(8,128)} %get-tuple-element.65) | copy-start | bytes 9830404
  756.9 26.6 %copy-start.5 = (pred[2560]{0:T(1024)(128)(4,1)S(1)}, pred[2560]{0:T(1024)(128)(4,1)}, u32[]{:S(2)}) copy-start(pred[2560]{0:T(1024)(128)(4,1)} %fusion.51) | copy-start | bytes 7684
  803.1 260.9 %all-reduce.8.cloned.1.call-start = ((), (), s32[]{:S(2)}) async-start(), calls=%async_computation.3 | async-start | bytes 5242880 | tf_op jit(solution)/shard_map/psum | solution.py:13
  (3 other events, 25.0 us)
Sparse Core Ops, SparseCore 0:
  10.3 59.3 all-gather.3
  803.2 178.4 all-reduce.5
  985.5 78.4 all-reduce.7

commit v5 on v4

--- a/solution.py
+++ b/solution.py
@@ -79,7 +79,7 @@
     return lax.dot_general(rows, inverse, (((1,), (1,)), ((), ())), precision=lax.Precision.HIGHEST)
 
 
-def early_corner(child_piece, row_map, col_map, own_diagonal):
+def early_corner(child_piece, row_map, col_map, full_diagonal):
     n_row = lax.axis_size("row")
     n_col = lax.axis_size("col")
     n_sub = lax.axis_size("sub")
@@ -111,8 +111,7 @@
         cb = jnp.where(cb < panel_blocks, cb, panel_blocks)
         corner = corner.at[rb[:, None], cb[None, :]].add(pieces[which])
     corner = corner[:panel_blocks, :panel_blocks].transpose(0, 2, 1, 3).reshape(PANEL, PANEL)
-    diagonal = lax.all_gather(own_diagonal, ("sub", "col"), tiled=True)[:PANEL]
-    return corner + jnp.diag(diagonal)
+    return corner + jnp.diag(full_diagonal[:PANEL])
 
 
 def shards(child, row_map, col_map, own_diagonal, coupling):
@@ -137,7 +136,50 @@
     my_rows_map = lax.dynamic_index_in_dim(row_map, my_sub, 0, keepdims=False)
     my_cols_map = lax.dynamic_index_in_dim(col_map, my_sub, 0, keepdims=False)
 
-    corner = early_corner(child_piece, row_map, col_map, own_diagonal)
+    full_diagonal = lax.all_gather(own_diagonal, ("sub", "col"), tiled=True)
+    corner = early_corner(child_piece, row_map, col_map, full_diagonal)
+    global_row = my_row * front_rows + jnp.arange(front_rows, dtype=jnp.int32)
+
+    panel_blocks = PANEL // BLOCK
+    first_cols = min(col_blocks, -(-panel_blocks // n_col))
+    cands = lax.all_gather(child_piece[:, : first_cols * BLOCK], ("sub", "col"))
+    cands = cands.reshape(n_sub, n_col, rows_here, first_cols, BLOCK).transpose(0, 1, 3, 2, 4)
+    cands = cands.reshape(n_sub, n_col * first_cols, rows_here, BLOCK)
+    cand_pos = (
+        jnp.arange(n_col, dtype=jnp.int32)[:, None] * col_blocks
+        + jnp.arange(first_cols, dtype=jnp.int32)[None, :]
+    ).reshape(-1)
+    panel_send = []
+    for which in range(n_sub):
+        found = col_map[which][cand_pos][None, :] == jnp.arange(panel_blocks, dtype=jnp.int32)[:, None]
+        pick = jnp.argmax(found, axis=1)
+        stored = jnp.where(jnp.any(found, axis=1)[:, None, None], cands[which][pick], 0.0)
+        stored = stored.reshape(panel_blocks, row_blocks, BLOCK, BLOCK)
+        pick_rows = sending_table(row_map[which], my_row, row_blocks, front_row_blocks, n_row, row_cap)
+        pick_rows = jnp.minimum(pick_rows, row_blocks - 1).reshape(n_row, row_cap)
+        panel_send.append(stored.at[:, pick_rows].get(mode="promise_in_bounds"))
+    panel_send = jnp.stack(panel_send).transpose(2, 0, 3, 1, 4, 5)
+    pieces = [lax.dynamic_index_in_dim(panel_send, my_row, 0, keepdims=False)]
+    for shift in range(1, n_row):
+        piece = lax.dynamic_index_in_dim(panel_send, (my_row + shift) % n_row, 0, keepdims=False)
+        pieces.append(lax.ppermute(piece, "row", [(i, (i + shift) % n_row) for i in range(n_row)]))
+    panel_got = jnp.stack(pieces)
+    panel_rows = None
+    for which in range(n_sub):
+        placement = receiving_table(
+            row_map[which], my_row, row_blocks, front_row_blocks, row_cap, 0, n_row * row_cap
+        )
+        row_valid = placement < n_row * row_cap
+        source = jnp.minimum(placement, n_row * row_cap - 1) // row_cap
+        placement = ((my_row - source) % n_row) * row_cap + placement % row_cap
+        got = panel_got[:, which].reshape(n_row * row_cap, panel_blocks, BLOCK, BLOCK)
+        got = jnp.where(row_valid[:, None, None, None], got.at[placement].get(mode="promise_in_bounds"), 0.0)
+        panel_rows = got if panel_rows is None else panel_rows + got
+    panel_rows = panel_rows.transpose(0, 2, 1, 3).reshape(front_rows, PANEL)
+    panel_rows = panel_rows + jnp.where(global_row[:, None] >= PANEL, coupling, 0.0)
+    panel_rows = panel_rows + jnp.where(
+        global_row[:, None] == jnp.arange(PANEL, dtype=jnp.int32)[None, :], full_diagonal[None, :PANEL], 0.0
+    )
 
     by_col = child_piece.reshape(rows_here, col_blocks, BLOCK)
     chosen = sending_table(my_cols_map, my_col, col_blocks, front_col_blocks, n_group, col_cap)
@@ -196,7 +238,6 @@
     )
     assembled = assembled.transpose(0, 2, 1, 3).reshape(front_rows, front_cols)
 
-    global_row = my_row * front_rows + jnp.arange(front_rows, dtype=jnp.int32)
     global_col = my_group * front_cols + jnp.arange(front_cols, dtype=jnp.int32)
     on_diagonal = global_row[:, None] == global_col[None, :]
     assembled = assembled + jnp.where(on_diagonal, own_diagonal[None, :], 0.0)
@@ -205,13 +246,11 @@
     )
     coupling_mask = (global_row[:, None] >= PANEL) & (global_col[None, :] < PANEL)
     front_part = assembled + jnp.where(coupling_mask, coupling_wide, 0.0)
-    panel_cols = front_part[:, :PANEL]
     theirs_start = my_group * front_cols % front_rows
     theirs_root = my_group * front_cols // front_rows
-    own_rows = apply_inverse(panel_cols, inverse)
+    own_rows = apply_inverse(panel_rows, inverse)
     top_rows = jnp.where(my_row == 0, lower, own_rows[:PANEL])
     own_rows = jnp.concatenate([top_rows, own_rows[PANEL:]], axis=0)
-    own_rows = from_root(own_rows, ("sub", "col"), 0)
     theirs = lax.dynamic_slice_in_dim(own_rows, theirs_start, front_cols, 0)
     theirs = from_root(theirs, "row", theirs_root)
     update = lax.dot_general(

time: 1110 us -> 981 us (0.88)
  waiting for transfers between devices: 430 us -> 215 us
  local copies, waits for them, and re-layouts: 174 us -> 212 us
  other arithmetic: 177 us -> 206 us
  matrix products: 48.5 us -> 59.9 us
    psum x2 -> x1, waiting for transfers between devices: 257 us -> 10.7 us  [from_root(): return lax.psum(kept, axis)]
    ppermute x6, waiting for transfers between devices: 125 us -> 177 us  [row_receiving(): pieces.append(lax.ppermute(piece, 'row', pairs))]
    all_to_all x1, waiting for transfers between devices: 34.6 us -> 0.01 us  [shards(): lax.all_to_all(own_outgoing, 'col', split_axis=0, concat_axis=0, tiled=True)]
    gather x0 -> x6, local copies, waits for them, and re-layouts: none -> 25.2 us  [the longest x2 11.7 us: shards(): got.at[placement].get(mode='promise_in_bounds')]
    ppermute x0 -> x3, waiting for transfers between devices: none -> 24.1 us  [shards(): lax.ppermute(piece, 'row', [(i, (i + shift) % n_row) for i in range(n_row)])]
    reshape x1, local copies, waits for them, and re-layouts: 26.6 us -> 14.4 us  [shards(): assembled = assembled.transpose(0, 2, 1, 3).reshape(front_rows, front_cols)]
    slice x1 -> x4, local copies, waits for them, and re-layouts: 0.01 us -> 11.9 us  [the longest x1 4.97 us: shards(): panel_got[:, which].reshape(n_row * row_cap, panel_blocks, BLOCK, BLOCK)]
  transfers between devices with their start and end apart: 11 -> 14, of which waited for: 9 -> 9; matrix products, arithmetic and copies ran while one was open for 23% -> 43% of each run, Pallas kernels for 0% -> 0%
where the time goes in v5:
time: 981 us; the launch traced here: 973 us
  blocking collectives  236 us (24%)
  waiting for transfers between devices  215 us (22%)
  local copies, waits for them, and re-layouts  212 us (22%)
  other arithmetic  206 us (21%)
  matrix products  59.9 us (6%)
  starting transfers between devices  24.6 us (3%)
  between operations  18.5 us (2%)
    all_to_all x1, blocking collectives, shards(): lax.all_to_all(outgoing[0], 'col', split_axis=0, concat_axis=0, tiled=True)  211 us
    ppermute x6, waiting for transfers between devices, row_receiving(): pieces.append(lax.ppermute(piece, 'row', pairs))  177 us
    another operation x15, other arithmetic, factor_corner(): lower = jnp.linalg.cholesky(symmetric_of(corner))  80.8 us
    another operation x4, other arithmetic, factor_corner(): jax.scipy.linalg.solve_triangular(lower, jnp.eye(PANEL, dtype=jnp.float32...  44 us
    gather x2, local copies, waits for them, and re-layouts, row_sending(): half.at[col_index[None, None, :], row_index[:, :, None]]  35.5 us
    dot_general x1, matrix products, shards(): lax.dot_general(own_rows, theirs, (((1,), (1,)), ((), ())), precision=lax...  35 us
    all_gather x1, blocking collectives, shards(): full_diagonal = lax.all_gather(own_diagonal, ('sub', 'col'), tiled=True)  25.3 us
    gather x2, local copies, waits for them, and re-layouts, row_receiving(): part = received.at[placement].get(mode='promise_in_bounds')  25.1 us
  transfers between devices with their start and end apart: 14, of which 9 were waited for; matrix products, arithmetic and copies ran while one was open for 43% of the time, Pallas kernels for 0%

profile of v5, /device:TPU:0, one launch (start us, length us, event | category | flops | bytes accessed | tf_op | source)
XLA Modules:
  0.0 973.0 jit_solution(7909669950928913487)
XLA Ops:
  10.7 9.6 copy.44
  21.1 9.7 copy.45
  33.8 25.3 %all-gather.2 = f32[8,1,1280]{2,1,0:T(1,128)S(1)} all-gather(f32[1,1,1280]{2,1,0:T(1,128)S(1)} %reshape.1340), channel_id=1, replica_groups=mesh['sub'=2,'row'=4,'col'=4] {'sub','col'}, dimensions={0}, use_global_device_ids=true | all-gather | bytes 46080 | tf_op jit(solution)/shard_map/all_gather | solution.py:139
  59.2 13.4 %gather_fusion = f32[24,1536,128]{2,1,0:T(8,128)} fusion(f32[1536,12,128]{2,0,1:T(8,128)} %copy.45, s32[1024]{0:T(1024)S(1)} %pad_clamp_fusion.9), kind=kCustom, calls=%fused_computation | custom fusion | bytes 37748832 | tf_op jit(solution)/shard_map/gather | solution.py:188
  81.0 11.0 %slice_bitcast_fusion = (f32[4,3,1536,128]{3,2,1,0:T(8,128)}, f32[4,3,1536,128]{3,2,1,0:T(8,128)S(1)}) fusion(f32[2,4,3,1536,128]{4,3,2,1,0:T(8,128)} %bitcast.331), kind=kLoop, calls=%fused_computation.36 | loop fusion | bytes 37748736 | tf_op jit(solution)/shard_map/squeeze | solution.py:230
  92.0 210.9 %all_to_all.10 = f32[4,3,1536,128]{3,2,1,0:T(8,128)} all-to-all(f32[4,3,1536,128]{3,2,1,0:T(8,128)S(1)} %get-tuple-element.74), channel_id=1, replica_groups=mesh['sub'=2,'row'=4,'col'=4] {'col'}, dimensions={0} | all-to-all | bytes 18874368 | tf_op jit(solution)/shard_map/all_to_all | solution.py:192
  317.9 17.8 %gather_fusion.5 = f32[200,128,128]{2,1,0:T(8,128)} fusion(f32[12,12,128,128]{3,2,1,0:T(8,128)} %bitcast.19, s32[200]{0:T(256)S(1)} %reshape.1238), kind=kCustom, calls=%fused_computation.5 | custom fusion | bytes 26216000 | tf_op jit(solution)/shard_map/gather | solution.py:206
  348.8 11.7 %cholesky.103 = f32[128,128]{1,0:T(8,128)S(1)} custom-call(f32[128,128]{1,0:T(8,128)S(1)} %cholesky.263), custom_call_target="Cholesky" | custom-call | tf_op jit(solution)/shard_map/jit(cholesky)/cholesky | solution.py:71
  361.2 9.8 %custom-call.31 = f32[1,128,128]{1,2,0:T(8,128)S(1)} custom-call(f32[1,128,128]{2,1,0:T(8,128)S(1)} %get-tuple-element.102), custom_call_target="InvertDiagBlocksLowerTriangular" | custom-call | tf_op jit(solution)/shard_map/jit(cholesky)/cholesky | solution.py:71
  371.7 11.7 %cholesky.215 = f32[128,128]{1,0:T(8,128)S(1)} custom-call(f32[128,128]{1,0:T(8,128)S(1)} %cholesky.267), custom_call_target="Cholesky" | custom-call | tf_op jit(solution)/shard_map/jit(cholesky)/cholesky | solution.py:71
  383.4 10.0 %custom-call.32 = f32[1,128,128]{1,2,0:T(8,128)S(1)} custom-call(f32[1,128,128]{2,1,0:T(8,128)S(1)} %get-tuple-element.99), custom_call_target="InvertDiagBlocksLowerTriangular" | custom-call | tf_op jit(solution)/shard_map/jit(cholesky)/cholesky | solution.py:71
  394.1 11.7 %cholesky.236 = f32[128,128]{1,0:T(8,128)S(1)} custom-call(f32[128,128]{1,0:T(8,128)S(1)} %cholesky.272), custom_call_target="Cholesky" | custom-call | tf_op jit(solution)/shard_map/jit(cholesky)/cholesky | solution.py:71
  406.4 9.8 %custom-call.33 = f32[1,128,128]{1,2,0:T(8,128)S(1)} custom-call(f32[1,128,128]{2,1,0:T(8,128)S(1)} %get-tuple-element.96), custom_call_target="InvertDiagBlocksLowerTriangular" | custom-call | tf_op jit(solution)/shard_map/jit(cholesky)/cholesky | solution.py:71
  416.8 12.1 %cholesky.253 = f32[128,128]{1,0:T(8,128)S(1)} custom-call(f32[128,128]{1,0:T(8,128)S(1)} %convolution_subtract_fusion.6), custom_call_target="Cholesky" | custom-call | tf_op jit(solution)/shard_map/jit(cholesky)/cholesky | solution.py:71
  473.0 9.1 constant_dynamic-slice_fusion.3
  484.0 16.9 %while.1 = (s32[]{:T(128)}, f32[512,512]{1,0:T(8,128)}, s32[4,2]{0,1:T(2,128)}, f32[4,128,128]{2,1,0:T(8,128)}, s32[]{:T(128)}) while((s32[]{:T(128)}, f32[512,512]{1,0:T(8,128)}, s32[4,2]{0,1:T(2,128)}, f32[4,128,128]{2,1,0:T(8,128)}, s32[]{:T(128)}) %tuple.103), condition=%wide.while_cond, body=%wide.while_body.sunk | while | flops 2 | bytes 132705 | solution.py:72
  500.8 40.8 %custom-call.34 = f32[4,128,128]{1,2,0:T(8,128)} custom-call(f32[4,128,128]{2,1,0:T(8,128)} %get-tuple-element.30), custom_call_target="InvertDiagBlocksLowerTriangular" | custom-call | tf_op jit(solution)/shard_map/jit(_solve_triangular)/triangular_solve | solution.py:72
  555.3 24.1 %collective-permute-done.2 = f32[2,5,4,128,128]{4,3,2,1,0:T(8,128)} collective-permute-done((f32[2,5,4,128,128]{4,3,2,1,0:T(8,128)}, f32[2,5,4,128,128]{4,3,2,1,0:T(8,128)}, u32[]{:S(2)}, u32[]{:S(2)}) %collective-permute-start.2) | collective-permute-done | bytes 2621472 | tf_op jit(solution)/shard_map/ppermute | solution.py:165
  600.4 17.7 %gather_fusion.13 = f32[200,128,128]{2,1,0:T(8,128)} fusion(f32[12,12,128,128]{3,2,1,0:T(8,128)} %bitcast.108, s32[200]{0:T(256)S(1)} %reshape.1300), kind=kCustom, calls=%fused_computation.13 | custom fusion | bytes 26216000 | tf_op jit(solution)/shard_map/gather | solution.py:206
  618.1 10.4 %constant_dynamic-slice_fusion.1 = (f32[1,5,10,128,128]{4,3,2,1,0:T(8,128)}, f32[5,10,128,128]{3,2,1,0:T(8,128)}, f32[5,10,128,128]{3,2,1,0:T(8,128)}, f32[5,10,128,128]{3,2,1,0:T(8,128)}) fusion(f32[4,5,10,128,128]{4,3,2,1,0:T(8,128)} %bitcast.333, s32[]{:T(128)S(6)} %select_n.910, s32[]{:T(128)S(6)} %select_n.914, s32[]{:T(128)S(6)} %select_n.912, ...), kind=kLoop, calls=%fused_computation.202 | loop fusion | bytes 26214416 | tf_op jit(solution)/shard_map/jit(dynamic_index_in_dim)/dynamic_slice | solution.py:212
  637.5 12.1 %collective-permute-done.4 = f32[5,10,128,128]{3,2,1,0:T(8,128)} collective-permute-done((f32[5,10,128,128]{3,2,1,0:T(8,128)}, f32[5,10,128,128]{3,2,1,0:T(8,128)}, u32[]{:S(2)}, u32[]{:S(2)}) %collective-permute-start.4) | collective-permute-done | bytes 3276832 | tf_op jit(solution)/shard_map/ppermute | solution.py:216
  662.7 57.2 %collective-permute-done.5 = f32[5,10,128,128]{3,2,1,0:T(8,128)} collective-permute-done((f32[5,10,128,128]{3,2,1,0:T(8,128)}, f32[5,10,128,128]{3,2,1,0:T(8,128)}, u32[]{:S(2)}, u32[]{:S(2)}) %collective-permute-start.5) | collective-permute-done | bytes 3276832 | tf_op jit(solution)/shard_map/ppermute | solution.py:216
  719.9 9.3 pad_maximum_fusion
  729.2 12.6 %gather_fusion.12 = f32[20,10,128,128]{3,2,1,0:T(8,128)} fusion(f32[20,10,128,128]{3,2,1,0:T(8,128)} %bitcast.334, s32[1024]{0:T(1024)} %pad_clamp_fusion.1), kind=kCustom, calls=%fused_computation.12 | custom fusion | bytes 26214480 | tf_op jit(solution)/shard_map/gather | solution.py:225
  741.8 13.7 %fusion.4 = f32[2560,512]{1,0:T(8,128)S(1)} fusion(f32[512,512]{1,0:T(8,128)S(1)} %copy-done.4, f32[320,8,4,128]{3,2,1,0:T(4,128)} %bitcast.337, f32[2560,512]{1,0:T(8,128)} %param.9, f32[512]{0:T(512)S(1)} %copy-done.8, s32[2560]{0:T(1024)S(1)} %iota_add_fusion, pred[2560]{0:T(1024)(128)(4,1)S(1)} %copy-done.9), kind=kOutput, calls=%fused_computation.43 | convolution fusion | flops 8059617280 | bytes 16792064 | tf_op jit(solution)/shard_map/dot_general | solution.py:79
  766.2 37.8 %collective-permute-done.7 = f32[5,10,128,128]{3,2,1,0:T(8,128)} collective-permute-done((f32[5,10,128,128]{3,2,1,0:T(8,128)}, f32[5,10,128,128]{3,2,1,0:T(8,128)}, u32[]{:S(2)}, u32[]{:S(2)}) %collective-permute-start.7) | collective-permute-done | bytes 3276832 | tf_op jit(solution)/shard_map/ppermute | solution.py:216
  804.0 69.5 %collective-permute-done.8 = f32[5,10,128,128]{3,2,1,0:T(8,128)} collective-permute-done((f32[5,10,128,128]{3,2,1,0:T(8,128)}, f32[5,10,128,128]{3,2,1,0:T(8,128)}, u32[]{:S(2)}, u32[]{:S(2)}) %collective-permute-start.8) | collective-permute-done | bytes 3276832 | tf_op jit(solution)/shard_map/ppermute | solution.py:216
  882.7 12.5 %gather_fusion.14 = f32[20,10,128,128]{3,2,1,0:T(8,128)} fusion(f32[20,10,128,128]{3,2,1,0:T(8,128)} %bitcast.335, s32[1024]{0:T(1024)} %pad_clamp_fusion), kind=kCustom, calls=%fused_computation.14 | custom fusion | bytes 26214480 | tf_op jit(solution)/shard_map/gather | solution.py:225
  895.3 9.9 %add_bitcast_fusion = f32[20,128,10,128]{3,1,2,0:T(8,128)S(1)} fusion(f32[20,10,128,128]{3,2,1,0:T(8,128)} %gather_fusion.14, f32[20,10,128,128]{3,2,1,0:T(8,128)} %gather_fusion.12, pred[20,10]{1,0:T(8,128)(4,1)S(1)} %copy-done.10, pred[20,10]{1,0:T(8,128)(4,1)S(1)} %copy-done.11), kind=kLoop, calls=%fused_computation.34 | loop fusion | flops 9830400 | bytes 39322000 | tf_op jit(solution)/shard_map/add | solution.py:236
  905.2 14.4 %copy.55 = f32[20,128,10,128]{3,2,1,0:T(8,128)} copy(f32[20,128,10,128]{3,1,2,0:T(8,128)S(1)} %add_bitcast_fusion) | data formatting | bytes 26214400 | tf_op jit(solution)/shard_map/reshape | solution.py:239
  919.6 10.7 %all-reduce.5.cloned.1.call-done = f32[1280,512]{1,0:T(8,128)} async-done(((f32[1280,512]{1,0:T(8,128)}), f32[1280,512]{1,0:T(8,128)}) %all-reduce.5.cloned.1.call-update) | async-done | bytes 2621456 | tf_op jit(solution)/shard_map/psum | solution.py:13
  930.4 35.0 %fusion.1 = f32[2560,1280]{1,0:T(8,128)} fusion(f32[2560,512]{1,0:T(8,128)} %pad_maximum_fusion.3, f32[1280,512]{1,0:T(8,128)} %all-reduce.5.cloned.1.call-done, f32[320,8,10,128]{3,2,1,0:T(8,128)} %bitcast.340, f32[2560,512]{1,0:T(8,128)} %param.9, f32[1280]{0:T(1024)S(1)} %copy-done.17, s32[1280]{0:T(1024)S(1)} %copy-done.15, s32[2560]{0:T(1024)S(1)} %iota_add_fusion, ...), kind=kOutput, calls=%fused_computation.29 | convolution fusion | flops 20162150400 | bytes 39348480 | tf_op jit(solution)/shard_map/dot_general | solution.py:256
  (265 shorter events, 183.2 us)
Async XLA Ops:
  7.4 65.2 %all-gather.6.cloned.1.call-start = ((), (), s32[]{:S(2)}) async-start(), calls=%async_computation.3 | async-start | bytes 2162688 | tf_op jit(solution)/shard_map/all_gather | solution.py:93
  8.9 421.7 %all-gather.8.cloned.1.call-start = ((), (), s32[]{:S(2)}) async-start(), calls=%async_computation.4 | async-start | bytes 7077888 | tf_op jit(solution)/shard_map/all_gather | solution.py:145
  21.1 10.4 %copy-start.12 = (s32[2,48]{1,0:T(2,128)S(1)}, s32[2,48]{1,0:T(2,128)}, u32[]{:S(2)}) copy-start(s32[2,48]{1,0:T(2,128)} %param.7) | copy-start | bytes 1156
  21.1 12.7 %copy-start.16 = (f32[1280]{0:T(1024)S(1)}, f32[1280]{0:T(1024)}, u32[]{:S(2)}) copy-start(f32[1280]{0:T(1024)} %param.8) | copy-start | bytes 15364
  59.2 21.7 %copy-start.7 = (f32[512]{0:T(512)}, f32[512]{0:T(512)S(1)}, u32[]{:S(2)}) copy-start(f32[512]{0:T(512)S(1)} %slice.250) | copy-start | bytes 6148
  302.9 15.0 %collective-permute-start = (f32[4,3,1536,128]{3,2,1,0:T(8,128)}, f32[4,3,1536,128]{3,2,1,0:T(8,128)}, u32[]{:S(2)}, u32[]{:S(2)}) collective-permute-start(f32[4,3,1536,128]{3,2,1,0:T(8,128)} %all_to_all.10), channel_id=1, source_target_pairs={{0,16},{16,0},{1,17},{17,1},{2,18},{18,2},{3,19},{19,3},{4,20},{20... | collective-permute-start | bytes 28311560 | tf_op jit(solution)/shard_map/ppermute | solution.py:193
  335.7 264.8 %all-to-all-start.1 = ((f32[4,3,1536,128]{3,2,1,0:T(8,128)}), f32[4,3,1536,128]{3,2,1,0:T(8,128)}, u32[]{:S(2)}, u32[]{:S(2)}) async-start(f32[4,3,1536,128]{3,2,1,0:T(8,128)} %get-tuple-element.15), calls=%async_computation.1 | async-start | bytes 18874368 | tf_op jit(solution)/shard_map/all_to_all | solution.py:232
  341.5 588.9 %all-reduce.5.cloned.1.call-start = ((), (), s32[]{:S(2)}) async-start(), calls=%async_computation.2 | async-start | bytes 5242880 | tf_op jit(solution)/shard_map/psum | solution.py:13
  416.4 13.1 %copy-start.2 = (f32[512,512]{1,0:T(8,128)}, f32[512,512]{1,0:T(8,128)S(1)}, u32[]{:S(2)}) copy-start(f32[512,512]{1,0:T(8,128)S(1)} %convolution_dynamic-update-slice_fusion.1) | copy-start | bytes 3145732
  453.7 12.1 %copy-start.25 = (f32[128]{0:T(128)S(1)}, f32[128]{0:T(128)}, u32[]{:S(2)}) copy-start(f32[128]{0:T(128)} %get-tuple-element.95) | copy-start | bytes 1540
  453.7 13.5 %copy-start.3 = (f32[512,512]{1,0:T(8,128)S(1)}, f32[512,512]{1,0:T(8,128)}, u32[]{:S(2)}) copy-start(f32[512,512]{1,0:T(8,128)} %copy-done.2) | copy-start | bytes 3145732
  462.2 81.3 %collective-permute-start.1 = (f32[2,5,4,128,128]{4,3,2,1,0:T(8,128)}, f32[2,5,4,128,128]{4,3,2,1,0:T(8,128)}, u32[]{:S(2)}, u32[]{:S(2)}) collective-permute-start(f32[2,5,4,128,128]{4,3,2,1,0:T(8,128)} %get-tuple-element.86), channel_id=1, source_target_pairs={{0,4},{4,8},{8,12},{12,0},{1,5},{5,9},{9,13},{13,1},{2,6},{6,10},{... | collective-permute-start | bytes 7864328 | tf_op jit(solution)/shard_map/ppermute | solution.py:165
  470.2 109.2 %collective-permute-start.2 = (f32[2,5,4,128,128]{4,3,2,1,0:T(8,128)}, f32[2,5,4,128,128]{4,3,2,1,0:T(8,128)}, u32[]{:S(2)}, u32[]{:S(2)}) collective-permute-start(f32[2,5,4,128,128]{4,3,2,1,0:T(8,128)} %get-tuple-element.87), channel_id=1, source_target_pairs={{0,8},{4,12},{8,0},{12,4},{1,9},{5,13},{9,1},{13,5},{2,10},{6,14},... | collective-permute-start | bytes 7864328 | tf_op jit(solution)/shard_map/ppermute | solution.py:165
  471.6 107.8 %collective-permute-start.3 = (f32[2,5,4,128,128]{4,3,2,1,0:T(8,128)}, f32[2,5,4,128,128]{4,3,2,1,0:T(8,128)}, u32[]{:S(2)}, u32[]{:S(2)}) collective-permute-start(f32[2,5,4,128,128]{4,3,2,1,0:T(8,128)} %get-tuple-element.88), channel_id=1, source_target_pairs={{0,12},{4,0},{8,4},{12,8},{1,13},{5,1},{9,5},{13,9},{2,14},{6,2},{... | collective-permute-start | bytes 7864328 | tf_op jit(solution)/shard_map/ppermute | solution.py:165
  482.1 167.5 %collective-permute-start.4 = (f32[5,10,128,128]{3,2,1,0:T(8,128)}, f32[5,10,128,128]{3,2,1,0:T(8,128)}, u32[]{:S(2)}, u32[]{:S(2)}) collective-permute-start(f32[5,10,128,128]{3,2,1,0:T(8,128)} %get-tuple-element.78), channel_id=1, source_target_pairs={{0,4},{4,8},{8,12},{12,0},{1,5},{5,9},{9,13},{13,1},{2,6},{6,10},{... | collective-permute-start | bytes 9830408 | tf_op jit(solution)/shard_map/ppermute | solution.py:216
  542.7 177.1 %collective-permute-start.5 = (f32[5,10,128,128]{3,2,1,0:T(8,128)}, f32[5,10,128,128]{3,2,1,0:T(8,128)}, u32[]{:S(2)}, u32[]{:S(2)}) collective-permute-start(f32[5,10,128,128]{3,2,1,0:T(8,128)} %get-tuple-element.77), channel_id=1, source_target_pairs={{0,8},{4,12},{8,0},{12,4},{1,9},{5,13},{9,1},{13,5},{2,10},{6,14},... | collective-permute-start | bytes 9830408 | tf_op jit(solution)/shard_map/ppermute | solution.py:216
  543.5 176.4 %collective-permute-start.6 = (f32[5,10,128,128]{3,2,1,0:T(8,128)}, f32[5,10,128,128]{3,2,1,0:T(8,128)}, u32[]{:S(2)}, u32[]{:S(2)}) collective-permute-start(f32[5,10,128,128]{3,2,1,0:T(8,128)} %get-tuple-element.76), channel_id=1, source_target_pairs={{0,12},{4,0},{8,4},{12,8},{1,13},{5,1},{9,5},{13,9},{2,14},{6,2},{... | collective-permute-start | bytes 9830408 | tf_op jit(solution)/shard_map/ppermute | solution.py:216
  618.1 32.9 %copy-start.19 = (pred[20]{0:T(512)(128)(4,1)S(1)}, pred[20]{0:T(512)(128)(4,1)}, u32[]{:S(2)}) copy-start(pred[20]{0:T(512)(128)(4,1)} %get-tuple-element.153) | copy-start | bytes 64
  618.1 32.9 %copy-start.20 = (pred[20]{0:T(512)(128)(4,1)S(1)}, pred[20]{0:T(512)(128)(4,1)}, u32[]{:S(2)}) copy-start(pred[20]{0:T(512)(128)(4,1)} %get-tuple-element.154) | copy-start | bytes 64
  628.5 175.5 %collective-permute-start.7 = (f32[5,10,128,128]{3,2,1,0:T(8,128)}, f32[5,10,128,128]{3,2,1,0:T(8,128)}, u32[]{:S(2)}, u32[]{:S(2)}) collective-permute-start(f32[5,10,128,128]{3,2,1,0:T(8,128)} %get-tuple-element.81), channel_id=1, source_target_pairs={{0,4},{4,8},{8,12},{12,0},{1,5},{5,9},{9,13},{13,1},{2,6},{6,10},{... | collective-permute-start | bytes 9830408 | tf_op jit(solution)/shard_map/ppermute | solution.py:216
  636.9 236.6 %collective-permute-start.8 = (f32[5,10,128,128]{3,2,1,0:T(8,128)}, f32[5,10,128,128]{3,2,1,0:T(8,128)}, u32[]{:S(2)}, u32[]{:S(2)}) collective-permute-start(f32[5,10,128,128]{3,2,1,0:T(8,128)} %get-tuple-element.80), channel_id=1, source_target_pairs={{0,8},{4,12},{8,0},{12,4},{1,9},{5,13},{9,1},{13,5},{2,10},{6,14},... | collective-permute-start | bytes 9830408 | tf_op jit(solution)/shard_map/ppermute | solution.py:216
  649.6 224.0 %collective-permute-start.9 = (f32[5,10,128,128]{3,2,1,0:T(8,128)}, f32[5,10,128,128]{3,2,1,0:T(8,128)}, u32[]{:S(2)}, u32[]{:S(2)}) collective-permute-start(f32[5,10,128,128]{3,2,1,0:T(8,128)} %get-tuple-element.82), channel_id=1, source_target_pairs={{0,12},{4,0},{8,4},{12,8},{1,13},{5,1},{9,5},{13,9},{2,14},{6,2},{... | collective-permute-start | bytes 9830408 | tf_op jit(solution)/shard_map/ppermute | solution.py:216
  729.2 12.6 %copy-start.4 = (f32[512,512]{1,0:T(8,128)S(1)}, f32[512,512]{1,0:T(8,128)}, u32[]{:S(2)}) copy-start(f32[512,512]{1,0:T(8,128)} %pad_maximum_fusion.4) | copy-start | bytes 3145732
  729.2 12.6 %copy-start.8 = (f32[512]{0:T(512)S(1)}, f32[512]{0:T(512)}, u32[]{:S(2)}) copy-start(f32[512]{0:T(512)} %copy-done.7) | copy-start | bytes 6148
  729.2 12.6 %copy-start.9 = (pred[2560]{0:T(1024)(128)(4,1)S(1)}, pred[2560]{0:T(1024)(128)(4,1)}, u32[]{:S(2)}) copy-start(pred[2560]{0:T(1024)(128)(4,1)} %fusion.79) | copy-start | bytes 7684
  761.0 112.6 %copy-start.1 = (f32[1,5,10,128,128]{4,3,2,1,0:T(8,128)S(1)}, f32[1,5,10,128,128]{4,3,2,1,0:T(8,128)}, u32[]{:S(2)}) copy-start(f32[1,5,10,128,128]{4,3,2,1,0:T(8,128)} %get-tuple-element.79) | copy-start | bytes 9830404
  882.7 12.5 %copy-start.10 = (pred[20,10]{1,0:T(8,128)(4,1)S(1)}, pred[20,10]{1,0:T(8,128)(4,1)}, u32[]{:S(2)}) copy-start(pred[20,10]{1,0:T(8,128)(4,1)} %broadcast_and_fusion) | copy-start | bytes 604
  882.7 12.6 %copy-start.11 = (pred[20,10]{1,0:T(8,128)(4,1)S(1)}, pred[20,10]{1,0:T(8,128)(4,1)}, u32[]{:S(2)}) copy-start(pred[20,10]{1,0:T(8,128)(4,1)} %broadcast_and_fusion.1) | copy-start | bytes 604
  905.2 25.2 %copy-start.15 = (s32[1280]{0:T(1024)S(1)}, s32[1280]{0:T(1024)}, u32[]{:S(2)}) copy-start(s32[1280]{0:T(1024)} %iota_add_fusion.1) | copy-start | bytes 15364
  905.2 25.2 %copy-start.17 = (f32[1280]{0:T(1024)S(1)}, f32[1280]{0:T(1024)}, u32[]{:S(2)}) copy-start(f32[1280]{0:T(1024)} %param.8) | copy-start | bytes 15364
  905.2 25.2 %copy-start.18 = (pred[2560]{0:T(1024)(128)(4,1)S(1)}, pred[2560]{0:T(1024)(128)(4,1)}, u32[]{:S(2)}) copy-start(pred[2560]{0:T(1024)(128)(4,1)} %fusion.78) | copy-start | bytes 7684
  905.2 25.1 %copy-start.21 = (pred[1280]{0:T(1024)(128)(4,1)S(1)}, pred[1280]{0:T(1024)(128)(4,1)}, u32[]{:S(2)}) copy-start(pred[1280]{0:T(1024)(128)(4,1)} %broadcast_compare_fusion) | copy-start | bytes 3844
  (8 other events, 41.9 us)
Sparse Core Ops, SparseCore 0:
  11.2 59.2 all-gather.5
  761.1 169.1 all-reduce.4
Sparse Core Ops, SparseCore 1:
  305.1 125.5 all-gather.7

commit v6 on v5

--- a/solution.py
+++ b/solution.py
@@ -159,6 +159,15 @@
         pick_rows = jnp.minimum(pick_rows, row_blocks - 1).reshape(n_row, row_cap)
         panel_send.append(stored.at[:, pick_rows].get(mode="promise_in_bounds"))
     panel_send = jnp.stack(panel_send).transpose(2, 0, 3, 1, 4, 5)
+
+    by_col = child_piece.reshape(rows_here, col_blocks, BLOCK)
+    chosen = sending_table(my_cols_map, my_col, col_blocks, front_col_blocks, n_group, col_cap)
+    chosen = jnp.minimum(chosen, col_blocks - 1).reshape(n_sub, n_col * col_cap)
+    chosen = jnp.stack([chosen[1 - my_sub], chosen[my_sub]]).reshape(-1)
+    outgoing = by_col.at[:, chosen].get(mode="promise_in_bounds")
+    outgoing = outgoing.transpose(1, 0, 2).reshape(2, n_col, col_cap, rows_here, BLOCK)
+    outgoing, corner, panel_send = lax.optimization_barrier((outgoing, corner, panel_send))
+    lower, inverse = factor_corner(corner)
     pieces = [lax.dynamic_index_in_dim(panel_send, my_row, 0, keepdims=False)]
     for shift in range(1, n_row):
         piece = lax.dynamic_index_in_dim(panel_send, (my_row + shift) % n_row, 0, keepdims=False)
@@ -180,16 +189,8 @@
     panel_rows = panel_rows + jnp.where(
         global_row[:, None] == jnp.arange(PANEL, dtype=jnp.int32)[None, :], full_diagonal[None, :PANEL], 0.0
     )
-
-    by_col = child_piece.reshape(rows_here, col_blocks, BLOCK)
-    chosen = sending_table(my_cols_map, my_col, col_blocks, front_col_blocks, n_group, col_cap)
-    chosen = jnp.minimum(chosen, col_blocks - 1).reshape(n_sub, n_col * col_cap)
-    chosen = jnp.stack([chosen[1 - my_sub], chosen[my_sub]]).reshape(-1)
-    outgoing = by_col.at[:, chosen].get(mode="promise_in_bounds")
-    outgoing = outgoing.transpose(1, 0, 2).reshape(2, n_col, col_cap, rows_here, BLOCK)
-    outgoing, corner = lax.optimization_barrier((outgoing, corner))
-    lower, inverse = factor_corner(corner)
     other_half = lax.all_to_all(outgoing[0], "col", split_axis=0, concat_axis=0, tiled=True)
+    other_half, lower, inverse = lax.optimization_barrier((other_half, lower, inverse))
     other_half = lax.ppermute(other_half, "sub", [(0, 1), (1, 0)])
 
     def row_sending(half, which):
@@ -208,31 +209,35 @@
         )
         return sending, col_valid, rows_of
 
-    def row_receiving(sending, col_valid, rows_of):
-        pieces = [lax.dynamic_index_in_dim(sending, my_row, 0, keepdims=False)]
-        for shift in range(1, n_row):
-            piece = lax.dynamic_index_in_dim(sending, (my_row + shift) % n_row, 0, keepdims=False)
-            pairs = [(i, (i + shift) % n_row) for i in range(n_row)]
-            pieces.append(lax.ppermute(piece, "row", pairs))
-        received = jnp.stack(pieces).reshape(n_row * row_cap, front_col_blocks, BLOCK, BLOCK)
+    def row_receiving(sending, col_valid, rows_of, by_permutes):
         placement = receiving_table(
             rows_of, my_row, row_blocks, front_row_blocks, row_cap, 0, n_row * row_cap
         )
         row_valid = placement < n_row * row_cap
-        source = jnp.minimum(placement, n_row * row_cap - 1) // row_cap
-        slot = placement % row_cap
-        placement = ((my_row - source) % n_row) * row_cap + slot
+        placement = jnp.minimum(placement, n_row * row_cap - 1)
+        if by_permutes:
+            pieces = [lax.dynamic_index_in_dim(sending, my_row, 0, keepdims=False)]
+            for shift in range(1, n_row):
+                piece = lax.dynamic_index_in_dim(sending, (my_row + shift) % n_row, 0, keepdims=False)
+                pairs = [(i, (i + shift) % n_row) for i in range(n_row)]
+                pieces.append(lax.ppermute(piece, "row", pairs))
+            received = jnp.stack(pieces)
+            source = placement // row_cap
+            placement = ((my_row - source) % n_row) * row_cap + placement % row_cap
+        else:
+            received = lax.all_to_all(sending, "row", split_axis=0, concat_axis=0, tiled=True)
+        received = received.reshape(n_row * row_cap, front_col_blocks, BLOCK, BLOCK)
         part = received.at[placement].get(mode="promise_in_bounds")
         keep = row_valid[:, None] & col_valid[None, :]
         return part, keep
 
     sending_other, col_valid_other, rows_other = row_sending(other_half, 1 - my_sub)
     sending_other, own_outgoing = lax.optimization_barrier((sending_other, outgoing[1]))
-    part_other, keep_other = row_receiving(sending_other, col_valid_other, rows_other)
+    part_other, keep_other = row_receiving(sending_other, col_valid_other, rows_other, True)
     own_half = lax.all_to_all(own_outgoing, "col", split_axis=0, concat_axis=0, tiled=True)
-    own_half, lower, inverse = lax.optimization_barrier((own_half, lower, inverse))
+    own_half, part_other, panel_rows = lax.optimization_barrier((own_half, part_other, panel_rows))
     sending_own, col_valid_own, rows_own = row_sending(own_half, my_sub)
-    part_own, keep_own = row_receiving(sending_own, col_valid_own, rows_own)
+    part_own, keep_own = row_receiving(sending_own, col_valid_own, rows_own, False)
     assembled = jnp.where(keep_other[:, :, None, None], part_other, 0.0) + jnp.where(
         keep_own[:, :, None, None], part_own, 0.0
     )

time: 981 us -> 1000 us (1.019)
  waiting for transfers between devices: 215 us -> 474 us
  blocking collectives: 236 us -> 25.3 us
  other arithmetic: 206 us -> 193 us
    all_to_all x1 -> x0, blocking collectives: 211 us -> none  [shards(): lax.all_to_all(outgoing[0], 'col', split_axis=0, concat_axis=0, tiled=True)]
    all_to_all x0 -> x2, waiting for transfers between devices: none -> 203 us  [the longest x1 143 us: row_receiving(): lax.all_to_all(sending, 'row', split_axis=0, concat_axis=0, tiled=True)]
    ppermute x3, waiting for transfers between devices: 24.1 us -> 99.5 us  [shards(): lax.ppermute(piece, 'row', [(i, (i + shift) % n_row) for i in range(n_row)])]
    ppermute x6 -> x3, waiting for transfers between devices: 177 us -> 103 us  [row_receiving(): pieces.append(lax.ppermute(piece, 'row', pairs))]
    all_gather x1, waiting for transfers between devices: 1.02 us -> 50.1 us  [shards(): cands = lax.all_gather(child_piece[:, :first_cols * BLOCK], ('sub', 'col'))]
    transpose x0 -> x2, other arithmetic: none -> 18.8 us  [the longest x1 9.53 us: shards(): panel_send = jnp.stack(panel_send).transpose(2, 0, 3, 1, 4, 5)]
    all_to_all x0 -> x2, starting transfers between devices: none -> 12.8 us  [the longest x1 6.63 us: row_receiving(): lax.all_to_all(sending, 'row', split_axis=0, concat_axis=0, tiled=True)]
    ppermute x1, waiting for transfers between devices: 2.7 us -> 14.3 us  [shards(): other_half = lax.ppermute(other_half, 'sub', [(0, 1), (1, 0)])]
  transfers between devices with their start and end apart: 14 -> 13, of which waited for: 9 -> 10; matrix products, arithmetic and copies ran while one was open for 43% -> 33% of each run, Pallas kernels for 0% -> 0%
where the time goes in v6:
time: 1000 us; the launch traced here: 990 us
  waiting for transfers between devices  474 us (47%)
  local copies, waits for them, and re-layouts  203 us (20%)
  other arithmetic  193 us (19%)
  matrix products  51.2 us (5%)
  starting transfers between devices  26.1 us (3%)
  blocking collectives  25.3 us (3%)
  between operations  17 us (2%)
    all_to_all x1, waiting for transfers between devices, row_receiving(): lax.all_to_all(sending, 'row', split_axis=0, concat_axis=0, tiled=True)  143 us
    ppermute x3, waiting for transfers between devices, row_receiving(): pieces.append(lax.ppermute(piece, 'row', pairs))  103 us
    ppermute x3, waiting for transfers between devices, shards(): lax.ppermute(piece, 'row', [(i, (i + shift) % n_row) for i in range(n_row)])  99.5 us
    another operation x15, other arithmetic, factor_corner(): lower = jnp.linalg.cholesky(symmetric_of(corner))  79.8 us
    all_to_all x1, waiting for transfers between devices, shards(): lax.all_to_all(outgoing[0], 'col', split_axis=0, concat_axis=0, tiled=True)  59.9 us
    all_gather x1, waiting for transfers between devices, shards(): cands = lax.all_gather(child_piece[:, :first_cols * BLOCK], ('sub', 'col'))  50.1 us
    another operation x4, other arithmetic, factor_corner(): jax.scipy.linalg.solve_triangular(lower, jnp.eye(PANEL, dtype=jnp.float32...  43 us
    gather x2, local copies, waits for them, and re-layouts, row_sending(): half.at[col_index[None, None, :], row_index[:, :, None]]  35.6 us
  transfers between devices with their start and end apart: 13, of which 10 were waited for; matrix products, arithmetic and copies ran while one was open for 33% of the time, Pallas kernels for 0%

profile of v6, /device:TPU:0, one launch (start us, length us, event | category | flops | bytes accessed | tf_op | source)
XLA Modules:
  0.0 989.7 jit_solution(10651659385161085736)
XLA Ops:
  10.2 9.6 copy.32
  23.9 9.6 copy.33
  35.2 25.3 %all-gather.2 = f32[8,1,1280]{2,1,0:T(1,128)S(1)} all-gather(f32[1,1,1280]{2,1,0:T(1,128)S(1)} %reshape.1233), channel_id=1, replica_groups=mesh['sub'=2,'row'=4,'col'=4] {'sub','col'}, dimensions={0}, use_global_device_ids=true | all-gather | bytes 46080 | tf_op jit(solution)/shard_map/all_gather | solution.py:139
  60.4 13.2 %gather_fusion = f32[24,1536,128]{2,1,0:T(8,128)} fusion(f32[1536,12,128]{2,0,1:T(8,128)} %copy.33, s32[1024]{0:T(1024)S(1)} %pad_clamp_fusion.9), kind=kCustom, calls=%fused_computation | custom fusion | bytes 37748832 | tf_op jit(solution)/shard_map/gather | solution.py:167
  84.8 50.1 %all-gather.8.cloned.1.call-done = f32[12288,128]{1,0:T(8,128)} async-done(((f32[1536,128]{1,0:T(8,128)}), f32[12288,128]{1,0:T(8,128)}) %all-gather.8.cloned.1.call-update) | async-done | bytes 6291472 | tf_op jit(solution)/shard_map/all_gather | solution.py:145
  157.6 9.5 maximum_bitcast_fusion
  167.1 13.4 %slice_bitcast_fusion = (f32[4,3,1536,128]{3,2,1,0:T(8,128)}, f32[4,3,1536,128]{3,2,1,0:T(8,128)}) fusion(f32[2,4,3,1536,128]{4,3,2,1,0:T(8,128)} %bitcast.301), kind=kLoop, calls=%fused_computation.28 | loop fusion | bytes 37748736 | tf_op jit(solution)/shard_map/squeeze | solution.py:235
  190.4 11.7 %cholesky.103 = f32[128,128]{1,0:T(8,128)S(1)} custom-call(f32[128,128]{1,0:T(8,128)S(1)} %cholesky.263), custom_call_target="Cholesky" | custom-call | tf_op jit(solution)/shard_map/jit(cholesky)/cholesky | solution.py:71
  202.3 9.8 custom-call.31
  212.8 11.7 %cholesky.215 = f32[128,128]{1,0:T(8,128)S(1)} custom-call(f32[128,128]{1,0:T(8,128)S(1)} %cholesky.267), custom_call_target="Cholesky" | custom-call | tf_op jit(solution)/shard_map/jit(cholesky)/cholesky | solution.py:71
  224.5 10.2 %custom-call.32 = f32[1,128,128]{1,2,0:T(8,128)S(1)} custom-call(f32[1,128,128]{2,1,0:T(8,128)S(1)} %get-tuple-element.103), custom_call_target="InvertDiagBlocksLowerTriangular" | custom-call | tf_op jit(solution)/shard_map/jit(cholesky)/cholesky | solution.py:71
  235.4 11.7 %cholesky.236 = f32[128,128]{1,0:T(8,128)S(1)} custom-call(f32[128,128]{1,0:T(8,128)S(1)} %cholesky.272), custom_call_target="Cholesky" | custom-call | tf_op jit(solution)/shard_map/jit(cholesky)/cholesky | solution.py:71
  247.1 9.8 custom-call.33
  257.6 11.9 %cholesky.253 = f32[128,128]{1,0:T(8,128)S(1)} custom-call(f32[128,128]{1,0:T(8,128)S(1)} %convolution_subtract_fusion.6), custom_call_target="Cholesky" | custom-call | tf_op jit(solution)/shard_map/jit(cholesky)/cholesky | solution.py:71
  276.9 10.8 %while.1 = (s32[]{:T(128)}, f32[512,512]{1,0:T(8,128)S(1)}, s32[4,2]{0,1:T(2,128)S(1)}, f32[4,128,128]{2,1,0:T(8,128)}, s32[]{:T(128)}) while((s32[]{:T(128)}, f32[512,512]{1,0:T(8,128)S(1)}, s32[4,2]{0,1:T(2,128)S(1)}, f32[4,128,128]{2,1,0:T(8,128)}, s32[]{:T(128)}) %tuple.103), condition=%wide.while_cond, body=%wide.while_body.sunk | while | flops 2 | bytes 132705 | solution.py:72
  287.7 40.1 %custom-call.34 = f32[4,128,128]{1,2,0:T(8,128)S(1)} custom-call(f32[4,128,128]{2,1,0:T(8,128)} %get-tuple-element.38), custom_call_target="InvertDiagBlocksLowerTriangular" | custom-call | tf_op jit(solution)/shard_map/jit(_solve_triangular)/triangular_solve | solution.py:72
  332.8 59.9 %all-to-all-done = f32[4,3,1536,128]{3,2,1,0:T(8,128)} async-done(((f32[4,3,1536,128]{3,2,1,0:T(8,128)}), f32[4,3,1536,128]{3,2,1,0:T(8,128)}, u32[]{:S(2)}, u32[]{:S(2)}) %all-to-all-start) | async-done | bytes 9437216 | tf_op jit(solution)/shard_map/all_to_all | solution.py:192
  393.4 14.3 %collective-permute-done = f32[4,3,1536,128]{3,2,1,0:T(8,128)} collective-permute-done((f32[4,3,1536,128]{3,2,1,0:T(8,128)}, f32[4,3,1536,128]{3,2,1,0:T(8,128)}, u32[]{:S(2)}, u32[]{:S(2)}) %collective-permute-start) | collective-permute-done | bytes 9437216 | tf_op jit(solution)/shard_map/ppermute | solution.py:194
  407.7 17.7 %gather_fusion.9 = f32[200,128,128]{2,1,0:T(8,128)} fusion(f32[12,12,128,128]{3,2,1,0:T(8,128)} %bitcast.48, s32[200]{0:T(256)S(1)} %reshape.1163), kind=kCustom, calls=%fused_computation.9 | custom fusion | bytes 26216000 | tf_op jit(solution)/shard_map/gather | solution.py:207
  445.8 9.2 constant_dynamic-slice_fusion.3
  456.1 44.7 %collective-permute-done.4 = f32[2,5,4,128,128]{4,3,2,1,0:T(8,128)} collective-permute-done((f32[2,5,4,128,128]{4,3,2,1,0:T(8,128)}, f32[2,5,4,128,128]{4,3,2,1,0:T(8,128)}, u32[]{:S(2)}, u32[]{:S(2)}) %collective-permute-start.4) | collective-permute-done | bytes 2621472 | tf_op jit(solution)/shard_map/ppermute | solution.py:174
  502.3 54.8 %collective-permute-done.5 = f32[2,5,4,128,128]{4,3,2,1,0:T(8,128)} collective-permute-done((f32[2,5,4,128,128]{4,3,2,1,0:T(8,128)}, f32[2,5,4,128,128]{4,3,2,1,0:T(8,128)}, u32[]{:S(2)}, u32[]{:S(2)}) %collective-permute-start.5) | collective-permute-done | bytes 2621472 | tf_op jit(solution)/shard_map/ppermute | solution.py:174
  593.9 33.4 %collective-permute-done.1 = f32[5,10,128,128]{3,2,1,0:T(8,128)} collective-permute-done((f32[5,10,128,128]{3,2,1,0:T(8,128)}, f32[5,10,128,128]{3,2,1,0:T(8,128)}, u32[]{:S(2)}, u32[]{:S(2)}) %collective-permute-start.1) | collective-permute-done | bytes 3276832 | tf_op jit(solution)/shard_map/ppermute | solution.py:223
  627.3 69.3 %collective-permute-done.2 = f32[5,10,128,128]{3,2,1,0:T(8,128)} collective-permute-done((f32[5,10,128,128]{3,2,1,0:T(8,128)}, f32[5,10,128,128]{3,2,1,0:T(8,128)}, u32[]{:S(2)}, u32[]{:S(2)}) %collective-permute-start.2) | collective-permute-done | bytes 3276832 | tf_op jit(solution)/shard_map/ppermute | solution.py:223
  705.7 12.5 %gather_fusion.10 = f32[20,10,128,128]{3,2,1,0:T(8,128)} fusion(f32[20,10,128,128]{3,2,1,0:T(8,128)} %bitcast.304, s32[1024]{0:T(1024)S(1)} %pad_clamp_fusion.3), kind=kCustom, calls=%fused_computation.10 | custom fusion | bytes 26214480 | tf_op jit(solution)/shard_map/gather | solution.py:230
  718.1 17.9 %gather_fusion.13 = f32[200,128,128]{2,1,0:T(8,128)} fusion(f32[12,12,128,128]{3,2,1,0:T(8,128)} %bitcast.102, s32[200]{0:T(256)S(1)} %reshape.1193), kind=kCustom, calls=%fused_computation.13 | custom fusion | bytes 26216000 | tf_op jit(solution)/shard_map/gather | solution.py:207
  743.2 10.4 %fusion.118 = f32[2560,512]{1,0:T(8,128)S(1)} fusion(f32[2560,512]{1,0:T(8,128)} %fusion.3, f32[512,512]{1,0:T(8,128)S(1)} %copy-done.2), kind=kOutput, calls=%fused_computation.380 | convolution fusion | flops 8053063680 | bytes 11534336 | tf_op jit(solution)/shard_map/dot_general | solution.py:79
  764.2 142.8 %all-to-all-done.2 = f32[4,5,10,128,128]{4,3,2,1,0:T(8,128)} async-done(((f32[4,5,10,128,128]{4,3,2,1,0:T(8,128)}), f32[4,5,10,128,128]{4,3,2,1,0:T(8,128)}, u32[]{:S(2)}, u32[]{:S(2)}) %all-to-all-start.2) | async-done | bytes 13107232 | tf_op jit(solution)/shard_map/all_to_all | solution.py:228
  907.0 12.6 %gather_fusion.14 = f32[20,10,128,128]{3,2,1,0:T(8,128)} fusion(f32[20,10,128,128]{3,2,1,0:T(8,128)} %bitcast.106, s32[1024]{0:T(1024)S(1)} %pad_clamp_fusion), kind=kCustom, calls=%fused_computation.14 | custom fusion | bytes 26214480 | tf_op jit(solution)/shard_map/gather | solution.py:230
  919.6 9.3 add_bitcast_fusion
  928.9 14.2 %copy.40 = f32[20,128,10,128]{3,2,1,0:T(8,128)} copy(f32[20,128,10,128]{3,1,2,0:T(8,128)S(1)} %add_bitcast_fusion) | data formatting | bytes 26214400 | tf_op jit(solution)/shard_map/reshape | solution.py:244
  947.8 35.2 %fusion.1 = f32[2560,1280]{1,0:T(8,128)} fusion(f32[2560,512]{1,0:T(8,128)} %pad_maximum_fusion.2, f32[1280,512]{1,0:T(8,128)} %all-reduce.5.cloned.1.call-done, f32[320,8,10,128]{3,2,1,0:T(8,128)} %bitcast.311, f32[2560,512]{1,0:T(8,128)} %param.9, f32[1280]{0:T(1024)S(1)} %copy-done.8, s32[1280]{0:T(1024)S(1)} %iota_add_fusion.1, ...), kind=kOutput, calls=%fused_computation.21 | convolution fusion | flops 20162150400 | bytes 39348480 | tf_op jit(solution)/shard_map/dot_general | solution.py:261
  (240 shorter events, 167.1 us)
Async XLA Ops:
  6.5 68.7 %all-gather.6.cloned.1.call-start = ((), (), s32[]{:S(2)}) async-start(), calls=%async_computation.4 | async-start | bytes 2162688 | tf_op jit(solution)/shard_map/all_gather | solution.py:93
  8.0 126.9 %all-gather.8.cloned.1.call-start = ((), (), s32[]{:S(2)}) async-start(), calls=%async_computation.5 | async-start | bytes 7077888 | tf_op jit(solution)/shard_map/all_gather | solution.py:145
  10.2 9.7 copy-start.6
  10.2 9.7 copy-start.5
  20.3 13.1 %copy-start.9 = (s32[48]{0:T(128)}, s32[48]{0:T(128)S(1)}, u32[]{:S(2)}) copy-start(s32[48]{0:T(128)S(1)} %get-tuple-element.50) | copy-start | bytes 580
  23.9 11.3 %copy-start.7 = (f32[1280]{0:T(1024)S(1)}, f32[1280]{0:T(1024)}, u32[]{:S(2)}) copy-start(f32[1280]{0:T(1024)} %param.8) | copy-start | bytes 15364
  180.5 8.7 copy-start.1
  180.5 212.2 %all-to-all-start = ((f32[4,3,1536,128]{3,2,1,0:T(8,128)}), f32[4,3,1536,128]{3,2,1,0:T(8,128)}, u32[]{:S(2)}, u32[]{:S(2)}) async-start(f32[4,3,1536,128]{3,2,1,0:T(8,128)} %get-tuple-element.82), calls=%async_computation | async-start | bytes 18874368 | tf_op jit(solution)/shard_map/all_to_all | solution.py:192
  190.4 138.6 %copy-start.4 = (f32[512,512]{1,0:T(8,128)S(1)}, f32[512,512]{1,0:T(8,128)}, u32[]{:S(2)}) copy-start(f32[512,512]{1,0:T(8,128)} %fusion.14) | copy-start | bytes 3145732
  274.9 117.7 %copy-start.13 = (pred[20]{0:T(512)(128)(4,1)S(1)}, pred[20]{0:T(512)(128)(4,1)}, u32[]{:S(2)}) copy-start(pred[20]{0:T(512)(128)(4,1)} %get-tuple-element.45) | copy-start | bytes 64
  275.0 117.7 %copy-start.14 = (s32[20]{0:T(128)S(1)}, s32[20]{0:T(128)}, u32[]{:S(2)}) copy-start(s32[20]{0:T(128)} %get-tuple-element.41) | copy-start | bytes 244
  275.0 117.8 %copy-start.11 = (pred[20]{0:T(512)(128)(4,1)S(1)}, pred[20]{0:T(512)(128)(4,1)}, u32[]{:S(2)}) copy-start(pred[20]{0:T(512)(128)(4,1)} %get-tuple-element.43) | copy-start | bytes 64
  275.0 117.8 %copy-start.12 = (s32[20]{0:T(128)S(1)}, s32[20]{0:T(128)}, u32[]{:S(2)}) copy-start(s32[20]{0:T(128)} %get-tuple-element.39) | copy-start | bytes 244
  392.7 15.0 %collective-permute-start = (f32[4,3,1536,128]{3,2,1,0:T(8,128)}, f32[4,3,1536,128]{3,2,1,0:T(8,128)}, u32[]{:S(2)}, u32[]{:S(2)}) collective-permute-start(f32[4,3,1536,128]{3,2,1,0:T(8,128)} %all-to-all-done), channel_id=1, source_target_pairs={{0,16},{16,0},{1,17},{17,1},{2,18},{18,2},{3,19},{19,3},{4,20},{20... | collective-permute-start | bytes 28311560 | tf_op jit(solution)/shard_map/ppermute | solution.py:194
  425.4 292.7 %all-to-all-start.1 = ((f32[4,3,1536,128]{3,2,1,0:T(8,128)}), f32[4,3,1536,128]{3,2,1,0:T(8,128)}, u32[]{:S(2)}, u32[]{:S(2)}) async-start(f32[4,3,1536,128]{3,2,1,0:T(8,128)} %get-tuple-element.24), calls=%async_computation.1 | async-start | bytes 18874368 | tf_op jit(solution)/shard_map/all_to_all | solution.py:237
  431.4 13.7 %copy-start.10 = (s32[48]{0:T(128)S(1)}, s32[48]{0:T(128)}, u32[]{:S(2)}) copy-start(s32[48]{0:T(128)} %copy-done.9) | copy-start | bytes 580
  439.9 61.0 %collective-permute-start.4 = (f32[2,5,4,128,128]{4,3,2,1,0:T(8,128)}, f32[2,5,4,128,128]{4,3,2,1,0:T(8,128)}, u32[]{:S(2)}, u32[]{:S(2)}) collective-permute-start(f32[2,5,4,128,128]{4,3,2,1,0:T(8,128)} %get-tuple-element.92), channel_id=1, source_target_pairs={{0,4},{4,8},{8,12},{12,0},{1,5},{5,9},{9,13},{13,1},{2,6},{6,10},{... | collective-permute-start | bytes 7864328 | tf_op jit(solution)/shard_map/ppermute | solution.py:174
  441.6 115.5 %collective-permute-start.5 = (f32[2,5,4,128,128]{4,3,2,1,0:T(8,128)}, f32[2,5,4,128,128]{4,3,2,1,0:T(8,128)}, u32[]{:S(2)}, u32[]{:S(2)}) collective-permute-start(f32[2,5,4,128,128]{4,3,2,1,0:T(8,128)} %get-tuple-element.91), channel_id=1, source_target_pairs={{0,8},{4,12},{8,0},{12,4},{1,9},{5,13},{9,1},{13,5},{2,10},{6,14},... | collective-permute-start | bytes 7864328 | tf_op jit(solution)/shard_map/ppermute | solution.py:174
  443.2 113.9 %collective-permute-start.6 = (f32[2,5,4,128,128]{4,3,2,1,0:T(8,128)}, f32[2,5,4,128,128]{4,3,2,1,0:T(8,128)}, u32[]{:S(2)}, u32[]{:S(2)}) collective-permute-start(f32[2,5,4,128,128]{4,3,2,1,0:T(8,128)} %get-tuple-element.90), channel_id=1, source_target_pairs={{0,12},{4,0},{8,4},{12,8},{1,13},{5,1},{9,5},{13,9},{2,14},{6,2},{... | collective-permute-start | bytes 7864328 | tf_op jit(solution)/shard_map/ppermute | solution.py:174
  455.0 172.3 %collective-permute-start.1 = (f32[5,10,128,128]{3,2,1,0:T(8,128)}, f32[5,10,128,128]{3,2,1,0:T(8,128)}, u32[]{:S(2)}, u32[]{:S(2)}) collective-permute-start(f32[5,10,128,128]{3,2,1,0:T(8,128)} %get-tuple-element.86), channel_id=1, source_target_pairs={{0,4},{4,8},{8,12},{12,0},{1,5},{5,9},{9,13},{13,1},{2,6},{6,10},{... | collective-permute-start | bytes 9830408 | tf_op jit(solution)/shard_map/ppermute | solution.py:223
  455.6 241.0 %collective-permute-start.2 = (f32[5,10,128,128]{3,2,1,0:T(8,128)}, f32[5,10,128,128]{3,2,1,0:T(8,128)}, u32[]{:S(2)}, u32[]{:S(2)}) collective-permute-start(f32[5,10,128,128]{3,2,1,0:T(8,128)} %get-tuple-element.85), channel_id=1, source_target_pairs={{0,8},{4,12},{8,0},{12,4},{1,9},{5,13},{9,1},{13,5},{2,10},{6,14},... | collective-permute-start | bytes 9830408 | tf_op jit(solution)/shard_map/ppermute | solution.py:223
  500.9 195.9 %collective-permute-start.3 = (f32[5,10,128,128]{3,2,1,0:T(8,128)}, f32[5,10,128,128]{3,2,1,0:T(8,128)}, u32[]{:S(2)}, u32[]{:S(2)}) collective-permute-start(f32[5,10,128,128]{3,2,1,0:T(8,128)} %get-tuple-element.84), channel_id=1, source_target_pairs={{0,12},{4,0},{8,4},{12,8},{1,13},{5,1},{9,5},{13,9},{2,14},{6,2},{... | collective-permute-start | bytes 9830408 | tf_op jit(solution)/shard_map/ppermute | solution.py:223
  736.0 7.1 copy-start.2
  736.0 170.9 %all-to-all-start.2 = ((f32[4,5,10,128,128]{4,3,2,1,0:T(8,128)}), f32[4,5,10,128,128]{4,3,2,1,0:T(8,128)}, u32[]{:S(2)}, u32[]{:S(2)}) async-start(f32[4,5,10,128,128]{4,3,2,1,0:T(8,128)} %bitcast.302), calls=%async_computation.2 | async-start | bytes 26214400 | tf_op jit(solution)/shard_map/all_to_all | solution.py:228
  742.7 205.1 %all-reduce.5.cloned.1.call-start = ((), (), s32[]{:S(2)}) async-start(), calls=%async_computation.3 | async-start | bytes 5242880 | tf_op jit(solution)/shard_map/psum | solution.py:13
  753.6 1.2 copy-start.3
  754.8 2.0 copy-start
  928.8 19.0 %copy-start.8 = (f32[1280]{0:T(1024)S(1)}, f32[1280]{0:T(1024)}, u32[]{:S(2)}) copy-start(f32[1280]{0:T(1024)} %param.8) | copy-start | bytes 15364
Sparse Core Ops, SparseCore 0:
  10.3 59.2 all-gather.5
  71.3 63.6 all-gather.7
  759.2 188.5 all-reduce.4

commit v7 on v6

--- a/solution.py
+++ b/solution.py
@@ -166,8 +166,12 @@
     chosen = jnp.stack([chosen[1 - my_sub], chosen[my_sub]]).reshape(-1)
     outgoing = by_col.at[:, chosen].get(mode="promise_in_bounds")
     outgoing = outgoing.transpose(1, 0, 2).reshape(2, n_col, col_cap, rows_here, BLOCK)
-    outgoing, corner, panel_send = lax.optimization_barrier((outgoing, corner, panel_send))
+    outgoing, corner = lax.optimization_barrier((outgoing, corner))
     lower, inverse = factor_corner(corner)
+    other_half = lax.all_to_all(outgoing[0], "col", split_axis=0, concat_axis=0, tiled=True)
+    other_half, lower, inverse, panel_send = lax.optimization_barrier(
+        (other_half, lower, inverse, panel_send)
+    )
     pieces = [lax.dynamic_index_in_dim(panel_send, my_row, 0, keepdims=False)]
     for shift in range(1, n_row):
         piece = lax.dynamic_index_in_dim(panel_send, (my_row + shift) % n_row, 0, keepdims=False)
@@ -189,8 +193,6 @@
     panel_rows = panel_rows + jnp.where(
         global_row[:, None] == jnp.arange(PANEL, dtype=jnp.int32)[None, :], full_diagonal[None, :PANEL], 0.0
     )
-    other_half = lax.all_to_all(outgoing[0], "col", split_axis=0, concat_axis=0, tiled=True)
-    other_half, lower, inverse = lax.optimization_barrier((other_half, lower, inverse))
     other_half = lax.ppermute(other_half, "sub", [(0, 1), (1, 0)])
 
     def row_sending(half, which):

time: 1000 us -> 964 us (0.964)
  waiting for transfers between devices: 474 us -> 434 us
    all_gather x1, waiting for transfers between devices: 50.1 us -> 0.01 us  [shards(): cands = lax.all_gather(child_piece[:, :first_cols * BLOCK], ('sub', 'col'))]
    all_to_all x1, waiting for transfers between devices: 59.9 us -> 70.1 us  [shards(): lax.all_to_all(outgoing[0], 'col', split_axis=0, concat_axis=0, tiled=True)]
  transfers between devices with their start and end apart: 13 -> 13, of which waited for: 10 -> 9; matrix products, arithmetic and copies ran while one was open for 33% -> 37% of each run, Pallas kernels for 0% -> 0%
where the time goes in v7:
time: 964 us; the launch traced here: 956 us
  waiting for transfers between devices  434 us (45%)
  local copies, waits for them, and re-layouts  202 us (21%)
  other arithmetic  198 us (21%)
  matrix products  51.5 us (5%)
  starting transfers between devices  25.4 us (3%)
  blocking collectives  25.3 us (3%)
  between operations  18.7 us (2%)
    all_to_all x1, waiting for transfers between devices, row_receiving(): lax.all_to_all(sending, 'row', split_axis=0, concat_axis=0, tiled=True)  143 us
    ppermute x3, waiting for transfers between devices, row_receiving(): pieces.append(lax.ppermute(piece, 'row', pairs))  103 us
    ppermute x3, waiting for transfers between devices, shards(): lax.ppermute(piece, 'row', [(i, (i + shift) % n_row) for i in range(n_row)])  99.8 us
    another operation x15, other arithmetic, factor_corner(): lower = jnp.linalg.cholesky(symmetric_of(corner))  82 us
    all_to_all x1, waiting for transfers between devices, shards(): lax.all_to_all(outgoing[0], 'col', split_axis=0, concat_axis=0, tiled=True)  70.1 us
    another operation x4, other arithmetic, factor_corner(): jax.scipy.linalg.solve_triangular(lower, jnp.eye(PANEL, dtype=jnp.float32...  42.9 us
    gather x2, local copies, waits for them, and re-layouts, row_sending(): half.at[col_index[None, None, :], row_index[:, :, None]]  35.8 us
    dot_general x1, matrix products, shards(): lax.dot_general(own_rows, theirs, (((1,), (1,)), ((), ())), precision=lax...  35.3 us
  transfers between devices with their start and end apart: 13, of which 9 were waited for; matrix products, arithmetic and copies ran while one was open for 37% of the time, Pallas kernels for 0%

profile of v7, /device:TPU:0, one launch (start us, length us, event | category | flops | bytes accessed | tf_op | source)
XLA Modules:
  0.0 956.0 jit_solution(12466643847533996789)
XLA Ops:
  10.6 9.6 %copy.32 = f32[1,1536,1536]{1,2,0:T(8,128)} copy(f32[1,1536,1536]{2,1,0:T(8,128)} %param.5) | data formatting | bytes 18874368 | tf_op args[0]
  21.6 9.7 %copy.33 = f32[1536,12,128]{2,0,1:T(8,128)} copy(f32[1536,12,128]{0,2,1:T(8,128)} %bitcast.305) | data formatting | bytes 18874368 | tf_op jit(solution)/shard_map/reshape;squeeze | solution.py:163
  34.3 25.3 %all-gather.2 = f32[8,1,1280]{2,1,0:T(1,128)S(1)} all-gather(f32[1,1,1280]{2,1,0:T(1,128)S(1)} %reshape.1233), channel_id=1, replica_groups=mesh['sub'=2,'row'=4,'col'=4] {'sub','col'}, dimensions={0}, use_global_device_ids=true | all-gather | bytes 46080 | tf_op jit(solution)/shard_map/all_gather | solution.py:139
  59.6 13.3 %gather_fusion = f32[24,1536,128]{2,1,0:T(8,128)} fusion(f32[1536,12,128]{2,0,1:T(8,128)} %copy.33, s32[1024]{0:T(1024)S(1)} %pad_clamp_fusion.9), kind=kCustom, calls=%fused_computation | custom fusion | bytes 37748832 | tf_op jit(solution)/shard_map/gather | solution.py:167
  81.3 13.4 %slice_bitcast_fusion = (f32[4,3,1536,128]{3,2,1,0:T(8,128)}, f32[4,3,1536,128]{3,2,1,0:T(8,128)}) fusion(f32[2,4,3,1536,128]{4,3,2,1,0:T(8,128)} %bitcast.301), kind=kLoop, calls=%fused_computation.28 | loop fusion | bytes 37748736 | tf_op jit(solution)/shard_map/squeeze | solution.py:237
  111.3 11.7 %cholesky.103 = f32[128,128]{1,0:T(8,128)S(1)} custom-call(f32[128,128]{1,0:T(8,128)S(1)} %cholesky.263), custom_call_target="Cholesky" | custom-call | tf_op jit(solution)/shard_map/jit(cholesky)/cholesky | solution.py:71
  123.8 9.8 %custom-call.31 = f32[1,128,128]{1,2,0:T(8,128)S(1)} custom-call(f32[1,128,128]{2,1,0:T(8,128)S(1)} %get-tuple-element.106), custom_call_target="InvertDiagBlocksLowerTriangular" | custom-call | tf_op jit(solution)/shard_map/jit(cholesky)/cholesky | solution.py:71
  134.3 11.7 %cholesky.215 = f32[128,128]{1,0:T(8,128)S(1)} custom-call(f32[128,128]{1,0:T(8,128)S(1)} %cholesky.267), custom_call_target="Cholesky" | custom-call | tf_op jit(solution)/shard_map/jit(cholesky)/cholesky | solution.py:71
  146.6 9.9 %custom-call.32 = f32[1,128,128]{1,2,0:T(8,128)S(1)} custom-call(f32[1,128,128]{2,1,0:T(8,128)S(1)} %get-tuple-element.103), custom_call_target="InvertDiagBlocksLowerTriangular" | custom-call | tf_op jit(solution)/shard_map/jit(cholesky)/cholesky | solution.py:71
  157.2 11.7 %cholesky.236 = f32[128,128]{1,0:T(8,128)S(1)} custom-call(f32[128,128]{1,0:T(8,128)S(1)} %cholesky.272), custom_call_target="Cholesky" | custom-call | tf_op jit(solution)/shard_map/jit(cholesky)/cholesky | solution.py:71
  169.0 9.8 %custom-call.33 = f32[1,128,128]{1,2,0:T(8,128)S(1)} custom-call(f32[1,128,128]{2,1,0:T(8,128)S(1)} %get-tuple-element.100), custom_call_target="InvertDiagBlocksLowerTriangular" | custom-call | tf_op jit(solution)/shard_map/jit(cholesky)/cholesky | solution.py:71
  179.4 11.9 %cholesky.253 = f32[128,128]{1,0:T(8,128)S(1)} custom-call(f32[128,128]{1,0:T(8,128)S(1)} %convolution_subtract_fusion.6), custom_call_target="Cholesky" | custom-call | tf_op jit(solution)/shard_map/jit(cholesky)/cholesky | solution.py:71
  199.8 10.4 %while.1 = (s32[]{:T(128)}, f32[512,512]{1,0:T(8,128)S(1)}, s32[4,2]{0,1:T(2,128)S(1)}, f32[4,128,128]{2,1,0:T(8,128)}, s32[]{:T(128)}) while((s32[]{:T(128)}, f32[512,512]{1,0:T(8,128)S(1)}, s32[4,2]{0,1:T(2,128)S(1)}, f32[4,128,128]{2,1,0:T(8,128)}, s32[]{:T(128)}) %tuple.103), condition=%wide.while_cond, body=%wide.while_body.sunk | while | flops 2 | bytes 132705 | solution.py:72
  210.2 40.1 %custom-call.34 = f32[4,128,128]{1,2,0:T(8,128)S(1)} custom-call(f32[4,128,128]{2,1,0:T(8,128)} %get-tuple-element.38), custom_call_target="InvertDiagBlocksLowerTriangular" | custom-call | tf_op jit(solution)/shard_map/jit(_solve_triangular)/triangular_solve | solution.py:72
  277.9 9.7 %maximum_bitcast_fusion = f32[4,2,5,4,128,128]{5,4,3,2,0,1:T(8,128)} fusion(f32[1,4,4,5,128,128]{5,4,1,3,2,0:T(8,128)} %bitcast.310, f32[1,4,4,5,128,128]{5,4,1,3,2,0:T(8,128)} %bitcast.307), kind=kLoop, calls=%fused_computation.26 | loop fusion | flops 2621440 | bytes 20971520 | tf_op jit(solution)/shard_map/transpose | solution.py:161
  287.6 70.1 %all-to-all-done = f32[4,3,1536,128]{3,2,1,0:T(8,128)} async-done(((f32[4,3,1536,128]{3,2,1,0:T(8,128)}), f32[4,3,1536,128]{3,2,1,0:T(8,128)}, u32[]{:S(2)}, u32[]{:S(2)}) %all-to-all-start) | async-done | bytes 9437216 | tf_op jit(solution)/shard_map/all_to_all | solution.py:171
  358.3 14.3 %collective-permute-done = f32[4,3,1536,128]{3,2,1,0:T(8,128)} collective-permute-done((f32[4,3,1536,128]{3,2,1,0:T(8,128)}, f32[4,3,1536,128]{3,2,1,0:T(8,128)}, u32[]{:S(2)}, u32[]{:S(2)}) %collective-permute-start) | collective-permute-done | bytes 9437216 | tf_op jit(solution)/shard_map/ppermute | solution.py:196
  372.6 18.1 %gather_fusion.9 = f32[200,128,128]{2,1,0:T(8,128)} fusion(f32[12,12,128,128]{3,2,1,0:T(8,128)} %bitcast.48, s32[200]{0:T(256)S(1)} %reshape.1163), kind=kCustom, calls=%fused_computation.9 | custom fusion | bytes 26216000 | tf_op jit(solution)/shard_map/gather | solution.py:209
  410.8 9.2 constant_dynamic-slice_fusion.3
  421.1 45.1 %collective-permute-done.4 = f32[2,5,4,128,128]{4,3,2,1,0:T(8,128)} collective-permute-done((f32[2,5,4,128,128]{4,3,2,1,0:T(8,128)}, f32[2,5,4,128,128]{4,3,2,1,0:T(8,128)}, u32[]{:S(2)}, u32[]{:S(2)}) %collective-permute-start.4) | collective-permute-done | bytes 2621472 | tf_op jit(solution)/shard_map/ppermute | solution.py:178
  467.7 54.7 %collective-permute-done.5 = f32[2,5,4,128,128]{4,3,2,1,0:T(8,128)} collective-permute-done((f32[2,5,4,128,128]{4,3,2,1,0:T(8,128)}, f32[2,5,4,128,128]{4,3,2,1,0:T(8,128)}, u32[]{:S(2)}, u32[]{:S(2)}) %collective-permute-start.5) | collective-permute-done | bytes 2621472 | tf_op jit(solution)/shard_map/ppermute | solution.py:178
  559.5 33.2 %collective-permute-done.1 = f32[5,10,128,128]{3,2,1,0:T(8,128)} collective-permute-done((f32[5,10,128,128]{3,2,1,0:T(8,128)}, f32[5,10,128,128]{3,2,1,0:T(8,128)}, u32[]{:S(2)}, u32[]{:S(2)}) %collective-permute-start.1) | collective-permute-done | bytes 3276832 | tf_op jit(solution)/shard_map/ppermute | solution.py:225
  592.6 69.3 %collective-permute-done.2 = f32[5,10,128,128]{3,2,1,0:T(8,128)} collective-permute-done((f32[5,10,128,128]{3,2,1,0:T(8,128)}, f32[5,10,128,128]{3,2,1,0:T(8,128)}, u32[]{:S(2)}, u32[]{:S(2)}) %collective-permute-start.2) | collective-permute-done | bytes 3276832 | tf_op jit(solution)/shard_map/ppermute | solution.py:225
  662.0 9.0 pad_maximum_fusion
  671.0 12.4 %gather_fusion.10 = f32[20,10,128,128]{3,2,1,0:T(8,128)} fusion(f32[20,10,128,128]{3,2,1,0:T(8,128)} %bitcast.304, s32[1024]{0:T(1024)S(1)} %pad_clamp_fusion.3), kind=kCustom, calls=%fused_computation.10 | custom fusion | bytes 26214480 | tf_op jit(solution)/shard_map/gather | solution.py:232
  683.4 17.7 %gather_fusion.13 = f32[200,128,128]{2,1,0:T(8,128)} fusion(f32[12,12,128,128]{3,2,1,0:T(8,128)} %bitcast.102, s32[200]{0:T(256)S(1)} %reshape.1193), kind=kCustom, calls=%fused_computation.13 | custom fusion | bytes 26216000 | tf_op jit(solution)/shard_map/gather | solution.py:209
  708.1 10.6 %fusion.118 = f32[2560,512]{1,0:T(8,128)S(1)} fusion(f32[2560,512]{1,0:T(8,128)} %fusion.3, f32[512,512]{1,0:T(8,128)S(1)} %copy-done.1), kind=kOutput, calls=%fused_computation.380 | convolution fusion | flops 8053063680 | bytes 11534336 | tf_op jit(solution)/shard_map/dot_general | solution.py:79
  729.3 142.7 %all-to-all-done.2 = f32[4,5,10,128,128]{4,3,2,1,0:T(8,128)} async-done(((f32[4,5,10,128,128]{4,3,2,1,0:T(8,128)}), f32[4,5,10,128,128]{4,3,2,1,0:T(8,128)}, u32[]{:S(2)}, u32[]{:S(2)}) %all-to-all-start.2) | async-done | bytes 13107232 | tf_op jit(solution)/shard_map/all_to_all | solution.py:230
  872.0 12.5 %gather_fusion.14 = f32[20,10,128,128]{3,2,1,0:T(8,128)} fusion(f32[20,10,128,128]{3,2,1,0:T(8,128)} %bitcast.106, s32[1024]{0:T(1024)S(1)} %pad_clamp_fusion), kind=kCustom, calls=%fused_computation.14 | custom fusion | bytes 26214480 | tf_op jit(solution)/shard_map/gather | solution.py:232
  884.4 9.3 add_bitcast_fusion
  893.7 14.1 %copy.40 = f32[20,128,10,128]{3,2,1,0:T(8,128)} copy(f32[20,128,10,128]{3,1,2,0:T(8,128)S(1)} %add_bitcast_fusion) | data formatting | bytes 26214400 | tf_op jit(solution)/shard_map/reshape | solution.py:246
  912.8 35.3 %fusion.1 = f32[2560,1280]{1,0:T(8,128)} fusion(f32[2560,512]{1,0:T(8,128)} %pad_maximum_fusion.2, f32[1280,512]{1,0:T(8,128)} %all-reduce.5.cloned.1.call-done, f32[320,8,10,128]{3,2,1,0:T(8,128)} %bitcast.311, f32[2560,512]{1,0:T(8,128)} %param.9, f32[1280]{0:T(1024)S(1)} %copy-done.7, s32[1280]{0:T(1024)S(1)} %iota_add_fusion.1, ...), kind=kOutput, calls=%fused_computation.21 | convolution fusion | flops 20162150400 | bytes 39348480 | tf_op jit(solution)/shard_map/dot_general | solution.py:263
  (248 shorter events, 162.2 us)
Async XLA Ops:
  7.4 65.6 %all-gather.6.cloned.1.call-start = ((), (), s32[]{:S(2)}) async-start(), calls=%async_computation.4 | async-start | bytes 2162688 | tf_op jit(solution)/shard_map/all_gather | solution.py:93
  10.6 9.6 %copy-start.4 = (s32[2,48]{1,0:T(2,128)S(1)}, s32[2,48]{1,0:T(2,128)}, u32[]{:S(2)}) copy-start(s32[2,48]{1,0:T(2,128)} %param.6) | copy-start | bytes 1156
  21.1 81.6 %copy-start.13 = (s32[48]{0:T(128)}, s32[48]{0:T(128)S(1)}, u32[]{:S(2)}) copy-start(s32[48]{0:T(128)S(1)} %get-tuple-element.50) | copy-start | bytes 580
  21.1 81.6 %copy-start.11 = (s32[48]{0:T(128)}, s32[48]{0:T(128)S(1)}, u32[]{:S(2)}) copy-start(s32[48]{0:T(128)S(1)} %get-tuple-element.52) | copy-start | bytes 580
  21.6 10.4 %copy-start.5 = (s32[2,48]{1,0:T(2,128)S(1)}, s32[2,48]{1,0:T(2,128)}, u32[]{:S(2)}) copy-start(s32[2,48]{1,0:T(2,128)} %param.7) | copy-start | bytes 1156
  21.6 12.7 %copy-start.6 = (f32[1280]{0:T(1024)S(1)}, f32[1280]{0:T(1024)}, u32[]{:S(2)}) copy-start(f32[1280]{0:T(1024)} %param.8) | copy-start | bytes 15364
  94.7 262.9 %all-to-all-start = ((f32[4,3,1536,128]{3,2,1,0:T(8,128)}), f32[4,3,1536,128]{3,2,1,0:T(8,128)}, u32[]{:S(2)}, u32[]{:S(2)}) async-start(f32[4,3,1536,128]{3,2,1,0:T(8,128)} %get-tuple-element.82), calls=%async_computation | async-start | bytes 18874368 | tf_op jit(solution)/shard_map/all_to_all | solution.py:171
  100.5 154.7 %all-gather.8.cloned.1.call-start = ((), (), s32[]{:S(2)}) async-start(), calls=%async_computation.5 | async-start | bytes 7077888 | tf_op jit(solution)/shard_map/all_gather | solution.py:145
  111.3 140.1 %copy-start.3 = (f32[512,512]{1,0:T(8,128)S(1)}, f32[512,512]{1,0:T(8,128)}, u32[]{:S(2)}) copy-start(f32[512,512]{1,0:T(8,128)} %fusion.14) | copy-start | bytes 3145732
  260.2 2.4 copy-start.10
  268.1 4.3 copy-start.9
  277.9 79.8 %copy-start.17 = (pred[20]{0:T(512)(128)(4,1)S(1)}, pred[20]{0:T(512)(128)(4,1)}, u32[]{:S(2)}) copy-start(pred[20]{0:T(512)(128)(4,1)} %get-tuple-element.45) | copy-start | bytes 64
  277.9 79.8 %copy-start.18 = (s32[20]{0:T(128)S(1)}, s32[20]{0:T(128)}, u32[]{:S(2)}) copy-start(s32[20]{0:T(128)} %get-tuple-element.41) | copy-start | bytes 244
  277.9 79.9 %copy-start.15 = (pred[20]{0:T(512)(128)(4,1)S(1)}, pred[20]{0:T(512)(128)(4,1)}, u32[]{:S(2)}) copy-start(pred[20]{0:T(512)(128)(4,1)} %get-tuple-element.43) | copy-start | bytes 64
  277.9 79.9 %copy-start.16 = (s32[20]{0:T(128)S(1)}, s32[20]{0:T(128)}, u32[]{:S(2)}) copy-start(s32[20]{0:T(128)} %get-tuple-element.39) | copy-start | bytes 244
  277.9 79.9 %copy-start.8 = (s32[48]{0:T(128)S(1)}, s32[48]{0:T(128)}, u32[]{:S(2)}) copy-start(s32[48]{0:T(128)} %get-tuple-element.49) | copy-start | bytes 580
  357.6 15.0 %collective-permute-start = (f32[4,3,1536,128]{3,2,1,0:T(8,128)}, f32[4,3,1536,128]{3,2,1,0:T(8,128)}, u32[]{:S(2)}, u32[]{:S(2)}) collective-permute-start(f32[4,3,1536,128]{3,2,1,0:T(8,128)} %all-to-all-done), channel_id=1, source_target_pairs={{0,16},{16,0},{1,17},{17,1},{2,18},{18,2},{3,19},{19,3},{4,20},{20... | collective-permute-start | bytes 28311560 | tf_op jit(solution)/shard_map/ppermute | solution.py:196
  390.8 292.6 %all-to-all-start.1 = ((f32[4,3,1536,128]{3,2,1,0:T(8,128)}), f32[4,3,1536,128]{3,2,1,0:T(8,128)}, u32[]{:S(2)}, u32[]{:S(2)}) async-start(f32[4,3,1536,128]{3,2,1,0:T(8,128)} %get-tuple-element.24), calls=%async_computation.1 | async-start | bytes 18874368 | tf_op jit(solution)/shard_map/all_to_all | solution.py:239
  396.7 13.4 %copy-start.14 = (s32[48]{0:T(128)S(1)}, s32[48]{0:T(128)}, u32[]{:S(2)}) copy-start(s32[48]{0:T(128)} %copy-done.13) | copy-start | bytes 580
  396.7 13.5 %copy-start.12 = (s32[48]{0:T(128)S(1)}, s32[48]{0:T(128)}, u32[]{:S(2)}) copy-start(s32[48]{0:T(128)} %copy-done.11) | copy-start | bytes 580
  405.2 61.0 %collective-permute-start.4 = (f32[2,5,4,128,128]{4,3,2,1,0:T(8,128)}, f32[2,5,4,128,128]{4,3,2,1,0:T(8,128)}, u32[]{:S(2)}, u32[]{:S(2)}) collective-permute-start(f32[2,5,4,128,128]{4,3,2,1,0:T(8,128)} %get-tuple-element.92), channel_id=1, source_target_pairs={{0,4},{4,8},{8,12},{12,0},{1,5},{5,9},{9,13},{13,1},{2,6},{6,10},{... | collective-permute-start | bytes 7864328 | tf_op jit(solution)/shard_map/ppermute | solution.py:178
  407.0 115.4 %collective-permute-start.5 = (f32[2,5,4,128,128]{4,3,2,1,0:T(8,128)}, f32[2,5,4,128,128]{4,3,2,1,0:T(8,128)}, u32[]{:S(2)}, u32[]{:S(2)}) collective-permute-start(f32[2,5,4,128,128]{4,3,2,1,0:T(8,128)} %get-tuple-element.91), channel_id=1, source_target_pairs={{0,8},{4,12},{8,0},{12,4},{1,9},{5,13},{9,1},{13,5},{2,10},{6,14},... | collective-permute-start | bytes 7864328 | tf_op jit(solution)/shard_map/ppermute | solution.py:178
  408.6 113.8 %collective-permute-start.6 = (f32[2,5,4,128,128]{4,3,2,1,0:T(8,128)}, f32[2,5,4,128,128]{4,3,2,1,0:T(8,128)}, u32[]{:S(2)}, u32[]{:S(2)}) collective-permute-start(f32[2,5,4,128,128]{4,3,2,1,0:T(8,128)} %get-tuple-element.90), channel_id=1, source_target_pairs={{0,12},{4,0},{8,4},{12,8},{1,13},{5,1},{9,5},{13,9},{2,14},{6,2},{... | collective-permute-start | bytes 7864328 | tf_op jit(solution)/shard_map/ppermute | solution.py:178
  420.0 172.6 %collective-permute-start.1 = (f32[5,10,128,128]{3,2,1,0:T(8,128)}, f32[5,10,128,128]{3,2,1,0:T(8,128)}, u32[]{:S(2)}, u32[]{:S(2)}) collective-permute-start(f32[5,10,128,128]{3,2,1,0:T(8,128)} %get-tuple-element.86), channel_id=1, source_target_pairs={{0,4},{4,8},{8,12},{12,0},{1,5},{5,9},{9,13},{13,1},{2,6},{6,10},{... | collective-permute-start | bytes 9830408 | tf_op jit(solution)/shard_map/ppermute | solution.py:225
  420.6 241.3 %collective-permute-start.2 = (f32[5,10,128,128]{3,2,1,0:T(8,128)}, f32[5,10,128,128]{3,2,1,0:T(8,128)}, u32[]{:S(2)}, u32[]{:S(2)}) collective-permute-start(f32[5,10,128,128]{3,2,1,0:T(8,128)} %get-tuple-element.85), channel_id=1, source_target_pairs={{0,8},{4,12},{8,0},{12,4},{1,9},{5,13},{9,1},{13,5},{2,10},{6,14},... | collective-permute-start | bytes 9830408 | tf_op jit(solution)/shard_map/ppermute | solution.py:225
  466.2 195.9 %collective-permute-start.3 = (f32[5,10,128,128]{3,2,1,0:T(8,128)}, f32[5,10,128,128]{3,2,1,0:T(8,128)}, u32[]{:S(2)}, u32[]{:S(2)}) collective-permute-start(f32[5,10,128,128]{3,2,1,0:T(8,128)} %get-tuple-element.84), channel_id=1, source_target_pairs={{0,12},{4,0},{8,4},{12,8},{1,13},{5,1},{9,5},{13,9},{2,14},{6,2},{... | collective-permute-start | bytes 9830408 | tf_op jit(solution)/shard_map/ppermute | solution.py:225
  701.1 7.1 copy-start.1
  701.1 170.9 %all-to-all-start.2 = ((f32[4,5,10,128,128]{4,3,2,1,0:T(8,128)}), f32[4,5,10,128,128]{4,3,2,1,0:T(8,128)}, u32[]{:S(2)}, u32[]{:S(2)}) async-start(f32[4,5,10,128,128]{4,3,2,1,0:T(8,128)} %bitcast.302), calls=%async_computation.2 | async-start | bytes 26214400 | tf_op jit(solution)/shard_map/all_to_all | solution.py:230
  707.7 205.2 %all-reduce.5.cloned.1.call-start = ((), (), s32[]{:S(2)}) async-start(), calls=%async_computation.3 | async-start | bytes 5242880 | tf_op jit(solution)/shard_map/psum | solution.py:13
  718.8 1.2 copy-start.2
  720.0 1.9 copy-start
  893.7 19.1 %copy-start.7 = (f32[1280]{0:T(1024)S(1)}, f32[1280]{0:T(1024)}, u32[]{:S(2)}) copy-start(f32[1280]{0:T(1024)} %param.8) | copy-start | bytes 15364
Sparse Core Ops, SparseCore 0:
  11.2 59.3 all-gather.5
  724.3 188.4 all-reduce.4
Sparse Core Ops, SparseCore 1:
  102.8 131.2 all-gather.7

commit v8 on v7

--- a/solution.py
+++ b/solution.py
@@ -142,7 +142,8 @@
 
     panel_blocks = PANEL // BLOCK
     first_cols = min(col_blocks, -(-panel_blocks // n_col))
-    cands = lax.all_gather(child_piece[:, : first_cols * BLOCK], ("sub", "col"))
+    cands = lax.all_gather(child_piece[:, : first_cols * BLOCK], "col")
+    cands = jnp.stack([cands, lax.ppermute(cands, "sub", [(0, 1), (1, 0)])])
     cands = cands.reshape(n_sub, n_col, rows_here, first_cols, BLOCK).transpose(0, 1, 3, 2, 4)
     cands = cands.reshape(n_sub, n_col * first_cols, rows_here, BLOCK)
     cand_pos = (
@@ -153,7 +154,8 @@
     for which in range(n_sub):
         found = col_map[which][cand_pos][None, :] == jnp.arange(panel_blocks, dtype=jnp.int32)[:, None]
         pick = jnp.argmax(found, axis=1)
-        stored = jnp.where(jnp.any(found, axis=1)[:, None, None], cands[which][pick], 0.0)
+        mine = lax.dynamic_index_in_dim(cands, (which + my_sub) % n_sub, 0, keepdims=False)
+        stored = jnp.where(jnp.any(found, axis=1)[:, None, None], mine[pick], 0.0)
         stored = stored.reshape(panel_blocks, row_blocks, BLOCK, BLOCK)
         pick_rows = sending_table(row_map[which], my_row, row_blocks, front_row_blocks, n_row, row_cap)
         pick_rows = jnp.minimum(pick_rows, row_blocks - 1).reshape(n_row, row_cap)

time: 964 us -> 961 us (level)
    all_gather x1, waiting for transfers between devices: 0.01 us -> 33.6 us  [shards(): cands = lax.all_gather(child_piece[:, :first_cols * BLOCK], 'col')]
    all_to_all x1, waiting for transfers between devices: 70.1 us -> 36.9 us  [shards(): lax.all_to_all(outgoing[0], 'col', split_axis=0, concat_axis=0, tiled=True)]
  transfers between devices with their start and end apart: 13 -> 14, of which waited for: 9 -> 9; matrix products, arithmetic and copies ran while one was open for 37% -> 37% of each run, Pallas kernels for 0% -> 0%
where the time goes in v8:
time: 961 us; the launch traced here: 954 us
  waiting for transfers between devices  432 us (45%)
  other arithmetic  201 us (21%)
  local copies, waits for them, and re-layouts  197 us (20%)
  matrix products  51.7 us (5%)
  starting transfers between devices  28 us (3%)
  blocking collectives  25.2 us (3%)
  between operations  18.8 us (2%)
    all_to_all x1, waiting for transfers between devices, row_receiving(): lax.all_to_all(sending, 'row', split_axis=0, concat_axis=0, tiled=True)  142 us
    ppermute x3, waiting for transfers between devices, row_receiving(): pieces.append(lax.ppermute(piece, 'row', pairs))  102 us
    ppermute x3, waiting for transfers between devices, shards(): lax.ppermute(piece, 'row', [(i, (i + shift) % n_row) for i in range(n_row)])  98.7 us
    another operation x15, other arithmetic, factor_corner(): lower = jnp.linalg.cholesky(symmetric_of(corner))  82 us
    another operation x4, other arithmetic, factor_corner(): jax.scipy.linalg.solve_triangular(lower, jnp.eye(PANEL, dtype=jnp.float32...  42.9 us
    all_to_all x1, waiting for transfers between devices, shards(): lax.all_to_all(outgoing[0], 'col', split_axis=0, concat_axis=0, tiled=True)  36.9 us
    gather x2, local copies, waits for them, and re-layouts, row_sending(): half.at[col_index[None, None, :], row_index[:, :, None]]  35.9 us
    dot_general x1, matrix products, shards(): lax.dot_general(own_rows, theirs, (((1,), (1,)), ((), ())), precision=lax...  35.3 us
  transfers between devices with their start and end apart: 14, of which 9 were waited for; matrix products, arithmetic and copies ran while one was open for 37% of the time, Pallas kernels for 0%

profile of v8, /device:TPU:0, one launch (start us, length us, event | category | flops | bytes accessed | tf_op | source)
XLA Modules:
  0.0 953.8 jit_solution(12618744392989941562)
XLA Ops:
  8.9 9.6 %copy.35 = f32[1,1536,1536]{1,2,0:T(8,128)} copy(f32[1,1536,1536]{2,1,0:T(8,128)} %param.5) | data formatting | bytes 18874368 | tf_op args[0]
  18.7 9.6 %copy.36 = f32[1536,12,128]{2,0,1:T(8,128)} copy(f32[1536,12,128]{0,2,1:T(8,128)} %bitcast.310) | data formatting | bytes 18874368 | tf_op jit(solution)/shard_map/reshape;squeeze | solution.py:165
  32.7 25.2 %all-gather.2 = f32[8,1,1280]{2,1,0:T(1,128)S(1)} all-gather(f32[1,1,1280]{2,1,0:T(1,128)S(1)} %reshape.1228), channel_id=1, replica_groups=mesh['sub'=2,'row'=4,'col'=4] {'sub','col'}, dimensions={0}, use_global_device_ids=true | all-gather | bytes 46080 | tf_op jit(solution)/shard_map/all_gather | solution.py:139
  57.9 13.4 %gather_fusion = f32[24,1536,128]{2,1,0:T(8,128)} fusion(f32[1536,12,128]{2,0,1:T(8,128)} %copy.36, s32[1024]{0:T(1024)S(1)} %pad_clamp_fusion.9), kind=kCustom, calls=%fused_computation | custom fusion | bytes 37748832 | tf_op jit(solution)/shard_map/gather | solution.py:169
  79.7 13.4 %slice_bitcast_fusion = (f32[4,3,1536,128]{3,2,1,0:T(8,128)}, f32[4,3,1536,128]{3,2,1,0:T(8,128)}) fusion(f32[2,4,3,1536,128]{4,3,2,1,0:T(8,128)} %bitcast.306), kind=kLoop, calls=%fused_computation.28 | loop fusion | bytes 37748736 | tf_op jit(solution)/shard_map/squeeze | solution.py:239
  109.8 11.7 %cholesky.103 = f32[128,128]{1,0:T(8,128)S(1)} custom-call(f32[128,128]{1,0:T(8,128)S(1)} %cholesky.263), custom_call_target="Cholesky" | custom-call | tf_op jit(solution)/shard_map/jit(cholesky)/cholesky | solution.py:71
  122.3 9.8 %custom-call.31 = f32[1,128,128]{1,2,0:T(8,128)S(1)} custom-call(f32[1,128,128]{2,1,0:T(8,128)S(1)} %get-tuple-element.106), custom_call_target="InvertDiagBlocksLowerTriangular" | custom-call | tf_op jit(solution)/shard_map/jit(cholesky)/cholesky | solution.py:71
  132.8 11.7 %cholesky.215 = f32[128,128]{1,0:T(8,128)S(1)} custom-call(f32[128,128]{1,0:T(8,128)S(1)} %cholesky.267), custom_call_target="Cholesky" | custom-call | tf_op jit(solution)/shard_map/jit(cholesky)/cholesky | solution.py:71
  145.1 9.9 %custom-call.32 = f32[1,128,128]{1,2,0:T(8,128)S(1)} custom-call(f32[1,128,128]{2,1,0:T(8,128)S(1)} %get-tuple-element.103), custom_call_target="InvertDiagBlocksLowerTriangular" | custom-call | tf_op jit(solution)/shard_map/jit(cholesky)/cholesky | solution.py:71
  155.7 11.7 %cholesky.236 = f32[128,128]{1,0:T(8,128)S(1)} custom-call(f32[128,128]{1,0:T(8,128)S(1)} %cholesky.272), custom_call_target="Cholesky" | custom-call | tf_op jit(solution)/shard_map/jit(cholesky)/cholesky | solution.py:71
  167.5 9.8 %custom-call.33 = f32[1,128,128]{1,2,0:T(8,128)S(1)} custom-call(f32[1,128,128]{2,1,0:T(8,128)S(1)} %get-tuple-element.100), custom_call_target="InvertDiagBlocksLowerTriangular" | custom-call | tf_op jit(solution)/shard_map/jit(cholesky)/cholesky | solution.py:71
  177.9 11.9 %cholesky.253 = f32[128,128]{1,0:T(8,128)S(1)} custom-call(f32[128,128]{1,0:T(8,128)S(1)} %convolution_subtract_fusion.6), custom_call_target="Cholesky" | custom-call | tf_op jit(solution)/shard_map/jit(cholesky)/cholesky | solution.py:71
  197.7 33.6 %all-gather.8.cloned.1.call-done = f32[6144,128]{1,0:T(8,128)} async-done(((f32[1536,128]{1,0:T(8,128)}), f32[6144,128]{1,0:T(8,128)}) %all-gather.8.cloned.1.call-update) | async-done | bytes 3145744 | tf_op jit(solution)/shard_map/all_gather | solution.py:145
  231.9 10.4 %while.1 = (s32[]{:T(128)}, f32[512,512]{1,0:T(8,128)S(1)}, s32[4,2]{0,1:T(2,128)S(1)}, f32[4,128,128]{2,1,0:T(8,128)}, s32[]{:T(128)}) while((s32[]{:T(128)}, f32[512,512]{1,0:T(8,128)S(1)}, s32[4,2]{0,1:T(2,128)S(1)}, f32[4,128,128]{2,1,0:T(8,128)}, s32[]{:T(128)}) %tuple.103), condition=%wide.while_cond, body=%wide.while_body.sunk | while | flops 2 | bytes 132205 | solution.py:72
  242.3 40.1 %custom-call.34 = f32[4,128,128]{1,2,0:T(8,128)S(1)} custom-call(f32[4,128,128]{2,1,0:T(8,128)} %get-tuple-element.38), custom_call_target="InvertDiagBlocksLowerTriangular" | custom-call | tf_op jit(solution)/shard_map/jit(_solve_triangular)/triangular_solve | solution.py:72
  309.7 9.7 %maximum_bitcast_fusion = f32[4,2,5,4,128,128]{5,4,3,2,0,1:T(8,128)} fusion(f32[1,4,4,5,128,128]{5,4,1,3,2,0:T(8,128)} %bitcast.312, f32[1,4,4,5,128,128]{5,4,1,3,2,0:T(8,128)} %bitcast.315), kind=kLoop, calls=%fused_computation.26 | loop fusion | flops 2621440 | bytes 20971520 | tf_op jit(solution)/shard_map/transpose | solution.py:163
  319.3 36.9 %all-to-all-done = f32[4,3,1536,128]{3,2,1,0:T(8,128)} async-done(((f32[4,3,1536,128]{3,2,1,0:T(8,128)}), f32[4,3,1536,128]{3,2,1,0:T(8,128)}, u32[]{:S(2)}, u32[]{:S(2)}) %all-to-all-start) | async-done | bytes 9437216 | tf_op jit(solution)/shard_map/all_to_all | solution.py:173
  356.9 14.3 %collective-permute-done.1 = f32[4,3,1536,128]{3,2,1,0:T(8,128)} collective-permute-done((f32[4,3,1536,128]{3,2,1,0:T(8,128)}, f32[4,3,1536,128]{3,2,1,0:T(8,128)}, u32[]{:S(2)}, u32[]{:S(2)}) %collective-permute-start.1) | collective-permute-done | bytes 9437216 | tf_op jit(solution)/shard_map/ppermute | solution.py:198
  371.2 18.1 %gather_fusion.9 = f32[200,128,128]{2,1,0:T(8,128)} fusion(f32[12,12,128,128]{3,2,1,0:T(8,128)} %bitcast.51, s32[200]{0:T(256)S(1)} %reshape.1159), kind=kCustom, calls=%fused_computation.9 | custom fusion | bytes 26216000 | tf_op jit(solution)/shard_map/gather | solution.py:211
  408.5 9.2 constant_dynamic-slice_fusion.3
  421.6 42.4 %collective-permute-done.7 = f32[2,5,4,128,128]{4,3,2,1,0:T(8,128)} collective-permute-done((f32[2,5,4,128,128]{4,3,2,1,0:T(8,128)}, f32[2,5,4,128,128]{4,3,2,1,0:T(8,128)}, u32[]{:S(2)}, u32[]{:S(2)}) %collective-permute-start.7) | collective-permute-done | bytes 2621472 | tf_op jit(solution)/shard_map/ppermute | solution.py:180
  466.3 56.3 %collective-permute-done.6 = f32[2,5,4,128,128]{4,3,2,1,0:T(8,128)} collective-permute-done((f32[2,5,4,128,128]{4,3,2,1,0:T(8,128)}, f32[2,5,4,128,128]{4,3,2,1,0:T(8,128)}, u32[]{:S(2)}, u32[]{:S(2)}) %collective-permute-start.6) | collective-permute-done | bytes 2621472 | tf_op jit(solution)/shard_map/ppermute | solution.py:180
  559.7 30.7 %collective-permute-done.4 = f32[5,10,128,128]{3,2,1,0:T(8,128)} collective-permute-done((f32[5,10,128,128]{3,2,1,0:T(8,128)}, f32[5,10,128,128]{3,2,1,0:T(8,128)}, u32[]{:S(2)}, u32[]{:S(2)}) %collective-permute-start.4) | collective-permute-done | bytes 3276832 | tf_op jit(solution)/shard_map/ppermute | solution.py:227
  590.4 71.6 %collective-permute-done.3 = f32[5,10,128,128]{3,2,1,0:T(8,128)} collective-permute-done((f32[5,10,128,128]{3,2,1,0:T(8,128)}, f32[5,10,128,128]{3,2,1,0:T(8,128)}, u32[]{:S(2)}, u32[]{:S(2)}) %collective-permute-start.3) | collective-permute-done | bytes 3276832 | tf_op jit(solution)/shard_map/ppermute | solution.py:227
  670.9 12.3 %gather_fusion.10 = f32[20,10,128,128]{3,2,1,0:T(8,128)} fusion(f32[20,10,128,128]{3,2,1,0:T(8,128)} %bitcast.309, s32[1024]{0:T(1024)S(1)} %pad_clamp_fusion.3), kind=kCustom, calls=%fused_computation.10 | custom fusion | bytes 26214480 | tf_op jit(solution)/shard_map/gather | solution.py:234
  683.2 17.7 %gather_fusion.13 = f32[200,128,128]{2,1,0:T(8,128)} fusion(f32[12,12,128,128]{3,2,1,0:T(8,128)} %bitcast.105, s32[200]{0:T(256)S(1)} %reshape.1189), kind=kCustom, calls=%fused_computation.13 | custom fusion | bytes 26216000 | tf_op jit(solution)/shard_map/gather | solution.py:211
  708.0 10.6 %fusion.121 = f32[2560,512]{1,0:T(8,128)S(1)} fusion(f32[2560,512]{1,0:T(8,128)} %fusion.3, f32[512,512]{1,0:T(8,128)S(1)} %copy-done.1), kind=kOutput, calls=%fused_computation.387 | convolution fusion | flops 8053063680 | bytes 11534336 | tf_op jit(solution)/shard_map/dot_general | solution.py:79
  729.2 141.8 %all-to-all-done.2 = f32[4,5,10,128,128]{4,3,2,1,0:T(8,128)} async-done(((f32[4,5,10,128,128]{4,3,2,1,0:T(8,128)}), f32[4,5,10,128,128]{4,3,2,1,0:T(8,128)}, u32[]{:S(2)}, u32[]{:S(2)}) %all-to-all-start.2) | async-done | bytes 13107232 | tf_op jit(solution)/shard_map/all_to_all | solution.py:232
  871.0 12.5 %gather_fusion.14 = f32[20,10,128,128]{3,2,1,0:T(8,128)} fusion(f32[20,10,128,128]{3,2,1,0:T(8,128)} %bitcast.109, s32[1024]{0:T(1024)S(1)} %pad_clamp_fusion), kind=kCustom, calls=%fused_computation.14 | custom fusion | bytes 26214480 | tf_op jit(solution)/shard_map/gather | solution.py:234
  883.4 9.3 add_bitcast_fusion
  892.7 14.1 %copy.43 = f32[20,128,10,128]{3,2,1,0:T(8,128)} copy(f32[20,128,10,128]{3,1,2,0:T(8,128)S(1)} %add_bitcast_fusion) | data formatting | bytes 26214400 | tf_op jit(solution)/shard_map/reshape | solution.py:248
  910.6 35.3 %fusion.1 = f32[2560,1280]{1,0:T(8,128)} fusion(f32[2560,512]{1,0:T(8,128)} %pad_maximum_fusion.2, f32[1280,512]{1,0:T(8,128)} %all-reduce.5.cloned.1.call-done, f32[320,8,10,128]{3,2,1,0:T(8,128)} %bitcast.316, f32[2560,512]{1,0:T(8,128)} %param.9, f32[1280]{0:T(1024)S(1)} %copy-done.8, s32[1280]{0:T(1024)S(1)} %iota_add_fusion.1, ...), kind=kOutput, calls=%fused_computation.21 | convolution fusion | flops 20162150400 | bytes 39348480 | tf_op jit(solution)/shard_map/dot_general | solution.py:265
  (252 shorter events, 170.7 us)
Async XLA Ops:
  7.4 64.0 %all-gather.6.cloned.1.call-start = ((), (), s32[]{:S(2)}) async-start(), calls=%async_computation.4 | async-start | bytes 2162688 | tf_op jit(solution)/shard_map/all_gather | solution.py:93
  8.9 9.6 %copy-start.5 = (s32[2,48]{1,0:T(2,128)S(1)}, s32[2,48]{1,0:T(2,128)}, u32[]{:S(2)}) copy-start(s32[2,48]{1,0:T(2,128)} %param.6) | copy-start | bytes 1156
  8.9 9.7 %copy-start.6 = (s32[2,48]{1,0:T(2,128)S(1)}, s32[2,48]{1,0:T(2,128)}, u32[]{:S(2)}) copy-start(s32[2,48]{1,0:T(2,128)} %param.7) | copy-start | bytes 1156
  18.7 14.0 %copy-start.7 = (f32[1280]{0:T(1024)S(1)}, f32[1280]{0:T(1024)}, u32[]{:S(2)}) copy-start(f32[1280]{0:T(1024)} %param.8) | copy-start | bytes 15364
  29.2 72.0 %copy-start.12 = (s32[48]{0:T(128)}, s32[48]{0:T(128)S(1)}, u32[]{:S(2)}) copy-start(s32[48]{0:T(128)S(1)} %get-tuple-element.50) | copy-start | bytes 580
  29.2 72.0 %copy-start.14 = (s32[48]{0:T(128)}, s32[48]{0:T(128)S(1)}, u32[]{:S(2)}) copy-start(s32[48]{0:T(128)S(1)} %get-tuple-element.52) | copy-start | bytes 580
  93.1 263.1 %all-to-all-start = ((f32[4,3,1536,128]{3,2,1,0:T(8,128)}), f32[4,3,1536,128]{3,2,1,0:T(8,128)}, u32[]{:S(2)}, u32[]{:S(2)}) async-start(f32[4,3,1536,128]{3,2,1,0:T(8,128)} %get-tuple-element.82), calls=%async_computation | async-start | bytes 18874368 | tf_op jit(solution)/shard_map/all_to_all | solution.py:173
  98.9 132.3 %all-gather.8.cloned.1.call-start = ((), (), s32[]{:S(2)}) async-start(), calls=%async_computation.5 | async-start | bytes 3932160 | tf_op jit(solution)/shard_map/all_gather | solution.py:145
  109.8 173.9 %copy-start.3 = (f32[512,512]{1,0:T(8,128)S(1)}, f32[512,512]{1,0:T(8,128)}, u32[]{:S(2)}) copy-start(f32[512,512]{1,0:T(8,128)} %fusion.18) | copy-start | bytes 3145732
  231.2 56.3 %collective-permute-start = (f32[4,1536,128]{2,1,0:T(8,128)}, f32[4,1536,128]{2,1,0:T(8,128)}, u32[]{:S(2)}, u32[]{:S(2)}) collective-permute-start(f32[4,1536,128]{2,1,0:T(8,128)} %bitcast.324), channel_id=1, source_target_pairs={{0,16},{16,0},{1,17},{17,1},{2,18},{18,2},{3,19},{19,3},{4,20},{20... | collective-permute-start | bytes 9437192 | tf_op jit(solution)/shard_map/ppermute | solution.py:146
  282.5 5.1 copy-start.4
  291.9 2.5 copy-start.10
  299.8 4.4 copy-start.11
  309.7 46.6 %copy-start.18 = (pred[20]{0:T(512)(128)(4,1)S(1)}, pred[20]{0:T(512)(128)(4,1)}, u32[]{:S(2)}) copy-start(pred[20]{0:T(512)(128)(4,1)} %get-tuple-element.45) | copy-start | bytes 64
  309.7 46.6 %copy-start.19 = (s32[20]{0:T(128)S(1)}, s32[20]{0:T(128)}, u32[]{:S(2)}) copy-start(s32[20]{0:T(128)} %get-tuple-element.41) | copy-start | bytes 244
  309.7 46.7 %copy-start.16 = (pred[20]{0:T(512)(128)(4,1)S(1)}, pred[20]{0:T(512)(128)(4,1)}, u32[]{:S(2)}) copy-start(pred[20]{0:T(512)(128)(4,1)} %get-tuple-element.43) | copy-start | bytes 64
  309.7 46.7 %copy-start.17 = (s32[20]{0:T(128)S(1)}, s32[20]{0:T(128)}, u32[]{:S(2)}) copy-start(s32[20]{0:T(128)} %get-tuple-element.39) | copy-start | bytes 244
  309.7 46.8 %copy-start.9 = (s32[48]{0:T(128)S(1)}, s32[48]{0:T(128)}, u32[]{:S(2)}) copy-start(s32[48]{0:T(128)} %get-tuple-element.49) | copy-start | bytes 580
  356.2 15.0 %collective-permute-start.1 = (f32[4,3,1536,128]{3,2,1,0:T(8,128)}, f32[4,3,1536,128]{3,2,1,0:T(8,128)}, u32[]{:S(2)}, u32[]{:S(2)}) collective-permute-start(f32[4,3,1536,128]{3,2,1,0:T(8,128)} %all-to-all-done), channel_id=1, source_target_pairs={{0,16},{16,0},{1,17},{17,1},{2,18},{18,2},{3,19},{19,3},{4,20},{20... | collective-permute-start | bytes 28311560 | tf_op jit(solution)/shard_map/ppermute | solution.py:198
  389.3 293.9 %all-to-all-start.1 = ((f32[4,3,1536,128]{3,2,1,0:T(8,128)}), f32[4,3,1536,128]{3,2,1,0:T(8,128)}, u32[]{:S(2)}, u32[]{:S(2)}) async-start(f32[4,3,1536,128]{3,2,1,0:T(8,128)} %get-tuple-element.24), calls=%async_computation.1 | async-start | bytes 18874368 | tf_op jit(solution)/shard_map/all_to_all | solution.py:241
  395.3 12.8 %copy-start.15 = (s32[48]{0:T(128)S(1)}, s32[48]{0:T(128)}, u32[]{:S(2)}) copy-start(s32[48]{0:T(128)} %copy-done.14) | copy-start | bytes 580
  395.3 13.0 %copy-start.13 = (s32[48]{0:T(128)S(1)}, s32[48]{0:T(128)}, u32[]{:S(2)}) copy-start(s32[48]{0:T(128)} %copy-done.12) | copy-start | bytes 580
  403.9 60.0 %collective-permute-start.7 = (f32[2,5,4,128,128]{4,3,2,1,0:T(8,128)}, f32[2,5,4,128,128]{4,3,2,1,0:T(8,128)}, u32[]{:S(2)}, u32[]{:S(2)}) collective-permute-start(f32[2,5,4,128,128]{4,3,2,1,0:T(8,128)} %get-tuple-element.90), channel_id=1, source_target_pairs={{0,12},{4,0},{8,4},{12,8},{1,13},{5,1},{9,5},{13,9},{2,14},{6,2},{... | collective-permute-start | bytes 7864328 | tf_op jit(solution)/shard_map/ppermute | solution.py:180
  406.4 116.2 %collective-permute-start.6 = (f32[2,5,4,128,128]{4,3,2,1,0:T(8,128)}, f32[2,5,4,128,128]{4,3,2,1,0:T(8,128)}, u32[]{:S(2)}, u32[]{:S(2)}) collective-permute-start(f32[2,5,4,128,128]{4,3,2,1,0:T(8,128)} %get-tuple-element.91), channel_id=1, source_target_pairs={{0,8},{4,12},{8,0},{12,4},{1,9},{5,13},{9,1},{13,5},{2,10},{6,14},... | collective-permute-start | bytes 7864328 | tf_op jit(solution)/shard_map/ppermute | solution.py:180
  406.9 115.8 %collective-permute-start.5 = (f32[2,5,4,128,128]{4,3,2,1,0:T(8,128)}, f32[2,5,4,128,128]{4,3,2,1,0:T(8,128)}, u32[]{:S(2)}, u32[]{:S(2)}) collective-permute-start(f32[2,5,4,128,128]{4,3,2,1,0:T(8,128)} %get-tuple-element.92), channel_id=1, source_target_pairs={{0,4},{4,8},{8,12},{12,0},{1,5},{5,9},{9,13},{13,1},{2,6},{6,10},{... | collective-permute-start | bytes 7864328 | tf_op jit(solution)/shard_map/ppermute | solution.py:180
  417.7 172.7 %collective-permute-start.4 = (f32[5,10,128,128]{3,2,1,0:T(8,128)}, f32[5,10,128,128]{3,2,1,0:T(8,128)}, u32[]{:S(2)}, u32[]{:S(2)}) collective-permute-start(f32[5,10,128,128]{3,2,1,0:T(8,128)} %get-tuple-element.84), channel_id=1, source_target_pairs={{0,12},{4,0},{8,4},{12,8},{1,13},{5,1},{9,5},{13,9},{2,14},{6,2},{... | collective-permute-start | bytes 9830408 | tf_op jit(solution)/shard_map/ppermute | solution.py:227
  420.0 242.0 %collective-permute-start.3 = (f32[5,10,128,128]{3,2,1,0:T(8,128)}, f32[5,10,128,128]{3,2,1,0:T(8,128)}, u32[]{:S(2)}, u32[]{:S(2)}) collective-permute-start(f32[5,10,128,128]{3,2,1,0:T(8,128)} %get-tuple-element.85), channel_id=1, source_target_pairs={{0,8},{4,12},{8,0},{12,4},{1,9},{5,13},{9,1},{13,5},{2,10},{6,14},... | collective-permute-start | bytes 9830408 | tf_op jit(solution)/shard_map/ppermute | solution.py:227
  463.9 198.0 %collective-permute-start.2 = (f32[5,10,128,128]{3,2,1,0:T(8,128)}, f32[5,10,128,128]{3,2,1,0:T(8,128)}, u32[]{:S(2)}, u32[]{:S(2)}) collective-permute-start(f32[5,10,128,128]{3,2,1,0:T(8,128)} %get-tuple-element.86), channel_id=1, source_target_pairs={{0,4},{4,8},{8,12},{12,0},{1,5},{5,9},{9,13},{13,1},{2,6},{6,10},{... | collective-permute-start | bytes 9830408 | tf_op jit(solution)/shard_map/ppermute | solution.py:227
  701.0 7.1 copy-start.1
  701.0 170.0 %all-to-all-start.2 = ((f32[4,5,10,128,128]{4,3,2,1,0:T(8,128)}), f32[4,5,10,128,128]{4,3,2,1,0:T(8,128)}, u32[]{:S(2)}, u32[]{:S(2)}) async-start(f32[4,5,10,128,128]{4,3,2,1,0:T(8,128)} %bitcast.307), calls=%async_computation.2 | async-start | bytes 26214400 | tf_op jit(solution)/shard_map/all_to_all | solution.py:232
  707.5 203.1 %all-reduce.5.cloned.1.call-start = ((), (), s32[]{:S(2)}) async-start(), calls=%async_computation.3 | async-start | bytes 5242880 | tf_op jit(solution)/shard_map/psum | solution.py:13
  892.7 18.0 %copy-start.8 = (f32[1280]{0:T(1024)S(1)}, f32[1280]{0:T(1024)}, u32[]{:S(2)}) copy-start(f32[1280]{0:T(1024)} %param.8) | copy-start | bytes 15364
  (2 other events, 3.2 us)
Sparse Core Ops, SparseCore 0:
  11.2 59.1 all-gather.5
  724.2 186.3 all-reduce.4
Sparse Core Ops, SparseCore 1:
  101.2 130.0 all-gather.7

commit v9 on v8

--- a/solution.py
+++ b/solution.py
@@ -142,25 +142,46 @@
 
     panel_blocks = PANEL // BLOCK
     first_cols = min(col_blocks, -(-panel_blocks // n_col))
-    cands = lax.all_gather(child_piece[:, : first_cols * BLOCK], "col")
+    own_cands = child_piece[:, : first_cols * BLOCK].reshape(row_blocks, BLOCK, first_cols * BLOCK)
+    pick_rows = sending_table(my_rows_map, my_row, row_blocks, front_row_blocks, n_row, row_cap)
+    pick_rows = jnp.minimum(pick_rows, row_blocks - 1).reshape(n_row, row_cap)
+    cand_send = own_cands.at[pick_rows].get(mode="promise_in_bounds")
+    pieces = [lax.dynamic_index_in_dim(cand_send, my_row, 0, keepdims=False)]
+    for shift in range(1, n_row):
+        piece = lax.dynamic_index_in_dim(cand_send, (my_row + shift) % n_row, 0, keepdims=False)
+        pieces.append(lax.ppermute(piece, "row", [(i, (i + shift) % n_row) for i in range(n_row)]))
+    cand_got = jnp.stack(pieces).reshape(n_row * row_cap, BLOCK, first_cols * BLOCK)
+    placement = receiving_table(
+        my_rows_map, my_row, row_blocks, front_row_blocks, row_cap, 0, n_row * row_cap
+    )
+    row_valid = placement < n_row * row_cap
+    source = jnp.minimum(placement, n_row * row_cap - 1) // row_cap
+    placement = ((my_row - source) % n_row) * row_cap + placement % row_cap
+    cand_rows = jnp.where(
+        row_valid[:, None, None], cand_got.at[placement].get(mode="promise_in_bounds"), 0.0
+    )
+    cands = lax.all_gather(cand_rows, "col")
     cands = jnp.stack([cands, lax.ppermute(cands, "sub", [(0, 1), (1, 0)])])
-    cands = cands.reshape(n_sub, n_col, rows_here, first_cols, BLOCK).transpose(0, 1, 3, 2, 4)
-    cands = cands.reshape(n_sub, n_col * first_cols, rows_here, BLOCK)
+    cands = cands.reshape(n_sub, n_col, front_row_blocks, BLOCK, first_cols, BLOCK)
+    cands = cands.transpose(0, 1, 4, 2, 3, 5).reshape(
+        n_sub, n_col * first_cols, front_row_blocks, BLOCK, BLOCK
+    )
     cand_pos = (
         jnp.arange(n_col, dtype=jnp.int32)[:, None] * col_blocks
         + jnp.arange(first_cols, dtype=jnp.int32)[None, :]
     ).reshape(-1)
-    panel_send = []
+    panel_rows = None
     for which in range(n_sub):
         found = col_map[which][cand_pos][None, :] == jnp.arange(panel_blocks, dtype=jnp.int32)[:, None]
         pick = jnp.argmax(found, axis=1)
         mine = lax.dynamic_index_in_dim(cands, (which + my_sub) % n_sub, 0, keepdims=False)
-        stored = jnp.where(jnp.any(found, axis=1)[:, None, None], mine[pick], 0.0)
-        stored = stored.reshape(panel_blocks, row_blocks, BLOCK, BLOCK)
-        pick_rows = sending_table(row_map[which], my_row, row_blocks, front_row_blocks, n_row, row_cap)
-        pick_rows = jnp.minimum(pick_rows, row_blocks - 1).reshape(n_row, row_cap)
-        panel_send.append(stored.at[:, pick_rows].get(mode="promise_in_bounds"))
-    panel_send = jnp.stack(panel_send).transpose(2, 0, 3, 1, 4, 5)
+        got = jnp.where(jnp.any(found, axis=1)[:, None, None, None], mine[pick], 0.0)
+        panel_rows = got if panel_rows is None else panel_rows + got
+    panel_rows = panel_rows.transpose(1, 2, 0, 3).reshape(front_rows, PANEL)
+    panel_rows = panel_rows + jnp.where(global_row[:, None] >= PANEL, coupling, 0.0)
+    panel_rows = panel_rows + jnp.where(
+        global_row[:, None] == jnp.arange(PANEL, dtype=jnp.int32)[None, :], full_diagonal[None, :PANEL], 0.0
+    )
 
     by_col = child_piece.reshape(rows_here, col_blocks, BLOCK)
     chosen = sending_table(my_cols_map, my_col, col_blocks, front_col_blocks, n_group, col_cap)
@@ -171,29 +192,8 @@
     outgoing, corner = lax.optimization_barrier((outgoing, corner))
     lower, inverse = factor_corner(corner)
     other_half = lax.all_to_all(outgoing[0], "col", split_axis=0, concat_axis=0, tiled=True)
-    other_half, lower, inverse, panel_send = lax.optimization_barrier(
-        (other_half, lower, inverse, panel_send)
-    )
-    pieces = [lax.dynamic_index_in_dim(panel_send, my_row, 0, keepdims=False)]
-    for shift in range(1, n_row):
-        piece = lax.dynamic_index_in_dim(panel_send, (my_row + shift) % n_row, 0, keepdims=False)
-        pieces.append(lax.ppermute(piece, "row", [(i, (i + shift) % n_row) for i in range(n_row)]))
-    panel_got = jnp.stack(pieces)
-    panel_rows = None
-    for which in range(n_sub):
-        placement = receiving_table(
-            row_map[which], my_row, row_blocks, front_row_blocks, row_cap, 0, n_row * row_cap
-        )
-        row_valid = placement < n_row * row_cap
-        source = jnp.minimum(placement, n_row * row_cap - 1) // row_cap
-        placement = ((my_row - source) % n_row) * row_cap + placement % row_cap
-        got = panel_got[:, which].reshape(n_row * row_cap, panel_blocks, BLOCK, BLOCK)
-        got = jnp.where(row_valid[:, None, None, None], got.at[placement].get(mode="promise_in_bounds"), 0.0)
-        panel_rows = got if panel_rows is None else panel_rows + got
-    panel_rows = panel_rows.transpose(0, 2, 1, 3).reshape(front_rows, PANEL)
-    panel_rows = panel_rows + jnp.where(global_row[:, None] >= PANEL, coupling, 0.0)
-    panel_rows = panel_rows + jnp.where(
-        global_row[:, None] == jnp.arange(PANEL, dtype=jnp.int32)[None, :], full_diagonal[None, :PANEL], 0.0
+    other_half, lower, inverse, panel_rows = lax.optimization_barrier(
+        (other_half, lower, inverse, panel_rows)
     )
     other_half = lax.ppermute(other_half, "sub", [(0, 1), (1, 0)])
 
@@ -239,7 +239,7 @@
     sending_other, own_outgoing = lax.optimization_barrier((sending_other, outgoing[1]))
     part_other, keep_other = row_receiving(sending_other, col_valid_other, rows_other, True)
     own_half = lax.all_to_all(own_outgoing, "col", split_axis=0, concat_axis=0, tiled=True)
-    own_half, part_other, panel_rows = lax.optimization_barrier((own_half, part_other, panel_rows))
+    own_half, part_other = lax.optimization_barrier((own_half, part_other))
     sending_own, col_valid_own, rows_own = row_sending(own_half, my_sub)
     part_own, keep_own = row_receiving(sending_own, col_valid_own, rows_own, False)
     assembled = jnp.where(keep_other[:, :, None, None], part_other, 0.0) + jnp.where(

time: 961 us -> 918 us (0.955)
  local copies, waits for them, and re-layouts: 197 us -> 172 us
  other arithmetic: 201 us -> 183 us
    ppermute x3, waiting for transfers between devices: 98.7 us -> 0.01 us  [shards(): lax.ppermute(piece, 'row', [(i, (i + shift) % n_row) for i in range(n_row)])]
    all_gather x1, waiting for transfers between devices: 33.6 us -> 102 us  [shards(): cands = lax.all_gather(cand_rows, 'col')]
    ppermute x3, waiting for transfers between devices: 102 us -> 140 us  [row_receiving(): pieces.append(lax.ppermute(piece, 'row', pairs))]
    all_to_all x1, waiting for transfers between devices: 36.9 us -> 0.01 us  [shards(): lax.all_to_all(outgoing[0], 'col', split_axis=0, concat_axis=0, tiled=True)]
    all_to_all x1, waiting for transfers between devices: 0.01 us -> 30.4 us  [shards(): lax.all_to_all(own_outgoing, 'col', split_axis=0, concat_axis=0, tiled=True)]
    gather x6 -> x4, local copies, waits for them, and re-layouts: 24.5 us -> 12.8 us  [the longest x2 11.5 us: shards(): mine[pick]]
    transpose x1 -> x0, other arithmetic: 9.65 us -> none  [shards(): panel_send = jnp.stack(panel_send).transpose(2, 0, 3, 1, 4, 5)]
  transfers between devices with their start and end apart: 14 -> 14, of which waited for: 9 -> 7; matrix products, arithmetic and copies ran while one was open for 37% -> 36% of each run, Pallas kernels for 0% -> 0%
where the time goes in v9:
time: 918 us; the launch traced here: 910 us
  waiting for transfers between devices  433 us (47%)
  other arithmetic  183 us (20%)
  local copies, waits for them, and re-layouts  172 us (19%)
  matrix products  51.5 us (6%)
  starting transfers between devices  29.8 us (3%)
  blocking collectives  23.9 us (3%)
  between operations  17.1 us (2%)
    all_to_all x1, waiting for transfers between devices, row_receiving(): lax.all_to_all(sending, 'row', split_axis=0, concat_axis=0, tiled=True)  143 us
    ppermute x3, waiting for transfers between devices, row_receiving(): pieces.append(lax.ppermute(piece, 'row', pairs))  140 us
    all_gather x1, waiting for transfers between devices, shards(): cands = lax.all_gather(cand_rows, 'col')  102 us
    another operation x15, other arithmetic, factor_corner(): lower = jnp.linalg.cholesky(symmetric_of(corner))  81.7 us
    another operation x4, other arithmetic, factor_corner(): jax.scipy.linalg.solve_triangular(lower, jnp.eye(PANEL, dtype=jnp.float32...  43 us
    gather x2, local copies, waits for them, and re-layouts, row_sending(): half.at[col_index[None, None, :], row_index[:, :, None]]  35.4 us
    dot_general x1, matrix products, shards(): lax.dot_general(own_rows, theirs, (((1,), (1,)), ((), ())), precision=lax...  35.1 us
    all_to_all x1, waiting for transfers between devices, shards(): lax.all_to_all(own_outgoing, 'col', split_axis=0, concat_axis=0, tiled=True)  30.4 us
  transfers between devices with their start and end apart: 14, of which 7 were waited for; matrix products, arithmetic and copies ran while one was open for 36% of the time, Pallas kernels for 0%

profile of v9, /device:TPU:0, one launch (start us, length us, event | category | flops | bytes accessed | tf_op | source)
XLA Modules:
  0.0 910.0 jit_solution(4509783773995426641)
XLA Ops:
  20.3 9.6 %copy.32 = f32[1,1536,1536]{1,2,0:T(8,128)} copy(f32[1,1536,1536]{2,1,0:T(8,128)} %param.5) | data formatting | bytes 18874368 | tf_op args[0]
  31.1 23.9 %all-gather.1 = f32[8,1,1280]{2,1,0:T(1,128)S(1)} all-gather(f32[1,1,1280]{2,1,0:T(1,128)S(1)} %reshape.978), channel_id=1, replica_groups=mesh['sub'=2,'row'=4,'col'=4] {'sub','col'}, dimensions={0}, use_global_device_ids=true | all-gather | bytes 46080 | tf_op jit(solution)/shard_map/all_gather | solution.py:139
  55.5 9.6 %copy.33 = f32[1536,12,128]{2,0,1:T(8,128)} copy(f32[1536,12,128]{0,2,1:T(8,128)} %bitcast.253) | data formatting | bytes 18874368 | tf_op jit(solution)/shard_map/reshape;squeeze | solution.py:186
  66.8 13.3 %gather_fusion = f32[24,1536,128]{2,1,0:T(8,128)} fusion(f32[1536,12,128]{2,0,1:T(8,128)} %copy.33, s32[1024]{0:T(1024)S(1)} %pad_clamp_fusion.7), kind=kCustom, calls=%fused_computation | custom fusion | bytes 37748832 | tf_op jit(solution)/shard_map/gather | solution.py:190
  90.9 13.9 %slice_bitcast_fusion = (f32[4,3,1536,128]{3,2,1,0:T(8,128)}, f32[4,3,1536,128]{3,2,1,0:T(8,128)}) fusion(f32[2,4,3,1536,128]{4,3,2,1,0:T(8,128)} %bitcast.249), kind=kLoop, calls=%fused_computation.28 | loop fusion | bytes 37748736 | tf_op jit(solution)/shard_map/squeeze | solution.py:239
  116.3 11.7 %cholesky.103 = f32[128,128]{1,0:T(8,128)S(1)} custom-call(f32[128,128]{1,0:T(8,128)S(1)} %cholesky.263), custom_call_target="Cholesky" | custom-call | tf_op jit(solution)/shard_map/jit(cholesky)/cholesky | solution.py:71
  128.7 9.8 %custom-call.31 = f32[1,128,128]{1,2,0:T(8,128)S(1)} custom-call(f32[1,128,128]{2,1,0:T(8,128)S(1)} %get-tuple-element.92), custom_call_target="InvertDiagBlocksLowerTriangular" | custom-call | tf_op jit(solution)/shard_map/jit(cholesky)/cholesky | solution.py:71
  139.2 11.7 %cholesky.215 = f32[128,128]{1,0:T(8,128)S(1)} custom-call(f32[128,128]{1,0:T(8,128)S(1)} %cholesky.267), custom_call_target="Cholesky" | custom-call | tf_op jit(solution)/shard_map/jit(cholesky)/cholesky | solution.py:71
  151.5 9.9 %custom-call.32 = f32[1,128,128]{1,2,0:T(8,128)S(1)} custom-call(f32[1,128,128]{2,1,0:T(8,128)S(1)} %get-tuple-element.89), custom_call_target="InvertDiagBlocksLowerTriangular" | custom-call | tf_op jit(solution)/shard_map/jit(cholesky)/cholesky | solution.py:71
  161.4 102.2 %all-gather.5.cloned.1.call-done = f32[4,20,128,128]{3,2,1,0:T(8,128)} async-done(((f32[1,20,128,128]{3,2,1,0:T(8,128)}), f32[4,20,128,128]{3,2,1,0:T(8,128)}) %all-gather.5.cloned.1.call-update) | async-done | bytes 5242896 | tf_op jit(solution)/shard_map/all_gather | solution.py:163
  264.3 11.7 %cholesky.236 = f32[128,128]{1,0:T(8,128)S(1)} custom-call(f32[128,128]{1,0:T(8,128)S(1)} %cholesky.272), custom_call_target="Cholesky" | custom-call | tf_op jit(solution)/shard_map/jit(cholesky)/cholesky | solution.py:71
  276.0 9.8 %custom-call.33 = f32[1,128,128]{1,2,0:T(8,128)S(1)} custom-call(f32[1,128,128]{2,1,0:T(8,128)S(1)} %get-tuple-element.86), custom_call_target="InvertDiagBlocksLowerTriangular" | custom-call | tf_op jit(solution)/shard_map/jit(cholesky)/cholesky | solution.py:71
  286.5 11.9 %cholesky.253 = f32[128,128]{1,0:T(8,128)S(1)} custom-call(f32[128,128]{1,0:T(8,128)S(1)} %convolution_subtract_fusion.6), custom_call_target="Cholesky" | custom-call | tf_op jit(solution)/shard_map/jit(cholesky)/cholesky | solution.py:71
  306.9 10.8 %while.1 = (s32[]{:T(128)}, f32[512,512]{1,0:T(8,128)S(1)}, s32[4,2]{0,1:T(2,128)S(1)}, f32[4,128,128]{2,1,0:T(8,128)}, s32[]{:T(128)}) while((s32[]{:T(128)}, f32[512,512]{1,0:T(8,128)S(1)}, s32[4,2]{0,1:T(2,128)S(1)}, f32[4,128,128]{2,1,0:T(8,128)}, s32[]{:T(128)}) %tuple.85), condition=%wide.while_cond, body=%wide.while_body.sunk | while | flops 2 | bytes 132705 | solution.py:72
  317.6 40.1 %custom-call.34 = f32[4,128,128]{1,2,0:T(8,128)S(1)} custom-call(f32[4,128,128]{2,1,0:T(8,128)} %get-tuple-element.36), custom_call_target="InvertDiagBlocksLowerTriangular" | custom-call | tf_op jit(solution)/shard_map/jit(_solve_triangular)/triangular_solve | solution.py:72
  362.8 7.2 fusion.6
  396.1 14.0 %collective-permute-done.4 = f32[4,3,1536,128]{3,2,1,0:T(8,128)} collective-permute-done((f32[4,3,1536,128]{3,2,1,0:T(8,128)}, f32[4,3,1536,128]{3,2,1,0:T(8,128)}, u32[]{:S(2)}, u32[]{:S(2)}) %collective-permute-start.4) | collective-permute-done | bytes 9437216 | tf_op jit(solution)/shard_map/ppermute | solution.py:198
  410.0 17.7 %gather_fusion.9 = f32[200,128,128]{2,1,0:T(8,128)} fusion(f32[12,12,128,128]{3,2,1,0:T(8,128)} %bitcast.66, s32[200]{0:T(256)S(1)} %reshape.928), kind=kCustom, calls=%fused_computation.9 | custom fusion | bytes 26216000 | tf_op jit(solution)/shard_map/gather | solution.py:211
  433.7 9.2 %constant_dynamic-slice_fusion.1 = (f32[1,5,10,128,128]{4,3,2,1,0:T(8,128)S(1)}, f32[5,10,128,128]{3,2,1,0:T(8,128)}, f32[5,10,128,128]{3,2,1,0:T(8,128)}, f32[5,10,128,128]{3,2,1,0:T(8,128)}) fusion(f32[4,5,10,128,128]{4,3,2,1,0:T(8,128)} %bitcast.251, s32[]{:T(128)S(6)} %select_n.707, s32[]{:T(128)S(6)} %select_n.713, s32[]{:T(128)S(6)} %select_n.711, ...), kind=kLoop, calls=%fused_computation.165 | loop fusion | bytes 26214416 | tf_op jit(solution)/shard_map/jit(dynamic_index_in_dim)/dynamic_slice | solution.py:223
  448.3 70.1 %collective-permute-done.5 = f32[5,10,128,128]{3,2,1,0:T(8,128)} collective-permute-done((f32[5,10,128,128]{3,2,1,0:T(8,128)}, f32[5,10,128,128]{3,2,1,0:T(8,128)}, u32[]{:S(2)}, u32[]{:S(2)}) %collective-permute-start.5) | collective-permute-done | bytes 3276832 | tf_op jit(solution)/shard_map/ppermute | solution.py:227
  518.4 69.9 %collective-permute-done.6 = f32[5,10,128,128]{3,2,1,0:T(8,128)} collective-permute-done((f32[5,10,128,128]{3,2,1,0:T(8,128)}, f32[5,10,128,128]{3,2,1,0:T(8,128)}, u32[]{:S(2)}, u32[]{:S(2)}) %collective-permute-start.6) | collective-permute-done | bytes 3276832 | tf_op jit(solution)/shard_map/ppermute | solution.py:227
  588.2 9.0 pad_maximum_fusion
  597.2 12.5 %gather_fusion.10 = f32[20,10,128,128]{3,2,1,0:T(8,128)} fusion(f32[20,10,128,128]{3,2,1,0:T(8,128)} %bitcast.252, s32[1024]{0:T(1024)S(1)} %pad_clamp_fusion.1), kind=kCustom, calls=%fused_computation.10 | custom fusion | bytes 26214480 | tf_op jit(solution)/shard_map/gather | solution.py:234
  609.7 30.4 %all-to-all-done.1 = f32[4,3,1536,128]{3,2,1,0:T(8,128)} async-done(((f32[4,3,1536,128]{3,2,1,0:T(8,128)}), f32[4,3,1536,128]{3,2,1,0:T(8,128)}, u32[]{:S(2)}, u32[]{:S(2)}) %all-to-all-start.1) | async-done | bytes 9437216 | tf_op jit(solution)/shard_map/all_to_all | solution.py:241
  640.1 17.7 %gather_fusion.11 = f32[200,128,128]{2,1,0:T(8,128)} fusion(f32[12,12,128,128]{3,2,1,0:T(8,128)} %bitcast.84, s32[200]{0:T(256)S(1)} %reshape.942), kind=kCustom, calls=%fused_computation.11 | custom fusion | bytes 26216000 | tf_op jit(solution)/shard_map/gather | solution.py:211
  657.8 6.5 all-to-all-start.2
  664.7 10.6 %fusion.99 = f32[2560,512]{1,0:T(8,128)S(1)} fusion(f32[2560,512]{1,0:T(8,128)} %fusion.7, f32[512,512]{1,0:T(8,128)S(1)} %copy-done.2), kind=kOutput, calls=%fused_computation.327 | convolution fusion | flops 8053063680 | bytes 11534336 | tf_op jit(solution)/shard_map/dot_general | solution.py:79
  685.9 142.7 %all-to-all-done.2 = f32[4,5,10,128,128]{4,3,2,1,0:T(8,128)} async-done(((f32[4,5,10,128,128]{4,3,2,1,0:T(8,128)}), f32[4,5,10,128,128]{4,3,2,1,0:T(8,128)}, u32[]{:S(2)}, u32[]{:S(2)}) %all-to-all-start.2) | async-done | bytes 13107232 | tf_op jit(solution)/shard_map/all_to_all | solution.py:232
  828.7 12.4 %gather_fusion.12 = f32[20,10,128,128]{3,2,1,0:T(8,128)} fusion(f32[20,10,128,128]{3,2,1,0:T(8,128)} %bitcast.86, s32[1024]{0:T(1024)S(1)} %pad_clamp_fusion), kind=kCustom, calls=%fused_computation.12 | custom fusion | bytes 26214480 | tf_op jit(solution)/shard_map/gather | solution.py:234
  841.1 9.3 %add_bitcast_fusion = f32[20,128,10,128]{3,1,2,0:T(8,128)S(1)} fusion(f32[20,10,128,128]{3,2,1,0:T(8,128)} %gather_fusion.12, f32[20,10,128,128]{3,2,1,0:T(8,128)} %gather_fusion.10, pred[20,10]{1,0:T(8,128)(4,1)S(1)} %broadcast_and_fusion, pred[20,10]{1,0:T(8,128)(4,1)S(1)} %broadcast_and_fusion.1), kind=kLoop, calls=%fused_computation.23 | loop fusion | flops 9830400 | bytes 39322000 | tf_op jit(solution)/shard_map/transpose | solution.py:248
  850.4 14.1 %copy.40 = f32[20,128,10,128]{3,2,1,0:T(8,128)} copy(f32[20,128,10,128]{3,1,2,0:T(8,128)S(1)} %add_bitcast_fusion) | data formatting | bytes 26214400 | tf_op jit(solution)/shard_map/reshape | solution.py:248
  867.9 35.1 %fusion.1 = f32[2560,1280]{1,0:T(8,128)} fusion(f32[2560,512]{1,0:T(8,128)} %pad_maximum_fusion.1, f32[1280,512]{1,0:T(8,128)} %all-reduce.5.cloned.1.call-done, f32[320,8,10,128]{3,2,1,0:T(8,128)} %bitcast.255, f32[2560,512]{1,0:T(8,128)} %param.9, f32[1280]{0:T(1024)S(1)} %copy-done.8, s32[1280]{0:T(1024)S(1)} %iota_add_fusion.1, ...), kind=kOutput, calls=%fused_computation.19 | convolution fusion | flops 20162150400 | bytes 39348480 | tf_op jit(solution)/shard_map/dot_general | solution.py:265
  (222 shorter events, 115.3 us)
Async XLA Ops:
  6.5 13.6 %copy-start.5 = (s32[2,48]{1,0:T(2,128)S(1)}, s32[2,48]{1,0:T(2,128)}, u32[]{:S(2)}) copy-start(s32[2,48]{1,0:T(2,128)} %param.7) | copy-start | bytes 1156
  6.5 76.0 %all-gather.7.cloned.1.call-start = ((), (), s32[]{:S(2)}) async-start(), calls=%async_computation.5 | async-start | bytes 2162688 | tf_op jit(solution)/shard_map/all_gather | solution.py:93
  12.7 67.7 %collective-permute-start = (f32[5,128,128]{2,1,0:T(8,128)S(1)}, f32[5,128,128]{2,1,0:T(8,128)S(1)}, u32[]{:S(2)}, u32[]{:S(2)}) collective-permute-start(f32[5,128,128]{2,1,0:T(8,128)S(1)} %get-tuple-element.81), channel_id=1, source_target_pairs={{0,4},{4,8},{8,12},{12,0},{1,5},{5,9},{9,13},{13,1},{2,6},{6,10},{... | collective-permute-start | bytes 983048 | tf_op jit(solution)/shard_map/ppermute | solution.py:152
  15.7 64.7 %collective-permute-start.1 = (f32[5,128,128]{2,1,0:T(8,128)S(1)}, f32[5,128,128]{2,1,0:T(8,128)S(1)}, u32[]{:S(2)}, u32[]{:S(2)}) collective-permute-start(f32[5,128,128]{2,1,0:T(8,128)S(1)} %get-tuple-element.80), channel_id=1, source_target_pairs={{0,8},{4,12},{8,0},{12,4},{1,9},{5,13},{9,1},{13,5},{2,10},{6,14},... | collective-permute-start | bytes 983048 | tf_op jit(solution)/shard_map/ppermute | solution.py:152
  17.2 63.2 %collective-permute-start.2 = (f32[5,128,128]{2,1,0:T(8,128)S(1)}, f32[5,128,128]{2,1,0:T(8,128)S(1)}, u32[]{:S(2)}, u32[]{:S(2)}) collective-permute-start(f32[5,128,128]{2,1,0:T(8,128)S(1)} %get-tuple-element.82), channel_id=1, source_target_pairs={{0,12},{4,0},{8,4},{12,8},{1,13},{5,1},{9,5},{13,9},{2,14},{6,2},{... | collective-permute-start | bytes 983048 | tf_op jit(solution)/shard_map/ppermute | solution.py:152
  20.1 243.5 %all-gather.5.cloned.1.call-start = ((), (), s32[]{:S(2)}) async-start(), calls=%async_computation.3 | async-start | bytes 6553600 | tf_op jit(solution)/shard_map/all_gather | solution.py:163
  20.3 10.9 %copy-start.7 = (f32[1280]{0:T(1024)S(1)}, f32[1280]{0:T(1024)}, u32[]{:S(2)}) copy-start(f32[1280]{0:T(1024)} %param.8) | copy-start | bytes 15364
  55.5 9.6 %copy-start.6 = (s32[2,48]{1,0:T(2,128)S(1)}, s32[2,48]{1,0:T(2,128)}, u32[]{:S(2)}) copy-start(s32[2,48]{1,0:T(2,128)} %param.6) | copy-start | bytes 1156
  80.4 4.8 copy-start.9
  104.8 290.1 %all-to-all-start = ((f32[4,3,1536,128]{3,2,1,0:T(8,128)}), f32[4,3,1536,128]{3,2,1,0:T(8,128)}, u32[]{:S(2)}, u32[]{:S(2)}) async-start(f32[4,3,1536,128]{3,2,1,0:T(8,128)} %get-tuple-element.70), calls=%async_computation | async-start | bytes 18874368 | tf_op jit(solution)/shard_map/all_to_all | solution.py:194
  116.3 242.7 %copy-start.4 = (f32[512,512]{1,0:T(8,128)S(1)}, f32[512,512]{1,0:T(8,128)}, u32[]{:S(2)}) copy-start(f32[512,512]{1,0:T(8,128)} %fusion.18) | copy-start | bytes 3145732
  263.6 99.2 %collective-permute-start.3 = (f32[4,20,128,128]{3,2,1,0:T(8,128)}, f32[4,20,128,128]{3,2,1,0:T(8,128)}, u32[]{:S(2)}, u32[]{:S(2)}) collective-permute-start(f32[4,20,128,128]{3,2,1,0:T(8,128)} %all-gather.5.cloned.1.call-done), channel_id=1, source_target_pairs={{0,16},{16,0},{1,17},{17,1},{2,18},{18,2},{3,19},{19,3},{4,20},{20... | collective-permute-start | bytes 15728648 | tf_op jit(solution)/shard_map/ppermute | solution.py:164
  357.8 5.1 copy-start.1
  375.8 15.1 %slice-start = ((s8[5242880]{0:T(1024)(128)(4,1)}), s8[1048576]{0:T(1024)(128)(4,1)S(1)}, s32[]{:S(2)}) async-start(s8[5242880]{0:T(1024)(128)(4,1)} %bitcast.259), calls=%async_computation.6 | async-start | bytes 2097152
  381.5 9.3 %slice-start.1 = ((s8[5242880]{0:T(1024)(128)(4,1)}), s8[4194304]{0:T(1024)(128)(4,1)S(1)}, s32[]{:S(2)}) async-start(s8[5242880]{0:T(1024)(128)(4,1)} %bitcast.259), calls=%async_computation.7 | async-start | bytes 8388608
  390.8 4.7 copy-start.12
  390.9 4.6 copy-start.13
  390.9 4.9 copy-start.11
  394.9 15.1 %collective-permute-start.4 = (f32[4,3,1536,128]{3,2,1,0:T(8,128)}, f32[4,3,1536,128]{3,2,1,0:T(8,128)}, u32[]{:S(2)}, u32[]{:S(2)}) collective-permute-start(f32[4,3,1536,128]{3,2,1,0:T(8,128)} %all-to-all-done), channel_id=1, source_target_pairs={{0,16},{16,0},{1,17},{17,1},{2,18},{18,2},{3,19},{19,3},{4,20},{20... | collective-permute-start | bytes 28311560 | tf_op jit(solution)/shard_map/ppermute | solution.py:198
  427.8 212.3 %all-to-all-start.1 = ((f32[4,3,1536,128]{3,2,1,0:T(8,128)}), f32[4,3,1536,128]{3,2,1,0:T(8,128)}, u32[]{:S(2)}, u32[]{:S(2)}) async-start(f32[4,3,1536,128]{3,2,1,0:T(8,128)} %get-tuple-element.25), calls=%async_computation.1 | async-start | bytes 18874368 | tf_op jit(solution)/shard_map/all_to_all | solution.py:241
  442.9 75.4 %collective-permute-start.5 = (f32[5,10,128,128]{3,2,1,0:T(8,128)}, f32[5,10,128,128]{3,2,1,0:T(8,128)}, u32[]{:S(2)}, u32[]{:S(2)}) collective-permute-start(f32[5,10,128,128]{3,2,1,0:T(8,128)} %get-tuple-element.74), channel_id=1, source_target_pairs={{0,4},{4,8},{8,12},{12,0},{1,5},{5,9},{9,13},{13,1},{2,6},{6,10},{... | collective-permute-start | bytes 9830408 | tf_op jit(solution)/shard_map/ppermute | solution.py:227
  444.9 143.3 %collective-permute-start.6 = (f32[5,10,128,128]{3,2,1,0:T(8,128)}, f32[5,10,128,128]{3,2,1,0:T(8,128)}, u32[]{:S(2)}, u32[]{:S(2)}) collective-permute-start(f32[5,10,128,128]{3,2,1,0:T(8,128)} %get-tuple-element.73), channel_id=1, source_target_pairs={{0,8},{4,12},{8,0},{12,4},{1,9},{5,13},{9,1},{13,5},{2,10},{6,14},... | collective-permute-start | bytes 9830408 | tf_op jit(solution)/shard_map/ppermute | solution.py:227
  446.8 141.4 %collective-permute-start.7 = (f32[5,10,128,128]{3,2,1,0:T(8,128)}, f32[5,10,128,128]{3,2,1,0:T(8,128)}, u32[]{:S(2)}, u32[]{:S(2)}) collective-permute-start(f32[5,10,128,128]{3,2,1,0:T(8,128)} %get-tuple-element.72), channel_id=1, source_target_pairs={{0,12},{4,0},{8,4},{12,8},{1,13},{5,1},{9,5},{13,9},{2,14},{6,2},{... | collective-permute-start | bytes 9830408 | tf_op jit(solution)/shard_map/ppermute | solution.py:227
  657.8 6.7 copy-start.10
  657.8 6.9 copy-start.2
  657.8 170.8 %all-to-all-start.2 = ((f32[4,5,10,128,128]{4,3,2,1,0:T(8,128)}), f32[4,5,10,128,128]{4,3,2,1,0:T(8,128)}, u32[]{:S(2)}, u32[]{:S(2)}) async-start(f32[4,5,10,128,128]{4,3,2,1,0:T(8,128)} %bitcast.250), calls=%async_computation.2 | async-start | bytes 26214400 | tf_op jit(solution)/shard_map/all_to_all | solution.py:232
  664.4 203.6 %all-reduce.5.cloned.1.call-start = ((), (), s32[]{:S(2)}) async-start(), calls=%async_computation.4 | async-start | bytes 5242880 | tf_op jit(solution)/shard_map/psum | solution.py:13
  675.3 1.2 copy-start.3
  676.5 2.1 copy-start
  850.4 17.6 %copy-start.8 = (f32[1280]{0:T(1024)S(1)}, f32[1280]{0:T(1024)}, u32[]{:S(2)}) copy-start(f32[1280]{0:T(1024)} %param.8) | copy-start | bytes 15364
Sparse Core Ops, SparseCore 0:
  20.2 56.4 all-gather.6
  82.6 180.9 all-gather.4
  681.0 186.8 all-reduce.4

commit v10 on v9

--- a/solution.py
+++ b/solution.py
@@ -136,7 +136,7 @@
     my_rows_map = lax.dynamic_index_in_dim(row_map, my_sub, 0, keepdims=False)
     my_cols_map = lax.dynamic_index_in_dim(col_map, my_sub, 0, keepdims=False)
 
-    full_diagonal = lax.all_gather(own_diagonal, ("sub", "col"), tiled=True)
+    full_diagonal = from_root(own_diagonal[:PANEL], ("sub", "col"), 0)
     corner = early_corner(child_piece, row_map, col_map, full_diagonal)
     global_row = my_row * front_rows + jnp.arange(front_rows, dtype=jnp.int32)
 

time: 918 us -> 913 us (level)
    all_gather x1 -> x0, blocking collectives: 23.9 us -> none  [shards(): full_diagonal = lax.all_gather(own_diagonal, ('sub', 'col'), tiled=True)]
    psum x0 -> x1, blocking collectives: none -> 16 us  [from_root(): return lax.psum(kept, axis)]
  transfers between devices with their start and end apart: 14 -> 14, of which waited for: 7 -> 8; matrix products, arithmetic and copies ran while one was open for 36% -> 36% of each run, Pallas kernels for 0% -> 0%
where the time goes in v10:
time: 913 us; the launch traced here: 905 us
  waiting for transfers between devices  436 us (48%)
  other arithmetic  184 us (20%)
  local copies, waits for them, and re-layouts  172 us (19%)
  matrix products  51.5 us (6%)
  starting transfers between devices  29.2 us (3%)
  between operations  17.1 us (2%)
  blocking collectives  16 us (2%)
    all_to_all x1, waiting for transfers between devices, row_receiving(): lax.all_to_all(sending, 'row', split_axis=0, concat_axis=0, tiled=True)  142 us
    ppermute x3, waiting for transfers between devices, row_receiving(): pieces.append(lax.ppermute(piece, 'row', pairs))  140 us
    all_gather x1, waiting for transfers between devices, shards(): cands = lax.all_gather(cand_rows, 'col')  104 us
    another operation x15, other arithmetic, factor_corner(): lower = jnp.linalg.cholesky(symmetric_of(corner))  81.7 us
    another operation x4, other arithmetic, factor_corner(): jax.scipy.linalg.solve_triangular(lower, jnp.eye(PANEL, dtype=jnp.float32...  43 us
    gather x2, local copies, waits for them, and re-layouts, row_sending(): half.at[col_index[None, None, :], row_index[:, :, None]]  35.4 us
    dot_general x1, matrix products, shards(): lax.dot_general(own_rows, theirs, (((1,), (1,)), ((), ())), precision=lax...  35.1 us
    all_to_all x1, waiting for transfers between devices, shards(): lax.all_to_all(own_outgoing, 'col', split_axis=0, concat_axis=0, tiled=True)  31.1 us
  transfers between devices with their start and end apart: 14, of which 8 were waited for; matrix products, arithmetic and copies ran while one was open for 36% of the time, Pallas kernels for 0%

profile of v10, /device:TPU:0, one launch (start us, length us, event | category | flops | bytes accessed | tf_op | source)
XLA Modules:
  0.0 905.0 jit_solution(8861360175937246031)
XLA Ops:
  20.5 9.6 %copy.32 = f32[1,1536,1536]{1,2,0:T(8,128)} copy(f32[1,1536,1536]{2,1,0:T(8,128)} %param.5) | data formatting | bytes 18874368 | tf_op args[0]
  31.6 9.6 %copy.33 = f32[1536,12,128]{2,0,1:T(8,128)} copy(f32[1536,12,128]{0,2,1:T(8,128)} %bitcast.252) | data formatting | bytes 18874368 | tf_op jit(solution)/shard_map/reshape;squeeze | solution.py:186
  42.9 13.2 %gather_fusion = f32[24,1536,128]{2,1,0:T(8,128)} fusion(f32[1536,12,128]{2,0,1:T(8,128)} %copy.33, s32[1024]{0:T(1024)S(1)} %pad_clamp_fusion.7), kind=kCustom, calls=%fused_computation | custom fusion | bytes 37748832 | tf_op jit(solution)/shard_map/gather | solution.py:190
  56.7 16.0 %psum.14 = f32[512]{0:T(512)S(1)} all-reduce(f32[512]{0:T(512)S(1)} %slice_select_fusion.1), channel_id=1, replica_groups=mesh['sub'=2,'row'=4,'col'=4] {'sub','col'}, use_global_device_ids=true, to_apply=%region_5.6 | all-reduce | flops 512 | bytes 4096 | tf_op jit(solution)/shard_map/psum | solution.py:13
  85.2 14.0 %slice_bitcast_fusion = (f32[4,3,1536,128]{3,2,1,0:T(8,128)}, f32[4,3,1536,128]{3,2,1,0:T(8,128)}) fusion(f32[2,4,3,1536,128]{4,3,2,1,0:T(8,128)} %bitcast.248), kind=kLoop, calls=%fused_computation.28 | loop fusion | bytes 37748736 | tf_op jit(solution)/shard_map/squeeze | solution.py:239
  110.7 11.7 %cholesky.103 = f32[128,128]{1,0:T(8,128)S(1)} custom-call(f32[128,128]{1,0:T(8,128)S(1)} %cholesky.263), custom_call_target="Cholesky" | custom-call | tf_op jit(solution)/shard_map/jit(cholesky)/cholesky | solution.py:71
  123.1 9.8 %custom-call.31 = f32[1,128,128]{1,2,0:T(8,128)S(1)} custom-call(f32[1,128,128]{2,1,0:T(8,128)S(1)} %get-tuple-element.92), custom_call_target="InvertDiagBlocksLowerTriangular" | custom-call | tf_op jit(solution)/shard_map/jit(cholesky)/cholesky | solution.py:71
  133.6 11.7 %cholesky.215 = f32[128,128]{1,0:T(8,128)S(1)} custom-call(f32[128,128]{1,0:T(8,128)S(1)} %cholesky.267), custom_call_target="Cholesky" | custom-call | tf_op jit(solution)/shard_map/jit(cholesky)/cholesky | solution.py:71
  145.9 9.9 %custom-call.32 = f32[1,128,128]{1,2,0:T(8,128)S(1)} custom-call(f32[1,128,128]{2,1,0:T(8,128)S(1)} %get-tuple-element.89), custom_call_target="InvertDiagBlocksLowerTriangular" | custom-call | tf_op jit(solution)/shard_map/jit(cholesky)/cholesky | solution.py:71
  155.8 103.5 %all-gather.4.cloned.1.call-done = f32[4,20,128,128]{3,2,1,0:T(8,128)} async-done(((f32[1,20,128,128]{3,2,1,0:T(8,128)}), f32[4,20,128,128]{3,2,1,0:T(8,128)}) %all-gather.4.cloned.1.call-update) | async-done | bytes 5242896 | tf_op jit(solution)/shard_map/all_gather | solution.py:163
  260.0 11.7 %cholesky.236 = f32[128,128]{1,0:T(8,128)S(1)} custom-call(f32[128,128]{1,0:T(8,128)S(1)} %cholesky.272), custom_call_target="Cholesky" | custom-call | tf_op jit(solution)/shard_map/jit(cholesky)/cholesky | solution.py:71
  271.8 9.8 %custom-call.33 = f32[1,128,128]{1,2,0:T(8,128)S(1)} custom-call(f32[1,128,128]{2,1,0:T(8,128)S(1)} %get-tuple-element.86), custom_call_target="InvertDiagBlocksLowerTriangular" | custom-call | tf_op jit(solution)/shard_map/jit(cholesky)/cholesky | solution.py:71
  282.2 11.9 %cholesky.253 = f32[128,128]{1,0:T(8,128)S(1)} custom-call(f32[128,128]{1,0:T(8,128)S(1)} %convolution_subtract_fusion.6), custom_call_target="Cholesky" | custom-call | tf_op jit(solution)/shard_map/jit(cholesky)/cholesky | solution.py:71
  302.6 10.8 %while.1 = (s32[]{:T(128)}, f32[512,512]{1,0:T(8,128)S(1)}, s32[4,2]{0,1:T(2,128)S(1)}, f32[4,128,128]{2,1,0:T(8,128)}, s32[]{:T(128)}) while((s32[]{:T(128)}, f32[512,512]{1,0:T(8,128)S(1)}, s32[4,2]{0,1:T(2,128)S(1)}, f32[4,128,128]{2,1,0:T(8,128)}, s32[]{:T(128)}) %tuple.85), condition=%wide.while_cond, body=%wide.while_body.sunk | while | flops 2 | bytes 132705 | solution.py:72
  313.3 40.1 %custom-call.34 = f32[4,128,128]{1,2,0:T(8,128)S(1)} custom-call(f32[4,128,128]{2,1,0:T(8,128)} %get-tuple-element.36), custom_call_target="InvertDiagBlocksLowerTriangular" | custom-call | tf_op jit(solution)/shard_map/jit(_solve_triangular)/triangular_solve | solution.py:72
  358.5 7.2 fusion.6
  391.8 14.0 %collective-permute-done.4 = f32[4,3,1536,128]{3,2,1,0:T(8,128)} collective-permute-done((f32[4,3,1536,128]{3,2,1,0:T(8,128)}, f32[4,3,1536,128]{3,2,1,0:T(8,128)}, u32[]{:S(2)}, u32[]{:S(2)}) %collective-permute-start.4) | collective-permute-done | bytes 9437216 | tf_op jit(solution)/shard_map/ppermute | solution.py:198
  405.8 17.7 %gather_fusion.9 = f32[200,128,128]{2,1,0:T(8,128)} fusion(f32[12,12,128,128]{3,2,1,0:T(8,128)} %bitcast.65, s32[200]{0:T(256)S(1)} %reshape.928), kind=kCustom, calls=%fused_computation.9 | custom fusion | bytes 26216000 | tf_op jit(solution)/shard_map/gather | solution.py:211
  429.4 9.2 %constant_dynamic-slice_fusion.1 = (f32[1,5,10,128,128]{4,3,2,1,0:T(8,128)S(1)}, f32[5,10,128,128]{3,2,1,0:T(8,128)}, f32[5,10,128,128]{3,2,1,0:T(8,128)}, f32[5,10,128,128]{3,2,1,0:T(8,128)}) fusion(f32[4,5,10,128,128]{4,3,2,1,0:T(8,128)} %bitcast.250, s32[]{:T(128)S(6)} %select_n.717, s32[]{:T(128)S(6)} %select_n.723, s32[]{:T(128)S(6)} %select_n.721, ...), kind=kLoop, calls=%fused_computation.165 | loop fusion | bytes 26214416 | tf_op jit(solution)/shard_map/jit(dynamic_index_in_dim)/dynamic_slice | solution.py:223
  443.4 70.3 %collective-permute-done.5 = f32[5,10,128,128]{3,2,1,0:T(8,128)} collective-permute-done((f32[5,10,128,128]{3,2,1,0:T(8,128)}, f32[5,10,128,128]{3,2,1,0:T(8,128)}, u32[]{:S(2)}, u32[]{:S(2)}) %collective-permute-start.5) | collective-permute-done | bytes 3276832 | tf_op jit(solution)/shard_map/ppermute | solution.py:227
  513.7 69.6 %collective-permute-done.6 = f32[5,10,128,128]{3,2,1,0:T(8,128)} collective-permute-done((f32[5,10,128,128]{3,2,1,0:T(8,128)}, f32[5,10,128,128]{3,2,1,0:T(8,128)}, u32[]{:S(2)}, u32[]{:S(2)}) %collective-permute-start.6) | collective-permute-done | bytes 3276832 | tf_op jit(solution)/shard_map/ppermute | solution.py:227
  583.3 9.0 pad_maximum_fusion
  592.2 12.5 %gather_fusion.10 = f32[20,10,128,128]{3,2,1,0:T(8,128)} fusion(f32[20,10,128,128]{3,2,1,0:T(8,128)} %bitcast.251, s32[1024]{0:T(1024)S(1)} %pad_clamp_fusion.1), kind=kCustom, calls=%fused_computation.10 | custom fusion | bytes 26214480 | tf_op jit(solution)/shard_map/gather | solution.py:234
  604.7 31.1 %all-to-all-done.1 = f32[4,3,1536,128]{3,2,1,0:T(8,128)} async-done(((f32[4,3,1536,128]{3,2,1,0:T(8,128)}), f32[4,3,1536,128]{3,2,1,0:T(8,128)}, u32[]{:S(2)}, u32[]{:S(2)}) %all-to-all-start.1) | async-done | bytes 9437216 | tf_op jit(solution)/shard_map/all_to_all | solution.py:241
  635.8 17.7 %gather_fusion.11 = f32[200,128,128]{2,1,0:T(8,128)} fusion(f32[12,12,128,128]{3,2,1,0:T(8,128)} %bitcast.83, s32[200]{0:T(256)S(1)} %reshape.942), kind=kCustom, calls=%fused_computation.11 | custom fusion | bytes 26216000 | tf_op jit(solution)/shard_map/gather | solution.py:211
  653.5 6.5 all-to-all-start.2
  660.4 10.6 %fusion.99 = f32[2560,512]{1,0:T(8,128)S(1)} fusion(f32[2560,512]{1,0:T(8,128)} %fusion.7, f32[512,512]{1,0:T(8,128)S(1)} %copy-done.2), kind=kOutput, calls=%fused_computation.328 | convolution fusion | flops 8053063680 | bytes 11534336 | tf_op jit(solution)/shard_map/dot_general | solution.py:79
  681.6 142.4 %all-to-all-done.2 = f32[4,5,10,128,128]{4,3,2,1,0:T(8,128)} async-done(((f32[4,5,10,128,128]{4,3,2,1,0:T(8,128)}), f32[4,5,10,128,128]{4,3,2,1,0:T(8,128)}, u32[]{:S(2)}, u32[]{:S(2)}) %all-to-all-start.2) | async-done | bytes 13107232 | tf_op jit(solution)/shard_map/all_to_all | solution.py:232
  824.0 12.4 %gather_fusion.12 = f32[20,10,128,128]{3,2,1,0:T(8,128)} fusion(f32[20,10,128,128]{3,2,1,0:T(8,128)} %bitcast.85, s32[1024]{0:T(1024)S(1)} %pad_clamp_fusion), kind=kCustom, calls=%fused_computation.12 | custom fusion | bytes 26214480 | tf_op jit(solution)/shard_map/gather | solution.py:234
  836.5 9.3 %add_bitcast_fusion = f32[20,128,10,128]{3,1,2,0:T(8,128)S(1)} fusion(f32[20,10,128,128]{3,2,1,0:T(8,128)} %gather_fusion.12, f32[20,10,128,128]{3,2,1,0:T(8,128)} %gather_fusion.10, pred[20,10]{1,0:T(8,128)(4,1)S(1)} %broadcast_and_fusion, pred[20,10]{1,0:T(8,128)(4,1)S(1)} %broadcast_and_fusion.1), kind=kLoop, calls=%fused_computation.23 | loop fusion | flops 9830400 | bytes 39322000 | tf_op jit(solution)/shard_map/transpose | solution.py:248
  845.8 14.1 %copy.40 = f32[20,128,10,128]{3,2,1,0:T(8,128)} copy(f32[20,128,10,128]{3,1,2,0:T(8,128)S(1)} %add_bitcast_fusion) | data formatting | bytes 26214400 | tf_op jit(solution)/shard_map/reshape | solution.py:248
  862.9 35.1 %fusion.1 = f32[2560,1280]{1,0:T(8,128)} fusion(f32[2560,512]{1,0:T(8,128)} %pad_maximum_fusion.1, f32[1280,512]{1,0:T(8,128)} %all-reduce.5.cloned.1.call-done, f32[320,8,10,128]{3,2,1,0:T(8,128)} %bitcast.254, f32[2560,512]{1,0:T(8,128)} %param.9, f32[1280]{0:T(1024)S(1)} %copy-done.11, s32[1280]{0:T(1024)S(1)} %iota_add_fusion.1, ...), kind=kOutput, calls=%fused_computation.19 | convolution fusion | flops 20162150400 | bytes 39348480 | tf_op jit(solution)/shard_map/dot_general | solution.py:265
  (219 shorter events, 116.5 us)
Async XLA Ops:
  6.5 13.6 %copy-start.5 = (s32[2,48]{1,0:T(2,128)S(1)}, s32[2,48]{1,0:T(2,128)}, u32[]{:S(2)}) copy-start(s32[2,48]{1,0:T(2,128)} %param.7) | copy-start | bytes 1156
  6.5 70.2 %all-gather.6.cloned.1.call-start = ((), (), s32[]{:S(2)}) async-start(), calls=%async_computation.5 | async-start | bytes 2162688 | tf_op jit(solution)/shard_map/all_gather | solution.py:93
  12.7 60.3 %collective-permute-start = (f32[5,128,128]{2,1,0:T(8,128)S(1)}, f32[5,128,128]{2,1,0:T(8,128)S(1)}, u32[]{:S(2)}, u32[]{:S(2)}) collective-permute-start(f32[5,128,128]{2,1,0:T(8,128)S(1)} %get-tuple-element.81), channel_id=1, source_target_pairs={{0,4},{4,8},{8,12},{12,0},{1,5},{5,9},{9,13},{13,1},{2,6},{6,10},{... | collective-permute-start | bytes 983048 | tf_op jit(solution)/shard_map/ppermute | solution.py:152
  15.7 57.4 %collective-permute-start.1 = (f32[5,128,128]{2,1,0:T(8,128)S(1)}, f32[5,128,128]{2,1,0:T(8,128)S(1)}, u32[]{:S(2)}, u32[]{:S(2)}) collective-permute-start(f32[5,128,128]{2,1,0:T(8,128)S(1)} %get-tuple-element.80), channel_id=1, source_target_pairs={{0,8},{4,12},{8,0},{12,4},{1,9},{5,13},{9,1},{13,5},{2,10},{6,14},... | collective-permute-start | bytes 983048 | tf_op jit(solution)/shard_map/ppermute | solution.py:152
  17.2 55.8 %collective-permute-start.2 = (f32[5,128,128]{2,1,0:T(8,128)S(1)}, f32[5,128,128]{2,1,0:T(8,128)S(1)}, u32[]{:S(2)}, u32[]{:S(2)}) collective-permute-start(f32[5,128,128]{2,1,0:T(8,128)S(1)} %get-tuple-element.82), channel_id=1, source_target_pairs={{0,12},{4,0},{8,4},{12,8},{1,13},{5,1},{9,5},{13,9},{2,14},{6,2},{... | collective-permute-start | bytes 983048 | tf_op jit(solution)/shard_map/ppermute | solution.py:152
  20.1 239.2 %all-gather.4.cloned.1.call-start = ((), (), s32[]{:S(2)}) async-start(), calls=%async_computation.3 | async-start | bytes 6553600 | tf_op jit(solution)/shard_map/all_gather | solution.py:163
  31.6 9.6 %copy-start.6 = (s32[2,48]{1,0:T(2,128)S(1)}, s32[2,48]{1,0:T(2,128)}, u32[]{:S(2)}) copy-start(s32[2,48]{1,0:T(2,128)} %param.6) | copy-start | bytes 1156
  73.0 6.4 copy-start.7
  99.2 291.4 %all-to-all-start = ((f32[4,3,1536,128]{3,2,1,0:T(8,128)}), f32[4,3,1536,128]{3,2,1,0:T(8,128)}, u32[]{:S(2)}, u32[]{:S(2)}) async-start(f32[4,3,1536,128]{3,2,1,0:T(8,128)} %get-tuple-element.70), calls=%async_computation | async-start | bytes 18874368 | tf_op jit(solution)/shard_map/all_to_all | solution.py:194
  110.7 244.0 %copy-start.4 = (f32[512,512]{1,0:T(8,128)S(1)}, f32[512,512]{1,0:T(8,128)}, u32[]{:S(2)}) copy-start(f32[512,512]{1,0:T(8,128)} %fusion.18) | copy-start | bytes 3145732
  259.4 99.2 %collective-permute-start.3 = (f32[4,20,128,128]{3,2,1,0:T(8,128)}, f32[4,20,128,128]{3,2,1,0:T(8,128)}, u32[]{:S(2)}, u32[]{:S(2)}) collective-permute-start(f32[4,20,128,128]{3,2,1,0:T(8,128)} %all-gather.4.cloned.1.call-done), channel_id=1, source_target_pairs={{0,16},{16,0},{1,17},{17,1},{2,18},{18,2},{3,19},{19,3},{4,20},{20... | collective-permute-start | bytes 15728648 | tf_op jit(solution)/shard_map/ppermute | solution.py:164
  353.5 5.1 copy-start.1
  371.5 15.1 %slice-start = ((s8[5242880]{0:T(1024)(128)(4,1)}), s8[1048576]{0:T(1024)(128)(4,1)S(1)}, s32[]{:S(2)}) async-start(s8[5242880]{0:T(1024)(128)(4,1)} %bitcast.258), calls=%async_computation.6 | async-start | bytes 2097152
  377.2 9.3 %slice-start.1 = ((s8[5242880]{0:T(1024)(128)(4,1)}), s8[4194304]{0:T(1024)(128)(4,1)S(1)}, s32[]{:S(2)}) async-start(s8[5242880]{0:T(1024)(128)(4,1)} %bitcast.258), calls=%async_computation.7 | async-start | bytes 8388608
  386.6 4.6 copy-start.10
  386.6 4.6 copy-start.12
  386.6 4.9 copy-start.9
  390.6 15.1 %collective-permute-start.4 = (f32[4,3,1536,128]{3,2,1,0:T(8,128)}, f32[4,3,1536,128]{3,2,1,0:T(8,128)}, u32[]{:S(2)}, u32[]{:S(2)}) collective-permute-start(f32[4,3,1536,128]{3,2,1,0:T(8,128)} %all-to-all-done), channel_id=1, source_target_pairs={{0,16},{16,0},{1,17},{17,1},{2,18},{18,2},{3,19},{19,3},{4,20},{20... | collective-permute-start | bytes 28311560 | tf_op jit(solution)/shard_map/ppermute | solution.py:198
  423.5 212.3 %all-to-all-start.1 = ((f32[4,3,1536,128]{3,2,1,0:T(8,128)}), f32[4,3,1536,128]{3,2,1,0:T(8,128)}, u32[]{:S(2)}, u32[]{:S(2)}) async-start(f32[4,3,1536,128]{3,2,1,0:T(8,128)} %get-tuple-element.25), calls=%async_computation.1 | async-start | bytes 18874368 | tf_op jit(solution)/shard_map/all_to_all | solution.py:241
  438.7 75.0 %collective-permute-start.5 = (f32[5,10,128,128]{3,2,1,0:T(8,128)}, f32[5,10,128,128]{3,2,1,0:T(8,128)}, u32[]{:S(2)}, u32[]{:S(2)}) collective-permute-start(f32[5,10,128,128]{3,2,1,0:T(8,128)} %get-tuple-element.74), channel_id=1, source_target_pairs={{0,4},{4,8},{8,12},{12,0},{1,5},{5,9},{9,13},{13,1},{2,6},{6,10},{... | collective-permute-start | bytes 9830408 | tf_op jit(solution)/shard_map/ppermute | solution.py:227
  440.1 143.2 %collective-permute-start.6 = (f32[5,10,128,128]{3,2,1,0:T(8,128)}, f32[5,10,128,128]{3,2,1,0:T(8,128)}, u32[]{:S(2)}, u32[]{:S(2)}) collective-permute-start(f32[5,10,128,128]{3,2,1,0:T(8,128)} %get-tuple-element.73), channel_id=1, source_target_pairs={{0,8},{4,12},{8,0},{12,4},{1,9},{5,13},{9,1},{13,5},{2,10},{6,14},... | collective-permute-start | bytes 9830408 | tf_op jit(solution)/shard_map/ppermute | solution.py:227
  441.9 141.4 %collective-permute-start.7 = (f32[5,10,128,128]{3,2,1,0:T(8,128)}, f32[5,10,128,128]{3,2,1,0:T(8,128)}, u32[]{:S(2)}, u32[]{:S(2)}) collective-permute-start(f32[5,10,128,128]{3,2,1,0:T(8,128)} %get-tuple-element.72), channel_id=1, source_target_pairs={{0,12},{4,0},{8,4},{12,8},{1,13},{5,1},{9,5},{13,9},{2,14},{6,2},{... | collective-permute-start | bytes 9830408 | tf_op jit(solution)/shard_map/ppermute | solution.py:227
  653.5 6.7 copy-start.8
  653.5 6.9 copy-start.2
  653.5 170.6 %all-to-all-start.2 = ((f32[4,5,10,128,128]{4,3,2,1,0:T(8,128)}), f32[4,5,10,128,128]{4,3,2,1,0:T(8,128)}, u32[]{:S(2)}, u32[]{:S(2)}) async-start(f32[4,5,10,128,128]{4,3,2,1,0:T(8,128)} %bitcast.249), calls=%async_computation.2 | async-start | bytes 26214400 | tf_op jit(solution)/shard_map/all_to_all | solution.py:232
  660.0 202.8 %all-reduce.5.cloned.1.call-start = ((), (), s32[]{:S(2)}) async-start(), calls=%async_computation.4 | async-start | bytes 5242880 | tf_op jit(solution)/shard_map/psum | solution.py:13
  671.0 1.2 copy-start.3
  672.2 2.1 copy-start
  845.8 17.1 %copy-start.11 = (f32[1280]{0:T(1024)S(1)}, f32[1280]{0:T(1024)}, u32[]{:S(2)}) copy-start(f32[1280]{0:T(1024)} %param.8) | copy-start | bytes 15364
Sparse Core Ops, SparseCore 0:
  20.2 56.5 all-gather.5
  78.3 180.9 all-gather.3
  676.7 186.1 all-reduce.4

commit v11 on v10

--- a/solution.py
+++ b/solution.py
@@ -240,21 +240,6 @@
     part_other, keep_other = row_receiving(sending_other, col_valid_other, rows_other, True)
     own_half = lax.all_to_all(own_outgoing, "col", split_axis=0, concat_axis=0, tiled=True)
     own_half, part_other = lax.optimization_barrier((own_half, part_other))
-    sending_own, col_valid_own, rows_own = row_sending(own_half, my_sub)
-    part_own, keep_own = row_receiving(sending_own, col_valid_own, rows_own, False)
-    assembled = jnp.where(keep_other[:, :, None, None], part_other, 0.0) + jnp.where(
-        keep_own[:, :, None, None], part_own, 0.0
-    )
-    assembled = assembled.transpose(0, 2, 1, 3).reshape(front_rows, front_cols)
-
-    global_col = my_group * front_cols + jnp.arange(front_cols, dtype=jnp.int32)
-    on_diagonal = global_row[:, None] == global_col[None, :]
-    assembled = assembled + jnp.where(on_diagonal, own_diagonal[None, :], 0.0)
-    coupling_wide = jnp.concatenate(
-        [coupling, jnp.zeros((front_rows, front_cols - PANEL), jnp.float32)], axis=1
-    )
-    coupling_mask = (global_row[:, None] >= PANEL) & (global_col[None, :] < PANEL)
-    front_part = assembled + jnp.where(coupling_mask, coupling_wide, 0.0)
     theirs_start = my_group * front_cols % front_rows
     theirs_root = my_group * front_cols // front_rows
     own_rows = apply_inverse(panel_rows, inverse)
@@ -265,6 +250,22 @@
     update = lax.dot_general(
         own_rows, theirs, (((1,), (1,)), ((), ())), precision=lax.Precision.HIGHEST
     )
+    sending_own, col_valid_own, rows_own = row_sending(own_half, my_sub)
+    sending_own, update = lax.optimization_barrier((sending_own, update))
+    part_own, keep_own = row_receiving(sending_own, col_valid_own, rows_own, False)
+    assembled = jnp.where(keep_other[:, :, None, None], part_other, 0.0) + jnp.where(
+        keep_own[:, :, None, None], part_own, 0.0
+    )
+    assembled = assembled.transpose(0, 2, 1, 3).reshape(front_rows, front_cols)
+
+    global_col = my_group * front_cols + jnp.arange(front_cols, dtype=jnp.int32)
+    on_diagonal = global_row[:, None] == global_col[None, :]
+    assembled = assembled + jnp.where(on_diagonal, own_diagonal[None, :], 0.0)
+    coupling_wide = jnp.concatenate(
+        [coupling, jnp.zeros((front_rows, front_cols - PANEL), jnp.float32)], axis=1
+    )
+    coupling_mask = (global_row[:, None] >= PANEL) & (global_col[None, :] < PANEL)
+    front_part = assembled + jnp.where(coupling_mask, coupling_wide, 0.0)
     panel_wide = jnp.concatenate(
         [own_rows, jnp.zeros((front_rows, front_cols - PANEL), jnp.float32)], axis=1
     )

time: 913 us -> 945 us (1.035)
  other arithmetic: 184 us -> 203 us
  waiting for transfers between devices: 436 us -> 452 us
    psum x1, waiting for transfers between devices: 2.94 us -> 199 us  [from_root(): return lax.psum(kept, axis)]
    ppermute x3, waiting for transfers between devices: 140 us -> 0.01 us  [row_receiving(): pieces.append(lax.ppermute(piece, 'row', pairs))]
    all_to_all x1, waiting for transfers between devices: 31.1 us -> 0.01 us  [shards(): lax.all_to_all(own_outgoing, 'col', split_axis=0, concat_axis=0, tiled=True)]
    select_n x0 -> x1, other arithmetic: none -> 14.5 us  [shards(): jnp.where(global_col[None, :] < PANEL, panel_wide, jnp.where(global_row[:...]
  transfers between devices with their start and end apart: 14 -> 14, of which waited for: 8 -> 4; matrix products, arithmetic and copies ran while one was open for 36% -> 35% of each run, Pallas kernels for 0% -> 0%
where the time goes in v11:
time: 945 us; the launch traced here: 936 us
  waiting for transfers between devices  452 us (48%)
  other arithmetic  203 us (21%)
  local copies, waits for them, and re-layouts  175 us (19%)
  matrix products  45.6 us (5%)
  starting transfers between devices  28 us (3%)
  between operations  16.8 us (2%)
  blocking collectives  15.9 us (2%)
    psum x1, waiting for transfers between devices, from_root(): return lax.psum(kept, axis)  199 us
    all_to_all x1, waiting for transfers between devices, row_receiving(): lax.all_to_all(sending, 'row', split_axis=0, concat_axis=0, tiled=True)  138 us
    all_gather x1, waiting for transfers between devices, shards(): cands = lax.all_gather(cand_rows, 'col')  101 us
    another operation x15, other arithmetic, factor_corner(): lower = jnp.linalg.cholesky(symmetric_of(corner))  82 us
    another operation x4, other arithmetic, factor_corner(): jax.scipy.linalg.solve_triangular(lower, jnp.eye(PANEL, dtype=jnp.float32...  42 us
    gather x2, local copies, waits for them, and re-layouts, row_sending(): half.at[col_index[None, None, :], row_index[:, :, None]]  35.4 us
    dot_general x1, matrix products, shards(): lax.dot_general(own_rows, theirs, (((1,), (1,)), ((), ())), precision=lax...  26.4 us
    gather x2, local copies, waits for them, and re-layouts, row_receiving(): part = received.at[placement].get(mode='promise_in_bounds')  24.7 us
  transfers between devices with their start and end apart: 14, of which 4 were waited for; matrix products, arithmetic and copies ran while one was open for 35% of the time, Pallas kernels for 0%

profile of v11, /device:TPU:0, one launch (start us, length us, event | category | flops | bytes accessed | tf_op | source)
XLA Modules:
  0.0 936.1 jit_solution(12211749659704077414)
XLA Ops:
  19.5 9.6 %copy.32 = f32[1,1536,1536]{1,2,0:T(8,128)} copy(f32[1,1536,1536]{2,1,0:T(8,128)} %param.5) | data formatting | bytes 18874368 | tf_op args[0]
  29.1 9.7 %copy.33 = f32[1536,12,128]{2,0,1:T(8,128)} copy(f32[1536,12,128]{0,2,1:T(8,128)} %bitcast.256) | data formatting | bytes 18874368 | tf_op jit(solution)/shard_map/reshape;squeeze | solution.py:186
  41.9 13.3 %gather_fusion = f32[24,1536,128]{2,1,0:T(8,128)} fusion(f32[1536,12,128]{2,0,1:T(8,128)} %copy.33, s32[1024]{0:T(1024)S(1)} %pad_clamp_fusion.7), kind=kCustom, calls=%fused_computation | custom fusion | bytes 37748832 | tf_op jit(solution)/shard_map/gather | solution.py:190
  56.0 15.9 %psum.14 = f32[512]{0:T(512)S(1)} all-reduce(f32[512]{0:T(512)S(1)} %slice_select_fusion.1), channel_id=1, replica_groups=mesh['sub'=2,'row'=4,'col'=4] {'sub','col'}, use_global_device_ids=true, to_apply=%region_5.6 | all-reduce | flops 512 | bytes 4096 | tf_op jit(solution)/shard_map/psum | solution.py:13
  82.7 13.8 %slice_bitcast_fusion = (f32[4,3,1536,128]{3,2,1,0:T(8,128)}, f32[4,3,1536,128]{3,2,1,0:T(8,128)}) fusion(f32[2,4,3,1536,128]{4,3,2,1,0:T(8,128)} %bitcast.252), kind=kLoop, calls=%fused_computation.28 | loop fusion | bytes 37748736 | tf_op jit(solution)/shard_map/squeeze | solution.py:239
  96.5 5.8 all-to-all-start
  107.7 11.7 %cholesky.103 = f32[128,128]{1,0:T(8,128)S(1)} custom-call(f32[128,128]{1,0:T(8,128)S(1)} %cholesky.263), custom_call_target="Cholesky" | custom-call | tf_op jit(solution)/shard_map/jit(cholesky)/cholesky | solution.py:71
  120.2 9.8 %custom-call.31 = f32[1,128,128]{1,2,0:T(8,128)S(1)} custom-call(f32[1,128,128]{2,1,0:T(8,128)S(1)} %get-tuple-element.96), custom_call_target="InvertDiagBlocksLowerTriangular" | custom-call | tf_op jit(solution)/shard_map/jit(cholesky)/cholesky | solution.py:71
  130.6 11.7 %cholesky.215 = f32[128,128]{1,0:T(8,128)S(1)} custom-call(f32[128,128]{1,0:T(8,128)S(1)} %cholesky.267), custom_call_target="Cholesky" | custom-call | tf_op jit(solution)/shard_map/jit(cholesky)/cholesky | solution.py:71
  142.9 10.2 %custom-call.32 = f32[1,128,128]{1,2,0:T(8,128)S(1)} custom-call(f32[1,128,128]{2,1,0:T(8,128)S(1)} %get-tuple-element.93), custom_call_target="InvertDiagBlocksLowerTriangular" | custom-call | tf_op jit(solution)/shard_map/jit(cholesky)/cholesky | solution.py:71
  153.1 101.4 %all-gather.4.cloned.1.call-done = f32[4,20,128,128]{3,2,1,0:T(8,128)} async-done(((f32[1,20,128,128]{3,2,1,0:T(8,128)}), f32[4,20,128,128]{3,2,1,0:T(8,128)}) %all-gather.4.cloned.1.call-update) | async-done | bytes 5242896 | tf_op jit(solution)/shard_map/all_gather | solution.py:163
  255.1 11.7 %cholesky.236 = f32[128,128]{1,0:T(8,128)S(1)} custom-call(f32[128,128]{1,0:T(8,128)S(1)} %cholesky.272), custom_call_target="Cholesky" | custom-call | tf_op jit(solution)/shard_map/jit(cholesky)/cholesky | solution.py:71
  266.9 9.8 %custom-call.33 = f32[1,128,128]{1,2,0:T(8,128)S(1)} custom-call(f32[1,128,128]{2,1,0:T(8,128)S(1)} %get-tuple-element.90), custom_call_target="InvertDiagBlocksLowerTriangular" | custom-call | tf_op jit(solution)/shard_map/jit(cholesky)/cholesky | solution.py:71
  277.3 11.9 %cholesky.253 = f32[128,128]{1,0:T(8,128)S(1)} custom-call(f32[128,128]{1,0:T(8,128)S(1)} %convolution_subtract_fusion.5), custom_call_target="Cholesky" | custom-call | tf_op jit(solution)/shard_map/jit(cholesky)/cholesky | solution.py:71
  297.4 13.3 %while.1 = (s32[]{:T(128)}, f32[512,512]{1,0:T(8,128)}, s32[4,2]{0,1:T(2,128)S(1)}, f32[4,128,128]{2,1,0:T(8,128)}, s32[]{:T(128)}) while((s32[]{:T(128)}, f32[512,512]{1,0:T(8,128)}, s32[4,2]{0,1:T(2,128)S(1)}, f32[4,128,128]{2,1,0:T(8,128)}, s32[]{:T(128)}) %tuple.87), condition=%wide.while_cond, body=%wide.while_body.sunk | while | flops 2 | bytes 132205 | solution.py:72
  310.7 40.1 %custom-call.34 = f32[4,128,128]{1,2,0:T(8,128)S(1)} custom-call(f32[4,128,128]{2,1,0:T(8,128)} %get-tuple-element.40), custom_call_target="InvertDiagBlocksLowerTriangular" | custom-call | tf_op jit(solution)/shard_map/jit(_solve_triangular)/triangular_solve | solution.py:72
  358.0 7.0 fusion.7
  391.0 14.0 %collective-permute-done.4 = f32[4,3,1536,128]{3,2,1,0:T(8,128)} collective-permute-done((f32[4,3,1536,128]{3,2,1,0:T(8,128)}, f32[4,3,1536,128]{3,2,1,0:T(8,128)}, u32[]{:S(2)}, u32[]{:S(2)}) %collective-permute-start.4) | collective-permute-done | bytes 9437216 | tf_op jit(solution)/shard_map/ppermute | solution.py:198
  405.0 17.7 %gather_fusion.9 = f32[200,128,128]{2,1,0:T(8,128)} fusion(f32[12,12,128,128]{3,2,1,0:T(8,128)} %bitcast.65, s32[200]{0:T(256)S(1)} %reshape.928), kind=kCustom, calls=%fused_computation.9 | custom fusion | bytes 26216000 | tf_op jit(solution)/shard_map/gather | solution.py:211
  428.8 10.4 %fusion.101 = f32[2560,512]{1,0:T(8,128)S(1)} fusion(f32[2560,512]{1,0:T(8,128)} %fusion.8, f32[512,512]{1,0:T(8,128)S(1)} %pad_maximum_fusion.3), kind=kOutput, calls=%fused_computation.329 | convolution fusion | flops 8053063680 | bytes 11534336 | tf_op jit(solution)/shard_map/dot_general | solution.py:79
  441.8 10.3 %constant_dynamic-slice_fusion.1 = (f32[1,5,10,128,128]{4,3,2,1,0:T(8,128)}, f32[5,10,128,128]{3,2,1,0:T(8,128)}, f32[5,10,128,128]{3,2,1,0:T(8,128)}, f32[5,10,128,128]{3,2,1,0:T(8,128)}) fusion(f32[4,5,10,128,128]{4,3,2,1,0:T(8,128)} %bitcast.254, s32[]{:T(128)S(6)} %select_n.717, s32[]{:T(128)S(6)} %select_n.723, s32[]{:T(128)S(6)} %select_n.721, ...), kind=kLoop, calls=%fused_computation.165 | loop fusion | bytes 26214416 | tf_op jit(solution)/shard_map/jit(dynamic_index_in_dim)/dynamic_slice | solution.py:223
  460.2 198.8 %all-reduce.5.cloned.1.call-done = f32[1280,512]{1,0:T(8,128)} async-done(((f32[1280,512]{1,0:T(8,128)}), f32[1280,512]{1,0:T(8,128)}) %all-reduce.5.cloned.1.call-update) | async-done | bytes 2621456 | tf_op jit(solution)/shard_map/psum | solution.py:13
  659.0 26.4 %fusion.98 = f32[2560,1280]{1,0:T(8,128)} fusion(f32[1280,512]{1,0:T(8,128)} %all-reduce.5.cloned.1.call-done, f32[512,512]{1,0:T(8,128)S(1)} %slice_select_fusion, f32[2048,512]{1,0:T(8,128)} %slice.223), kind=kOutput, calls=%fused_computation.326 | convolution fusion | flops 20133969920 | bytes 20971520 | tf_op jit(solution)/shard_map/dot_general | solution.py:250
  685.4 9.1 pad_maximum_fusion
  694.5 12.4 %gather_fusion.10 = f32[20,10,128,128]{3,2,1,0:T(8,128)} fusion(f32[20,10,128,128]{3,2,1,0:T(8,128)} %bitcast.255, s32[1024]{0:T(1024)S(1)} %pad_clamp_fusion.1), kind=kCustom, calls=%fused_computation.10 | custom fusion | bytes 26214480 | tf_op jit(solution)/shard_map/gather | solution.py:234
  706.9 17.7 %gather_fusion.11 = f32[200,128,128]{2,1,0:T(8,128)} fusion(f32[12,12,128,128]{3,2,1,0:T(8,128)} %bitcast.83, s32[200]{0:T(256)S(1)} %reshape.942), kind=kCustom, calls=%fused_computation.11 | custom fusion | bytes 26216000 | tf_op jit(solution)/shard_map/gather | solution.py:211
  724.6 6.5 all-to-all-start.2
  736.4 137.9 %all-to-all-done.2 = f32[4,5,10,128,128]{4,3,2,1,0:T(8,128)} async-done(((f32[4,5,10,128,128]{4,3,2,1,0:T(8,128)}), f32[4,5,10,128,128]{4,3,2,1,0:T(8,128)}, u32[]{:S(2)}, u32[]{:S(2)}) %all-to-all-start.2) | async-done | bytes 13107232 | tf_op jit(solution)/shard_map/all_to_all | solution.py:232
  874.3 12.3 %gather_fusion.12 = f32[20,10,128,128]{3,2,1,0:T(8,128)} fusion(f32[20,10,128,128]{3,2,1,0:T(8,128)} %bitcast.85, s32[1024]{0:T(1024)S(1)} %pad_clamp_fusion), kind=kCustom, calls=%fused_computation.12 | custom fusion | bytes 26214480 | tf_op jit(solution)/shard_map/gather | solution.py:234
  886.6 14.1 %add_bitcast_fusion = f32[20,128,10,128]{3,1,2,0:T(8,128)} fusion(f32[20,10,128,128]{3,2,1,0:T(8,128)} %gather_fusion.12, f32[20,10,128,128]{3,2,1,0:T(8,128)} %gather_fusion.10, pred[20,10]{1,0:T(8,128)(4,1)S(1)} %broadcast_and_fusion, pred[20,10]{1,0:T(8,128)(4,1)S(1)} %broadcast_and_fusion.1), kind=kLoop, calls=%fused_computation.23 | loop fusion | flops 9830400 | bytes 39322000 | tf_op jit(solution)/shard_map/transpose | solution.py:259
  900.7 14.2 %copy.40 = f32[20,128,10,128]{3,2,1,0:T(8,128)S(1)} copy(f32[20,128,10,128]{3,1,2,0:T(8,128)} %add_bitcast_fusion) | data formatting | bytes 26214400 | tf_op jit(solution)/shard_map/reshape | solution.py:259
  914.9 14.5 %fusion.3 = f32[2560,1280]{1,0:T(8,128)} fusion(f32[2560,1280]{1,0:T(8,128)} %fusion.98, f32[320,8,10,128]{3,2,1,0:T(8,128)S(1)} %bitcast.251, f32[2560,512]{1,0:T(8,128)S(1)} %bitcast.260, f32[2560,512]{1,0:T(8,128)} %pad_maximum_fusion.1, f32[1280]{0:T(1024)S(1)} %copy-done.3, s32[1280]{0:T(1024)S(1)} %iota_add_fusion.1, s32[2560]{0:T(1024)S(1)} %iota_add_fusion, ...), kind=kLoop, calls=%fused_computation.21 | loop fusion | flops 29491200 | bytes 49834240 | tf_op jit(solution)/shard_map/jit(_where)/select_n | solution.py:273
  (221 shorter events, 109.7 us)
Async XLA Ops:
  6.5 67.7 %all-gather.6.cloned.1.call-start = ((), (), s32[]{:S(2)}) async-start(), calls=%async_computation.5 | async-start | bytes 2162688 | tf_op jit(solution)/shard_map/all_gather | solution.py:93
  8.0 246.4 %all-gather.4.cloned.1.call-start = ((), (), s32[]{:S(2)}) async-start(), calls=%async_computation.3 | async-start | bytes 6553600 | tf_op jit(solution)/shard_map/all_gather | solution.py:163
  14.1 58.1 %collective-permute-start.2 = (f32[5,128,128]{2,1,0:T(8,128)S(1)}, f32[5,128,128]{2,1,0:T(8,128)S(1)}, u32[]{:S(2)}, u32[]{:S(2)}) collective-permute-start(f32[5,128,128]{2,1,0:T(8,128)S(1)} %get-tuple-element.86), channel_id=1, source_target_pairs={{0,12},{4,0},{8,4},{12,8},{1,13},{5,1},{9,5},{13,9},{2,14},{6,2},{... | collective-permute-start | bytes 983048 | tf_op jit(solution)/shard_map/ppermute | solution.py:152
  18.0 54.1 %collective-permute-start.1 = (f32[5,128,128]{2,1,0:T(8,128)S(1)}, f32[5,128,128]{2,1,0:T(8,128)S(1)}, u32[]{:S(2)}, u32[]{:S(2)}) collective-permute-start(f32[5,128,128]{2,1,0:T(8,128)S(1)} %get-tuple-element.84), channel_id=1, source_target_pairs={{0,8},{4,12},{8,0},{12,4},{1,9},{5,13},{9,1},{13,5},{2,10},{6,14},... | collective-permute-start | bytes 983048 | tf_op jit(solution)/shard_map/ppermute | solution.py:152
  18.5 53.6 %collective-permute-start = (f32[5,128,128]{2,1,0:T(8,128)S(1)}, f32[5,128,128]{2,1,0:T(8,128)S(1)}, u32[]{:S(2)}, u32[]{:S(2)}) collective-permute-start(f32[5,128,128]{2,1,0:T(8,128)S(1)} %get-tuple-element.85), channel_id=1, source_target_pairs={{0,4},{4,8},{8,12},{12,0},{1,5},{5,9},{9,13},{13,1},{2,6},{6,10},{... | collective-permute-start | bytes 983048 | tf_op jit(solution)/shard_map/ppermute | solution.py:152
  29.1 9.8 %copy-start.4 = (s32[2,48]{1,0:T(2,128)S(1)}, s32[2,48]{1,0:T(2,128)}, u32[]{:S(2)}) copy-start(s32[2,48]{1,0:T(2,128)} %param.7) | copy-start | bytes 1156
  29.1 10.5 %copy-start.5 = (s32[2,48]{1,0:T(2,128)S(1)}, s32[2,48]{1,0:T(2,128)}, u32[]{:S(2)}) copy-start(s32[2,48]{1,0:T(2,128)} %param.6) | copy-start | bytes 1156
  72.2 4.8 copy-start.6
  96.5 293.3 %all-to-all-start = ((f32[4,3,1536,128]{3,2,1,0:T(8,128)}), f32[4,3,1536,128]{3,2,1,0:T(8,128)}, u32[]{:S(2)}, u32[]{:S(2)}) async-start(f32[4,3,1536,128]{3,2,1,0:T(8,128)} %get-tuple-element.74), calls=%async_computation | async-start | bytes 18874368 | tf_op jit(solution)/shard_map/all_to_all | solution.py:194
  107.7 244.5 %copy-start.2 = (f32[512,512]{1,0:T(8,128)S(1)}, f32[512,512]{1,0:T(8,128)}, u32[]{:S(2)}) copy-start(f32[512,512]{1,0:T(8,128)} %fusion.19) | copy-start | bytes 3145732
  254.5 103.5 %collective-permute-start.3 = (f32[4,20,128,128]{3,2,1,0:T(8,128)}, f32[4,20,128,128]{3,2,1,0:T(8,128)}, u32[]{:S(2)}, u32[]{:S(2)}) collective-permute-start(f32[4,20,128,128]{3,2,1,0:T(8,128)} %all-gather.4.cloned.1.call-done), channel_id=1, source_target_pairs={{0,16},{16,0},{1,17},{17,1},{2,18},{18,2},{3,19},{19,3},{4,20},{20... | collective-permute-start | bytes 15728648 | tf_op jit(solution)/shard_map/ppermute | solution.py:164
  350.9 7.1 copy-start.1
  370.7 15.1 %slice-start = ((s8[5242880]{0:T(1024)(128)(4,1)}), s8[1048576]{0:T(1024)(128)(4,1)S(1)}, s32[]{:S(2)}) async-start(s8[5242880]{0:T(1024)(128)(4,1)} %bitcast.257), calls=%async_computation.6 | async-start | bytes 2097152
  376.5 9.3 slice-start.1
  385.8 4.6 copy-start.9
  385.8 4.6 copy-start.10
  385.8 4.8 copy-start.8
  389.9 15.1 %collective-permute-start.4 = (f32[4,3,1536,128]{3,2,1,0:T(8,128)}, f32[4,3,1536,128]{3,2,1,0:T(8,128)}, u32[]{:S(2)}, u32[]{:S(2)}) collective-permute-start(f32[4,3,1536,128]{3,2,1,0:T(8,128)} %all-to-all-done), channel_id=1, source_target_pairs={{0,16},{16,0},{1,17},{17,1},{2,18},{18,2},{3,19},{19,3},{4,20},{20... | collective-permute-start | bytes 28311560 | tf_op jit(solution)/shard_map/ppermute | solution.py:198
  422.7 284.2 %all-to-all-start.1 = ((f32[4,3,1536,128]{3,2,1,0:T(8,128)}), f32[4,3,1536,128]{3,2,1,0:T(8,128)}, u32[]{:S(2)}, u32[]{:S(2)}) async-start(f32[4,3,1536,128]{3,2,1,0:T(8,128)} %get-tuple-element.27), calls=%async_computation.1 | async-start | bytes 18874368 | tf_op jit(solution)/shard_map/all_to_all | solution.py:241
  428.5 230.5 %all-reduce.5.cloned.1.call-start = ((), (), s32[]{:S(2)}) async-start(), calls=%async_computation.4 | async-start | bytes 5242880 | tf_op jit(solution)/shard_map/psum | solution.py:13
  452.2 233.3 %collective-permute-start.7 = (f32[5,10,128,128]{3,2,1,0:T(8,128)}, f32[5,10,128,128]{3,2,1,0:T(8,128)}, u32[]{:S(2)}, u32[]{:S(2)}) collective-permute-start(f32[5,10,128,128]{3,2,1,0:T(8,128)} %get-tuple-element.76), channel_id=1, source_target_pairs={{0,12},{4,0},{8,4},{12,8},{1,13},{5,1},{9,5},{13,9},{2,14},{6,2},{... | collective-permute-start | bytes 9830408 | tf_op jit(solution)/shard_map/ppermute | solution.py:227
  454.5 230.9 %collective-permute-start.6 = (f32[5,10,128,128]{3,2,1,0:T(8,128)}, f32[5,10,128,128]{3,2,1,0:T(8,128)}, u32[]{:S(2)}, u32[]{:S(2)}) collective-permute-start(f32[5,10,128,128]{3,2,1,0:T(8,128)} %get-tuple-element.77), channel_id=1, source_target_pairs={{0,8},{4,12},{8,0},{12,4},{1,9},{5,13},{9,1},{13,5},{2,10},{6,14},... | collective-permute-start | bytes 9830408 | tf_op jit(solution)/shard_map/ppermute | solution.py:227
  454.5 230.9 %collective-permute-start.5 = (f32[5,10,128,128]{3,2,1,0:T(8,128)}, f32[5,10,128,128]{3,2,1,0:T(8,128)}, u32[]{:S(2)}, u32[]{:S(2)}) collective-permute-start(f32[5,10,128,128]{3,2,1,0:T(8,128)} %get-tuple-element.78), channel_id=1, source_target_pairs={{0,4},{4,8},{8,12},{12,0},{1,5},{5,9},{9,13},{13,1},{2,6},{6,10},{... | collective-permute-start | bytes 9830408 | tf_op jit(solution)/shard_map/ppermute | solution.py:227
  659.0 26.4 %copy-start = (f32[1,5,10,128,128]{4,3,2,1,0:T(8,128)S(1)}, f32[1,5,10,128,128]{4,3,2,1,0:T(8,128)}, u32[]{:S(2)}) copy-start(f32[1,5,10,128,128]{4,3,2,1,0:T(8,128)} %get-tuple-element.75) | copy-start | bytes 9830404
  724.6 6.6 copy-start.7
  724.6 149.7 %all-to-all-start.2 = ((f32[4,5,10,128,128]{4,3,2,1,0:T(8,128)}), f32[4,5,10,128,128]{4,3,2,1,0:T(8,128)}, u32[]{:S(2)}, u32[]{:S(2)}) async-start(f32[4,5,10,128,128]{4,3,2,1,0:T(8,128)} %bitcast.253), calls=%async_computation.2 | async-start | bytes 26214400 | tf_op jit(solution)/shard_map/all_to_all | solution.py:232
  874.3 40.5 %slice-start.2 = ((s8[5242880]{0:T(1024)(128)(4,1)}), s8[1048576]{0:T(1024)(128)(4,1)S(1)}, s32[]{:S(2)}) async-start(s8[5242880]{0:T(1024)(128)(4,1)} %bitcast.259), calls=%async_computation.8 | async-start | bytes 2097152
  886.6 28.2 %slice-start.3 = ((s8[5242880]{0:T(1024)(128)(4,1)}), s8[4194304]{0:T(1024)(128)(4,1)S(1)}, s32[]{:S(2)}) async-start(s8[5242880]{0:T(1024)(128)(4,1)} %bitcast.259), calls=%async_computation.9 | async-start | bytes 8388608
  900.7 14.2 %copy-start.3 = (f32[1280]{0:T(1024)S(1)}, f32[1280]{0:T(1024)}, u32[]{:S(2)}) copy-start(f32[1280]{0:T(1024)} %param.8) | copy-start | bytes 15364
Sparse Core Ops, SparseCore 0:
  10.3 61.4 all-gather.5
  74.4 180.0 all-gather.3
  459.9 199.0 all-reduce.4

commit v12 on v11

--- a/solution.py
+++ b/solution.py
@@ -213,7 +213,7 @@
         )
         return sending, col_valid, rows_of
 
-    def row_receiving(sending, col_valid, rows_of, by_permutes):
+    def row_receiving(sending, col_valid, rows_of, by_permutes, extra=None):
         placement = receiving_table(
             rows_of, my_row, row_blocks, front_row_blocks, row_cap, 0, n_row * row_cap
         )
@@ -230,16 +230,18 @@
             placement = ((my_row - source) % n_row) * row_cap + placement % row_cap
         else:
             received = lax.all_to_all(sending, "row", split_axis=0, concat_axis=0, tiled=True)
+            received, extra = lax.optimization_barrier((received, extra))
         received = received.reshape(n_row * row_cap, front_col_blocks, BLOCK, BLOCK)
         part = received.at[placement].get(mode="promise_in_bounds")
         keep = row_valid[:, None] & col_valid[None, :]
-        return part, keep
+        return part, keep, extra
 
     sending_other, col_valid_other, rows_other = row_sending(other_half, 1 - my_sub)
     sending_other, own_outgoing = lax.optimization_barrier((sending_other, outgoing[1]))
-    part_other, keep_other = row_receiving(sending_other, col_valid_other, rows_other, True)
+    part_other, keep_other, _ = row_receiving(sending_other, col_valid_other, rows_other, True)
     own_half = lax.all_to_all(own_outgoing, "col", split_axis=0, concat_axis=0, tiled=True)
     own_half, part_other = lax.optimization_barrier((own_half, part_other))
+    sending_own, col_valid_own, rows_own = row_sending(own_half, my_sub)
     theirs_start = my_group * front_cols % front_rows
     theirs_root = my_group * front_cols // front_rows
     own_rows = apply_inverse(panel_rows, inverse)
@@ -250,9 +252,9 @@
     update = lax.dot_general(
         own_rows, theirs, (((1,), (1,)), ((), ())), precision=lax.Precision.HIGHEST
     )
-    sending_own, col_valid_own, rows_own = row_sending(own_half, my_sub)
-    sending_own, update = lax.optimization_barrier((sending_own, update))
-    part_own, keep_own = row_receiving(sending_own, col_valid_own, rows_own, False)
+    part_own, keep_own, update = row_receiving(
+        sending_own, col_valid_own, rows_own, False, update
+    )
     assembled = jnp.where(keep_other[:, :, None, None], part_other, 0.0) + jnp.where(
         keep_own[:, :, None, None], part_own, 0.0
     )

time: 945 us -> 954 us (level)
  waiting for transfers between devices: 452 us -> 469 us
    ppermute x3, waiting for transfers between devices: 0.01 us -> 142 us  [row_receiving(): pieces.append(lax.ppermute(piece, 'row', pairs))]
    all_to_all x1, waiting for transfers between devices: 138 us -> 0.01 us  [row_receiving(): lax.all_to_all(sending, 'row', split_axis=0, concat_axis=0, tiled=True)]
    all_to_all x1, waiting for transfers between devices: 0.01 us -> 30.1 us  [shards(): lax.all_to_all(own_outgoing, 'col', split_axis=0, concat_axis=0, tiled=True)]
    psum x1, waiting for transfers between devices: 199 us -> 181 us  [from_root(): return lax.psum(kept, axis)]
  transfers between devices with their start and end apart: 14 -> 14, of which waited for: 4 -> 6; matrix products, arithmetic and copies ran while one was open for 35% -> 34% of each run, Pallas kernels for 0% -> 0%
where the time goes in v12:
time: 954 us; the launch traced here: 946 us
  waiting for transfers between devices  469 us (49%)
  other arithmetic  203 us (21%)
  local copies, waits for them, and re-layouts  171 us (18%)
  matrix products  42.6 us (4%)
  starting transfers between devices  27.8 us (3%)
  between operations  16.8 us (2%)
  blocking collectives  15.9 us (2%)
    psum x1, waiting for transfers between devices, from_root(): return lax.psum(kept, axis)  181 us
    ppermute x3, waiting for transfers between devices, row_receiving(): pieces.append(lax.ppermute(piece, 'row', pairs))  142 us
    all_gather x1, waiting for transfers between devices, shards(): cands = lax.all_gather(cand_rows, 'col')  102 us
    another operation x15, other arithmetic, factor_corner(): lower = jnp.linalg.cholesky(symmetric_of(corner))  82 us
    another operation x4, other arithmetic, factor_corner(): jax.scipy.linalg.solve_triangular(lower, jnp.eye(PANEL, dtype=jnp.float32...  43 us
    gather x2, local copies, waits for them, and re-layouts, row_sending(): half.at[col_index[None, None, :], row_index[:, :, None]]  35.2 us
    all_to_all x1, waiting for transfers between devices, shards(): lax.all_to_all(own_outgoing, 'col', split_axis=0, concat_axis=0, tiled=True)  30.1 us
    dot_general x1, matrix products, shards(): lax.dot_general(own_rows, theirs, (((1,), (1,)), ((), ())), precision=lax...  26.4 us
  transfers between devices with their start and end apart: 14, of which 6 were waited for; matrix products, arithmetic and copies ran while one was open for 34% of the time, Pallas kernels for 0%

profile of v12, /device:TPU:0, one launch (start us, length us, event | category | flops | bytes accessed | tf_op | source)
XLA Modules:
  0.0 946.0 jit_solution(2887763647790777401)
XLA Ops:
  19.6 9.6 %copy.32 = f32[1,1536,1536]{1,2,0:T(8,128)} copy(f32[1,1536,1536]{2,1,0:T(8,128)} %param.5) | data formatting | bytes 18874368 | tf_op args[0]
  29.3 9.7 %copy.33 = f32[1536,12,128]{2,0,1:T(8,128)} copy(f32[1536,12,128]{0,2,1:T(8,128)} %bitcast.256) | data formatting | bytes 18874368 | tf_op jit(solution)/shard_map/reshape;squeeze | solution.py:186
  42.1 13.3 %gather_fusion = f32[24,1536,128]{2,1,0:T(8,128)} fusion(f32[1536,12,128]{2,0,1:T(8,128)} %copy.33, s32[1024]{0:T(1024)S(1)} %pad_clamp_fusion.7), kind=kCustom, calls=%fused_computation | custom fusion | bytes 37748832 | tf_op jit(solution)/shard_map/gather | solution.py:190
  56.0 15.9 %psum.14 = f32[512]{0:T(512)S(1)} all-reduce(f32[512]{0:T(512)S(1)} %slice_select_fusion.1), channel_id=1, replica_groups=mesh['sub'=2,'row'=4,'col'=4] {'sub','col'}, use_global_device_ids=true, to_apply=%region_5.6 | all-reduce | flops 512 | bytes 4096 | tf_op jit(solution)/shard_map/psum | solution.py:13
  82.8 13.8 %slice_bitcast_fusion = (f32[4,3,1536,128]{3,2,1,0:T(8,128)}, f32[4,3,1536,128]{3,2,1,0:T(8,128)}) fusion(f32[2,4,3,1536,128]{4,3,2,1,0:T(8,128)} %bitcast.252), kind=kLoop, calls=%fused_computation.28 | loop fusion | bytes 37748736 | tf_op jit(solution)/shard_map/squeeze | solution.py:240
  107.8 11.7 %cholesky.103 = f32[128,128]{1,0:T(8,128)S(1)} custom-call(f32[128,128]{1,0:T(8,128)S(1)} %cholesky.263), custom_call_target="Cholesky" | custom-call | tf_op jit(solution)/shard_map/jit(cholesky)/cholesky | solution.py:71
  120.3 9.8 %custom-call.31 = f32[1,128,128]{1,2,0:T(8,128)S(1)} custom-call(f32[1,128,128]{2,1,0:T(8,128)S(1)} %get-tuple-element.96), custom_call_target="InvertDiagBlocksLowerTriangular" | custom-call | tf_op jit(solution)/shard_map/jit(cholesky)/cholesky | solution.py:71
  130.8 11.7 %cholesky.215 = f32[128,128]{1,0:T(8,128)S(1)} custom-call(f32[128,128]{1,0:T(8,128)S(1)} %cholesky.267), custom_call_target="Cholesky" | custom-call | tf_op jit(solution)/shard_map/jit(cholesky)/cholesky | solution.py:71
  143.1 10.2 %custom-call.32 = f32[1,128,128]{1,2,0:T(8,128)S(1)} custom-call(f32[1,128,128]{2,1,0:T(8,128)S(1)} %get-tuple-element.93), custom_call_target="InvertDiagBlocksLowerTriangular" | custom-call | tf_op jit(solution)/shard_map/jit(cholesky)/cholesky | solution.py:71
  153.3 101.6 %all-gather.4.cloned.1.call-done = f32[4,20,128,128]{3,2,1,0:T(8,128)} async-done(((f32[1,20,128,128]{3,2,1,0:T(8,128)}), f32[4,20,128,128]{3,2,1,0:T(8,128)}) %all-gather.4.cloned.1.call-update) | async-done | bytes 5242896 | tf_op jit(solution)/shard_map/all_gather | solution.py:163
  255.6 11.7 %cholesky.236 = f32[128,128]{1,0:T(8,128)S(1)} custom-call(f32[128,128]{1,0:T(8,128)S(1)} %cholesky.272), custom_call_target="Cholesky" | custom-call | tf_op jit(solution)/shard_map/jit(cholesky)/cholesky | solution.py:71
  267.3 9.8 %custom-call.33 = f32[1,128,128]{1,2,0:T(8,128)S(1)} custom-call(f32[1,128,128]{2,1,0:T(8,128)S(1)} %get-tuple-element.90), custom_call_target="InvertDiagBlocksLowerTriangular" | custom-call | tf_op jit(solution)/shard_map/jit(cholesky)/cholesky | solution.py:71
  277.7 11.9 %cholesky.253 = f32[128,128]{1,0:T(8,128)S(1)} custom-call(f32[128,128]{1,0:T(8,128)S(1)} %convolution_subtract_fusion.5), custom_call_target="Cholesky" | custom-call | tf_op jit(solution)/shard_map/jit(cholesky)/cholesky | solution.py:71
  298.0 10.1 %while.1 = (s32[]{:T(128)}, f32[512,512]{1,0:T(8,128)S(1)}, s32[4,2]{0,1:T(2,128)S(1)}, f32[4,128,128]{2,1,0:T(8,128)}, s32[]{:T(128)}) while((s32[]{:T(128)}, f32[512,512]{1,0:T(8,128)S(1)}, s32[4,2]{0,1:T(2,128)S(1)}, f32[4,128,128]{2,1,0:T(8,128)}, s32[]{:T(128)}) %tuple.87), condition=%wide.while_cond, body=%wide.while_body.sunk | while | flops 2 | bytes 132205 | solution.py:72
  308.1 40.1 %custom-call.34 = f32[4,128,128]{1,2,0:T(8,128)S(1)} custom-call(f32[4,128,128]{2,1,0:T(8,128)} %get-tuple-element.40), custom_call_target="InvertDiagBlocksLowerTriangular" | custom-call | tf_op jit(solution)/shard_map/jit(_solve_triangular)/triangular_solve | solution.py:72
  353.3 7.1 fusion.7
  386.6 14.0 %collective-permute-done.4 = f32[4,3,1536,128]{3,2,1,0:T(8,128)} collective-permute-done((f32[4,3,1536,128]{3,2,1,0:T(8,128)}, f32[4,3,1536,128]{3,2,1,0:T(8,128)}, u32[]{:S(2)}, u32[]{:S(2)}) %collective-permute-start.4) | collective-permute-done | bytes 9437216 | tf_op jit(solution)/shard_map/ppermute | solution.py:198
  400.6 17.7 %gather_fusion.9 = f32[200,128,128]{2,1,0:T(8,128)} fusion(f32[12,12,128,128]{3,2,1,0:T(8,128)} %bitcast.65, s32[200]{0:T(256)S(1)} %reshape.928), kind=kCustom, calls=%fused_computation.9 | custom fusion | bytes 26216000 | tf_op jit(solution)/shard_map/gather | solution.py:211
  424.5 9.2 constant_dynamic-slice_fusion.1
  437.7 70.1 %collective-permute-done.7 = f32[5,10,128,128]{3,2,1,0:T(8,128)} collective-permute-done((f32[5,10,128,128]{3,2,1,0:T(8,128)}, f32[5,10,128,128]{3,2,1,0:T(8,128)}, u32[]{:S(2)}, u32[]{:S(2)}) %collective-permute-start.7) | collective-permute-done | bytes 3276832 | tf_op jit(solution)/shard_map/ppermute | solution.py:227
  507.8 71.7 %collective-permute-done.6 = f32[5,10,128,128]{3,2,1,0:T(8,128)} collective-permute-done((f32[5,10,128,128]{3,2,1,0:T(8,128)}, f32[5,10,128,128]{3,2,1,0:T(8,128)}, u32[]{:S(2)}, u32[]{:S(2)}) %collective-permute-start.6) | collective-permute-done | bytes 3276832 | tf_op jit(solution)/shard_map/ppermute | solution.py:227
  579.5 9.0 pad_maximum_fusion
  588.4 12.4 %gather_fusion.10 = f32[20,10,128,128]{3,2,1,0:T(8,128)} fusion(f32[20,10,128,128]{3,2,1,0:T(8,128)} %bitcast.255, s32[1024]{0:T(1024)S(1)} %pad_clamp_fusion.1), kind=kCustom, calls=%fused_computation.10 | custom fusion | bytes 26214480 | tf_op jit(solution)/shard_map/gather | solution.py:235
  600.8 30.1 %all-to-all-done.1 = f32[4,3,1536,128]{3,2,1,0:T(8,128)} async-done(((f32[4,3,1536,128]{3,2,1,0:T(8,128)}), f32[4,3,1536,128]{3,2,1,0:T(8,128)}, u32[]{:S(2)}, u32[]{:S(2)}) %all-to-all-start.1) | async-done | bytes 9437216 | tf_op jit(solution)/shard_map/all_to_all | solution.py:242
  630.9 17.5 %gather_fusion.11 = f32[200,128,128]{2,1,0:T(8,128)} fusion(f32[12,12,128,128]{3,2,1,0:T(8,128)} %bitcast.83, s32[200]{0:T(256)S(1)} %reshape.942), kind=kCustom, calls=%fused_computation.11 | custom fusion | bytes 26216000 | tf_op jit(solution)/shard_map/gather | solution.py:211
  655.0 10.4 %fusion.101 = f32[2560,512]{1,0:T(8,128)S(1)} fusion(f32[2560,512]{1,0:T(8,128)} %fusion.8, f32[512,512]{1,0:T(8,128)S(1)} %copy-done.2), kind=kOutput, calls=%fused_computation.329 | convolution fusion | flops 8053063680 | bytes 11534336 | tf_op jit(solution)/shard_map/dot_general | solution.py:79
  676.6 181.2 %all-reduce.5.cloned.1.call-done = f32[1280,512]{1,0:T(8,128)} async-done(((f32[1280,512]{1,0:T(8,128)}), f32[1280,512]{1,0:T(8,128)}) %all-reduce.5.cloned.1.call-update) | async-done | bytes 2621456 | tf_op jit(solution)/shard_map/psum | solution.py:13
  857.7 26.4 %fusion.98 = f32[2560,1280]{1,0:T(8,128)} fusion(f32[1280,512]{1,0:T(8,128)} %all-reduce.5.cloned.1.call-done, f32[512,512]{1,0:T(8,128)S(1)} %slice_select_fusion, f32[2048,512]{1,0:T(8,128)} %copy-done), kind=kOutput, calls=%fused_computation.326 | convolution fusion | flops 20133969920 | bytes 20971520 | tf_op jit(solution)/shard_map/dot_general | solution.py:252
  884.2 12.3 %gather_fusion.12 = f32[20,10,128,128]{3,2,1,0:T(8,128)} fusion(f32[20,10,128,128]{3,2,1,0:T(8,128)} %bitcast.85, s32[1024]{0:T(1024)S(1)} %pad_clamp_fusion), kind=kCustom, calls=%fused_computation.12 | custom fusion | bytes 26214480 | tf_op jit(solution)/shard_map/gather | solution.py:235
  896.5 14.1 %add_bitcast_fusion = f32[20,128,10,128]{3,1,2,0:T(8,128)} fusion(f32[20,10,128,128]{3,2,1,0:T(8,128)} %gather_fusion.12, f32[20,10,128,128]{3,2,1,0:T(8,128)} %gather_fusion.10, pred[20,10]{1,0:T(8,128)(4,1)S(1)} %broadcast_and_fusion, pred[20,10]{1,0:T(8,128)(4,1)S(1)} %broadcast_and_fusion.1), kind=kLoop, calls=%fused_computation.23 | loop fusion | flops 9830400 | bytes 39322000 | tf_op jit(solution)/shard_map/transpose | solution.py:261
  910.6 14.2 %copy.40 = f32[20,128,10,128]{3,2,1,0:T(8,128)S(1)} copy(f32[20,128,10,128]{3,1,2,0:T(8,128)} %add_bitcast_fusion) | data formatting | bytes 26214400 | tf_op jit(solution)/shard_map/reshape | solution.py:261
  924.8 14.5 %fusion.3 = f32[2560,1280]{1,0:T(8,128)} fusion(f32[2560,1280]{1,0:T(8,128)} %fusion.98, f32[320,8,10,128]{3,2,1,0:T(8,128)S(1)} %bitcast.251, f32[2560,512]{1,0:T(8,128)S(1)} %bitcast.260, f32[2560,512]{1,0:T(8,128)} %pad_maximum_fusion.1, f32[1280]{0:T(1024)S(1)} %copy-done.5, s32[1280]{0:T(1024)S(1)} %iota_add_fusion.1, s32[2560]{0:T(1024)S(1)} %iota_add_fusion, ...), kind=kLoop, calls=%fused_computation.21 | loop fusion | flops 29491200 | bytes 49834240 | tf_op jit(solution)/shard_map/jit(_where)/select_n | solution.py:275
  (225 shorter events, 116.5 us)
Async XLA Ops:
  6.5 67.8 %all-gather.6.cloned.1.call-start = ((), (), s32[]{:S(2)}) async-start(), calls=%async_computation.5 | async-start | bytes 2162688 | tf_op jit(solution)/shard_map/all_gather | solution.py:93
  8.0 246.9 %all-gather.4.cloned.1.call-start = ((), (), s32[]{:S(2)}) async-start(), calls=%async_computation.3 | async-start | bytes 6553600 | tf_op jit(solution)/shard_map/all_gather | solution.py:163
  14.2 58.1 %collective-permute-start.2 = (f32[5,128,128]{2,1,0:T(8,128)S(1)}, f32[5,128,128]{2,1,0:T(8,128)S(1)}, u32[]{:S(2)}, u32[]{:S(2)}) collective-permute-start(f32[5,128,128]{2,1,0:T(8,128)S(1)} %get-tuple-element.86), channel_id=1, source_target_pairs={{0,12},{4,0},{8,4},{12,8},{1,13},{5,1},{9,5},{13,9},{2,14},{6,2},{... | collective-permute-start | bytes 983048 | tf_op jit(solution)/shard_map/ppermute | solution.py:152
  18.2 54.1 %collective-permute-start.1 = (f32[5,128,128]{2,1,0:T(8,128)S(1)}, f32[5,128,128]{2,1,0:T(8,128)S(1)}, u32[]{:S(2)}, u32[]{:S(2)}) collective-permute-start(f32[5,128,128]{2,1,0:T(8,128)S(1)} %get-tuple-element.84), channel_id=1, source_target_pairs={{0,8},{4,12},{8,0},{12,4},{1,9},{5,13},{9,1},{13,5},{2,10},{6,14},... | collective-permute-start | bytes 983048 | tf_op jit(solution)/shard_map/ppermute | solution.py:152
  18.7 53.7 %collective-permute-start = (f32[5,128,128]{2,1,0:T(8,128)S(1)}, f32[5,128,128]{2,1,0:T(8,128)S(1)}, u32[]{:S(2)}, u32[]{:S(2)}) collective-permute-start(f32[5,128,128]{2,1,0:T(8,128)S(1)} %get-tuple-element.85), channel_id=1, source_target_pairs={{0,4},{4,8},{8,12},{12,0},{1,5},{5,9},{9,13},{13,1},{2,6},{6,10},{... | collective-permute-start | bytes 983048 | tf_op jit(solution)/shard_map/ppermute | solution.py:152
  29.2 9.8 %copy-start.6 = (s32[2,48]{1,0:T(2,128)S(1)}, s32[2,48]{1,0:T(2,128)}, u32[]{:S(2)}) copy-start(s32[2,48]{1,0:T(2,128)} %param.7) | copy-start | bytes 1156
  29.3 10.5 %copy-start.7 = (s32[2,48]{1,0:T(2,128)S(1)}, s32[2,48]{1,0:T(2,128)}, u32[]{:S(2)}) copy-start(s32[2,48]{1,0:T(2,128)} %param.6) | copy-start | bytes 1156
  72.3 4.7 copy-start.8
  96.6 288.8 %all-to-all-start = ((f32[4,3,1536,128]{3,2,1,0:T(8,128)}), f32[4,3,1536,128]{3,2,1,0:T(8,128)}, u32[]{:S(2)}, u32[]{:S(2)}) async-start(f32[4,3,1536,128]{3,2,1,0:T(8,128)} %get-tuple-element.74), calls=%async_computation | async-start | bytes 18874368 | tf_op jit(solution)/shard_map/all_to_all | solution.py:194
  107.8 241.7 %copy-start.4 = (f32[512,512]{1,0:T(8,128)S(1)}, f32[512,512]{1,0:T(8,128)}, u32[]{:S(2)}) copy-start(f32[512,512]{1,0:T(8,128)} %fusion.19) | copy-start | bytes 3145732
  254.9 98.4 %collective-permute-start.3 = (f32[4,20,128,128]{3,2,1,0:T(8,128)}, f32[4,20,128,128]{3,2,1,0:T(8,128)}, u32[]{:S(2)}, u32[]{:S(2)}) collective-permute-start(f32[4,20,128,128]{3,2,1,0:T(8,128)} %all-gather.4.cloned.1.call-done), channel_id=1, source_target_pairs={{0,16},{16,0},{1,17},{17,1},{2,18},{18,2},{3,19},{19,3},{4,20},{20... | collective-permute-start | bytes 15728648 | tf_op jit(solution)/shard_map/ppermute | solution.py:164
  348.3 5.1 copy-start.1
  366.2 15.2 %slice-start = ((s8[5242880]{0:T(1024)(128)(4,1)}), s8[1048576]{0:T(1024)(128)(4,1)S(1)}, s32[]{:S(2)}) async-start(s8[5242880]{0:T(1024)(128)(4,1)} %bitcast.257), calls=%async_computation.6 | async-start | bytes 2097152
  372.1 9.3 slice-start.1
  381.4 4.6 copy-start.11
  381.4 4.6 copy-start.12
  381.4 4.8 copy-start.10
  385.4 15.1 %collective-permute-start.4 = (f32[4,3,1536,128]{3,2,1,0:T(8,128)}, f32[4,3,1536,128]{3,2,1,0:T(8,128)}, u32[]{:S(2)}, u32[]{:S(2)}) collective-permute-start(f32[4,3,1536,128]{3,2,1,0:T(8,128)} %all-to-all-done), channel_id=1, source_target_pairs={{0,16},{16,0},{1,17},{17,1},{2,18},{18,2},{3,19},{19,3},{4,20},{20... | collective-permute-start | bytes 28311560 | tf_op jit(solution)/shard_map/ppermute | solution.py:198
  418.3 212.6 %all-to-all-start.1 = ((f32[4,3,1536,128]{3,2,1,0:T(8,128)}), f32[4,3,1536,128]{3,2,1,0:T(8,128)}, u32[]{:S(2)}, u32[]{:S(2)}) async-start(f32[4,3,1536,128]{3,2,1,0:T(8,128)} %get-tuple-element.27), calls=%async_computation.1 | async-start | bytes 18874368 | tf_op jit(solution)/shard_map/all_to_all | solution.py:242
  433.7 74.1 %collective-permute-start.7 = (f32[5,10,128,128]{3,2,1,0:T(8,128)}, f32[5,10,128,128]{3,2,1,0:T(8,128)}, u32[]{:S(2)}, u32[]{:S(2)}) collective-permute-start(f32[5,10,128,128]{3,2,1,0:T(8,128)} %get-tuple-element.76), channel_id=1, source_target_pairs={{0,12},{4,0},{8,4},{12,8},{1,13},{5,1},{9,5},{13,9},{2,14},{6,2},{... | collective-permute-start | bytes 9830408 | tf_op jit(solution)/shard_map/ppermute | solution.py:227
  436.1 143.4 %collective-permute-start.6 = (f32[5,10,128,128]{3,2,1,0:T(8,128)}, f32[5,10,128,128]{3,2,1,0:T(8,128)}, u32[]{:S(2)}, u32[]{:S(2)}) collective-permute-start(f32[5,10,128,128]{3,2,1,0:T(8,128)} %get-tuple-element.77), channel_id=1, source_target_pairs={{0,8},{4,12},{8,0},{12,4},{1,9},{5,13},{9,1},{13,5},{2,10},{6,14},... | collective-permute-start | bytes 9830408 | tf_op jit(solution)/shard_map/ppermute | solution.py:227
  436.1 143.4 %collective-permute-start.5 = (f32[5,10,128,128]{3,2,1,0:T(8,128)}, f32[5,10,128,128]{3,2,1,0:T(8,128)}, u32[]{:S(2)}, u32[]{:S(2)}) collective-permute-start(f32[5,10,128,128]{3,2,1,0:T(8,128)} %get-tuple-element.78), channel_id=1, source_target_pairs={{0,4},{4,8},{8,12},{12,0},{1,5},{5,9},{9,13},{13,1},{2,6},{6,10},{... | collective-permute-start | bytes 9830408 | tf_op jit(solution)/shard_map/ppermute | solution.py:227
  648.4 6.6 copy-start.2
  648.4 235.8 %all-to-all-start.2 = ((f32[4,5,10,128,128]{4,3,2,1,0:T(8,128)}), f32[4,5,10,128,128]{4,3,2,1,0:T(8,128)}, u32[]{:S(2)}, u32[]{:S(2)}) async-start(f32[4,5,10,128,128]{4,3,2,1,0:T(8,128)} %bitcast.253), calls=%async_computation.2 | async-start | bytes 26214400 | tf_op jit(solution)/shard_map/all_to_all | solution.py:232
  654.9 202.8 %all-reduce.5.cloned.1.call-start = ((), (), s32[]{:S(2)}) async-start(), calls=%async_computation.4 | async-start | bytes 5242880 | tf_op jit(solution)/shard_map/psum | solution.py:13
  665.4 1.2 copy-start.3
  666.7 2.1 copy-start
  668.7 2.4 copy-start.9
  884.2 40.6 %slice-start.2 = ((s8[5242880]{0:T(1024)(128)(4,1)}), s8[1048576]{0:T(1024)(128)(4,1)S(1)}, s32[]{:S(2)}) async-start(s8[5242880]{0:T(1024)(128)(4,1)} %bitcast.259), calls=%async_computation.8 | async-start | bytes 2097152
  896.5 28.2 %slice-start.3 = ((s8[5242880]{0:T(1024)(128)(4,1)}), s8[4194304]{0:T(1024)(128)(4,1)S(1)}, s32[]{:S(2)}) async-start(s8[5242880]{0:T(1024)(128)(4,1)} %bitcast.259), calls=%async_computation.9 | async-start | bytes 8388608
  910.6 14.2 %copy-start.5 = (f32[1280]{0:T(1024)S(1)}, f32[1280]{0:T(1024)}, u32[]{:S(2)}) copy-start(f32[1280]{0:T(1024)} %param.8) | copy-start | bytes 15364
Sparse Core Ops, SparseCore 0:
  10.3 61.5 all-gather.5
  74.4 180.4 all-gather.3
  671.1 186.5 all-reduce.4

commit v13 on v11

--- a/solution.py
+++ b/solution.py
@@ -239,7 +239,6 @@
     sending_other, own_outgoing = lax.optimization_barrier((sending_other, outgoing[1]))
     part_other, keep_other = row_receiving(sending_other, col_valid_other, rows_other, True)
     own_half = lax.all_to_all(own_outgoing, "col", split_axis=0, concat_axis=0, tiled=True)
-    own_half, part_other = lax.optimization_barrier((own_half, part_other))
     theirs_start = my_group * front_cols % front_rows
     theirs_root = my_group * front_cols // front_rows
     own_rows = apply_inverse(panel_rows, inverse)
@@ -247,11 +246,8 @@
     own_rows = jnp.concatenate([top_rows, own_rows[PANEL:]], axis=0)
     theirs = lax.dynamic_slice_in_dim(own_rows, theirs_start, front_cols, 0)
     theirs = from_root(theirs, "row", theirs_root)
-    update = lax.dot_general(
-        own_rows, theirs, (((1,), (1,)), ((), ())), precision=lax.Precision.HIGHEST
-    )
+    own_half, part_other, theirs = lax.optimization_barrier((own_half, part_other, theirs))
     sending_own, col_valid_own, rows_own = row_sending(own_half, my_sub)
-    sending_own, update = lax.optimization_barrier((sending_own, update))
     part_own, keep_own = row_receiving(sending_own, col_valid_own, rows_own, False)
     assembled = jnp.where(keep_other[:, :, None, None], part_other, 0.0) + jnp.where(
         keep_own[:, :, None, None], part_own, 0.0
@@ -266,6 +262,9 @@
     )
     coupling_mask = (global_row[:, None] >= PANEL) & (global_col[None, :] < PANEL)
     front_part = assembled + jnp.where(coupling_mask, coupling_wide, 0.0)
+    update = lax.dot_general(
+        own_rows, theirs, (((1,), (1,)), ((), ())), precision=lax.Precision.HIGHEST
+    )
     panel_wide = jnp.concatenate(
         [own_rows, jnp.zeros((front_rows, front_cols - PANEL), jnp.float32)], axis=1
     )

time: 945 us -> 911 us (0.964)
  waiting for transfers between devices: 452 us -> 421 us
  other arithmetic: 203 us -> 184 us
  local copies, waits for them, and re-layouts: 175 us -> 185 us
    psum x1, waiting for transfers between devices: 199 us -> 19.7 us  [from_root(): return lax.psum(kept, axis)]
    ppermute x3, waiting for transfers between devices: 0.01 us -> 144 us  [row_receiving(): pieces.append(lax.ppermute(piece, 'row', pairs))]
    select_n x1 -> x0, other arithmetic: 14.5 us -> none  [shards(): jnp.where(global_col[None, :] < PANEL, panel_wide, jnp.where(global_row[:...]
    reshape x1, local copies, waits for them, and re-layouts: 14.2 us -> 26.6 us  [shards(): assembled = assembled.transpose(0, 2, 1, 3).reshape(front_rows, front_cols)]
  transfers between devices with their start and end apart: 14 -> 14, of which waited for: 4 -> 7; matrix products, arithmetic and copies ran while one was open for 35% -> 32% of each run, Pallas kernels for 0% -> 0%
where the time goes in v13:
time: 911 us; the launch traced here: 903 us
  waiting for transfers between devices  421 us (46%)
  local copies, waits for them, and re-layouts  185 us (20%)
  other arithmetic  184 us (20%)
  matrix products  50.6 us (6%)
  starting transfers between devices  29.6 us (3%)
  between operations  16.8 us (2%)
  blocking collectives  15.9 us (2%)
    ppermute x3, waiting for transfers between devices, row_receiving(): pieces.append(lax.ppermute(piece, 'row', pairs))  144 us
    all_to_all x1, waiting for transfers between devices, row_receiving(): lax.all_to_all(sending, 'row', split_axis=0, concat_axis=0, tiled=True)  138 us
    all_gather x1, waiting for transfers between devices, shards(): cands = lax.all_gather(cand_rows, 'col')  104 us
    another operation x15, other arithmetic, factor_corner(): lower = jnp.linalg.cholesky(symmetric_of(corner))  82.1 us
    another operation x4, other arithmetic, factor_corner(): jax.scipy.linalg.solve_triangular(lower, jnp.eye(PANEL, dtype=jnp.float32...  43 us
    gather x2, local copies, waits for them, and re-layouts, row_sending(): half.at[col_index[None, None, :], row_index[:, :, None]]  35.5 us
    dot_general x1, matrix products, shards(): lax.dot_general(own_rows, theirs, (((1,), (1,)), ((), ())), precision=lax...  34.2 us
    reshape x1, local copies, waits for them, and re-layouts, shards(): assembled = assembled.transpose(0, 2, 1, 3).reshape(front_rows, front_cols)  26.6 us
  transfers between devices with their start and end apart: 14, of which 7 were waited for; matrix products, arithmetic and copies ran while one was open for 32% of the time, Pallas kernels for 0%

profile of v13, /device:TPU:0, one launch (start us, length us, event | category | flops | bytes accessed | tf_op | source)
XLA Modules:
  0.0 902.6 jit_solution(14177149182014029454)
XLA Ops:
  20.5 9.6 %copy.32 = f32[1,1536,1536]{1,2,0:T(8,128)} copy(f32[1,1536,1536]{2,1,0:T(8,128)} %param.5) | data formatting | bytes 18874368 | tf_op args[0]
  31.6 9.6 %copy.33 = f32[1536,12,128]{2,0,1:T(8,128)} copy(f32[1536,12,128]{0,2,1:T(8,128)} %bitcast.252) | data formatting | bytes 18874368 | tf_op jit(solution)/shard_map/reshape;squeeze | solution.py:186
  42.9 13.2 %gather_fusion = f32[24,1536,128]{2,1,0:T(8,128)} fusion(f32[1536,12,128]{2,0,1:T(8,128)} %copy.33, s32[1024]{0:T(1024)S(1)} %pad_clamp_fusion.7), kind=kCustom, calls=%fused_computation | custom fusion | bytes 37748832 | tf_op jit(solution)/shard_map/gather | solution.py:190
  56.8 15.9 %psum.14 = f32[512]{0:T(512)S(1)} all-reduce(f32[512]{0:T(512)S(1)} %slice_select_fusion.1), channel_id=1, replica_groups=mesh['sub'=2,'row'=4,'col'=4] {'sub','col'}, use_global_device_ids=true, to_apply=%region_5.6 | all-reduce | flops 512 | bytes 4096 | tf_op jit(solution)/shard_map/psum | solution.py:13
  85.2 14.0 %slice_bitcast_fusion = (f32[4,3,1536,128]{3,2,1,0:T(8,128)}, f32[4,3,1536,128]{3,2,1,0:T(8,128)}) fusion(f32[2,4,3,1536,128]{4,3,2,1,0:T(8,128)} %bitcast.248), kind=kLoop, calls=%fused_computation.28 | loop fusion | bytes 37748736 | tf_op jit(solution)/shard_map/squeeze | solution.py:239
  110.4 11.7 %cholesky.103 = f32[128,128]{1,0:T(8,128)S(1)} custom-call(f32[128,128]{1,0:T(8,128)S(1)} %cholesky.263), custom_call_target="Cholesky" | custom-call | tf_op jit(solution)/shard_map/jit(cholesky)/cholesky | solution.py:71
  122.9 9.8 %custom-call.31 = f32[1,128,128]{1,2,0:T(8,128)S(1)} custom-call(f32[1,128,128]{2,1,0:T(8,128)S(1)} %get-tuple-element.94), custom_call_target="InvertDiagBlocksLowerTriangular" | custom-call | tf_op jit(solution)/shard_map/jit(cholesky)/cholesky | solution.py:71
  133.3 11.7 %cholesky.215 = f32[128,128]{1,0:T(8,128)S(1)} custom-call(f32[128,128]{1,0:T(8,128)S(1)} %cholesky.267), custom_call_target="Cholesky" | custom-call | tf_op jit(solution)/shard_map/jit(cholesky)/cholesky | solution.py:71
  145.7 10.0 %custom-call.32 = f32[1,128,128]{1,2,0:T(8,128)S(1)} custom-call(f32[1,128,128]{2,1,0:T(8,128)S(1)} %get-tuple-element.91), custom_call_target="InvertDiagBlocksLowerTriangular" | custom-call | tf_op jit(solution)/shard_map/jit(cholesky)/cholesky | solution.py:71
  155.7 103.7 %all-gather.4.cloned.1.call-done = f32[4,20,128,128]{3,2,1,0:T(8,128)} async-done(((f32[1,20,128,128]{3,2,1,0:T(8,128)}), f32[4,20,128,128]{3,2,1,0:T(8,128)}) %all-gather.4.cloned.1.call-update) | async-done | bytes 5242896 | tf_op jit(solution)/shard_map/all_gather | solution.py:163
  260.0 11.7 %cholesky.236 = f32[128,128]{1,0:T(8,128)S(1)} custom-call(f32[128,128]{1,0:T(8,128)S(1)} %cholesky.272), custom_call_target="Cholesky" | custom-call | tf_op jit(solution)/shard_map/jit(cholesky)/cholesky | solution.py:71
  271.7 9.8 %custom-call.33 = f32[1,128,128]{1,2,0:T(8,128)S(1)} custom-call(f32[1,128,128]{2,1,0:T(8,128)S(1)} %get-tuple-element.88), custom_call_target="InvertDiagBlocksLowerTriangular" | custom-call | tf_op jit(solution)/shard_map/jit(cholesky)/cholesky | solution.py:71
  282.2 12.1 %cholesky.253 = f32[128,128]{1,0:T(8,128)S(1)} custom-call(f32[128,128]{1,0:T(8,128)S(1)} %convolution_subtract_fusion.6), custom_call_target="Cholesky" | custom-call | tf_op jit(solution)/shard_map/jit(cholesky)/cholesky | solution.py:71
  302.8 10.8 %while.1 = (s32[]{:T(128)}, f32[512,512]{1,0:T(8,128)S(1)}, s32[4,2]{0,1:T(2,128)S(1)}, f32[4,128,128]{2,1,0:T(8,128)}, s32[]{:T(128)}) while((s32[]{:T(128)}, f32[512,512]{1,0:T(8,128)S(1)}, s32[4,2]{0,1:T(2,128)S(1)}, f32[4,128,128]{2,1,0:T(8,128)}, s32[]{:T(128)}) %tuple.85), condition=%wide.while_cond, body=%wide.while_body.sunk | while | flops 2 | bytes 132705 | solution.py:72
  313.5 40.1 %custom-call.34 = f32[4,128,128]{1,2,0:T(8,128)S(1)} custom-call(f32[4,128,128]{2,1,0:T(8,128)} %get-tuple-element.38), custom_call_target="InvertDiagBlocksLowerTriangular" | custom-call | tf_op jit(solution)/shard_map/jit(_solve_triangular)/triangular_solve | solution.py:72
  358.7 7.0 fusion.6
  391.8 14.0 %collective-permute-done.4 = f32[4,3,1536,128]{3,2,1,0:T(8,128)} collective-permute-done((f32[4,3,1536,128]{3,2,1,0:T(8,128)}, f32[4,3,1536,128]{3,2,1,0:T(8,128)}, u32[]{:S(2)}, u32[]{:S(2)}) %collective-permute-start.4) | collective-permute-done | bytes 9437216 | tf_op jit(solution)/shard_map/ppermute | solution.py:198
  405.7 17.7 %gather_fusion.9 = f32[200,128,128]{2,1,0:T(8,128)} fusion(f32[12,12,128,128]{3,2,1,0:T(8,128)} %bitcast.65, s32[200]{0:T(256)S(1)} %reshape.928), kind=kCustom, calls=%fused_computation.9 | custom fusion | bytes 26216000 | tf_op jit(solution)/shard_map/gather | solution.py:211
  429.7 9.1 %constant_dynamic-slice_fusion.1 = (f32[1,5,10,128,128]{4,3,2,1,0:T(8,128)S(1)}, f32[5,10,128,128]{3,2,1,0:T(8,128)}, f32[5,10,128,128]{3,2,1,0:T(8,128)}, f32[5,10,128,128]{3,2,1,0:T(8,128)}) fusion(f32[4,5,10,128,128]{4,3,2,1,0:T(8,128)} %bitcast.250, s32[]{:T(128)S(6)} %select_n.717, s32[]{:T(128)S(6)} %select_n.723, s32[]{:T(128)S(6)} %select_n.721, ...), kind=kLoop, calls=%fused_computation.165 | loop fusion | bytes 26214416 | tf_op jit(solution)/shard_map/jit(dynamic_index_in_dim)/dynamic_slice | solution.py:223
  443.2 10.7 %fusion.99 = f32[2560,512]{1,0:T(8,128)S(1)} fusion(f32[2560,512]{1,0:T(8,128)} %fusion.7, f32[512,512]{1,0:T(8,128)} %pad_maximum_fusion.3), kind=kOutput, calls=%fused_computation.328 | convolution fusion | flops 8053063680 | bytes 11534336 | tf_op jit(solution)/shard_map/dot_general | solution.py:79
  460.7 67.1 %collective-permute-done.5 = f32[5,10,128,128]{3,2,1,0:T(8,128)} collective-permute-done((f32[5,10,128,128]{3,2,1,0:T(8,128)}, f32[5,10,128,128]{3,2,1,0:T(8,128)}, u32[]{:S(2)}, u32[]{:S(2)}) %collective-permute-start.5) | collective-permute-done | bytes 3276832 | tf_op jit(solution)/shard_map/ppermute | solution.py:227
  527.9 76.6 %collective-permute-done.6 = f32[5,10,128,128]{3,2,1,0:T(8,128)} collective-permute-done((f32[5,10,128,128]{3,2,1,0:T(8,128)}, f32[5,10,128,128]{3,2,1,0:T(8,128)}, u32[]{:S(2)}, u32[]{:S(2)}) %collective-permute-start.6) | collective-permute-done | bytes 3276832 | tf_op jit(solution)/shard_map/ppermute | solution.py:227
  604.4 9.0 pad_maximum_fusion
  613.4 12.6 %gather_fusion.10 = f32[20,10,128,128]{3,2,1,0:T(8,128)} fusion(f32[20,10,128,128]{3,2,1,0:T(8,128)} %bitcast.251, s32[1024]{0:T(1024)S(1)} %pad_clamp_fusion.1), kind=kCustom, calls=%fused_computation.10 | custom fusion | bytes 26214480 | tf_op jit(solution)/shard_map/gather | solution.py:234
  626.0 19.7 %all-reduce.5.cloned.1.call-done = f32[1280,512]{1,0:T(8,128)} async-done(((f32[1280,512]{1,0:T(8,128)}), f32[1280,512]{1,0:T(8,128)}) %all-reduce.5.cloned.1.call-update) | async-done | bytes 2621456 | tf_op jit(solution)/shard_map/psum | solution.py:13
  645.7 17.7 %gather_fusion.11 = f32[200,128,128]{2,1,0:T(8,128)} fusion(f32[12,12,128,128]{3,2,1,0:T(8,128)} %bitcast.83, s32[200]{0:T(256)S(1)} %reshape.942), kind=kCustom, calls=%fused_computation.11 | custom fusion | bytes 26216000 | tf_op jit(solution)/shard_map/gather | solution.py:211
  663.4 6.7 all-to-all-start.2
  675.4 137.9 %all-to-all-done.2 = f32[4,5,10,128,128]{4,3,2,1,0:T(8,128)} async-done(((f32[4,5,10,128,128]{4,3,2,1,0:T(8,128)}), f32[4,5,10,128,128]{4,3,2,1,0:T(8,128)}, u32[]{:S(2)}, u32[]{:S(2)}) %all-to-all-start.2) | async-done | bytes 13107232 | tf_op jit(solution)/shard_map/all_to_all | solution.py:232
  813.3 12.6 %gather_fusion.12 = f32[20,10,128,128]{3,2,1,0:T(8,128)} fusion(f32[20,10,128,128]{3,2,1,0:T(8,128)} %bitcast.85, s32[1024]{0:T(1024)S(1)} %pad_clamp_fusion), kind=kCustom, calls=%fused_computation.12 | custom fusion | bytes 26214480 | tf_op jit(solution)/shard_map/gather | solution.py:234
  825.8 9.3 %add_bitcast_fusion = f32[20,128,10,128]{3,1,2,0:T(8,128)S(1)} fusion(f32[20,10,128,128]{3,2,1,0:T(8,128)} %gather_fusion.12, f32[20,10,128,128]{3,2,1,0:T(8,128)} %gather_fusion.10, pred[20,10]{1,0:T(8,128)(4,1)S(1)} %broadcast_and_fusion, pred[20,10]{1,0:T(8,128)(4,1)S(1)} %broadcast_and_fusion.1), kind=kLoop, calls=%fused_computation.23 | loop fusion | flops 9830400 | bytes 39322000 | tf_op jit(solution)/shard_map/transpose | solution.py:255
  835.1 26.6 %copy.40 = f32[20,128,10,128]{3,2,1,0:T(8,128)S(1)} copy(f32[20,128,10,128]{3,1,2,0:T(8,128)S(1)} %add_bitcast_fusion) | data formatting | bytes 26214400 | tf_op jit(solution)/shard_map/reshape | solution.py:255
  861.7 34.2 %fusion.1 = f32[2560,1280]{1,0:T(8,128)} fusion(f32[2560,512]{1,0:T(8,128)} %pad_maximum_fusion.1, f32[1280,512]{1,0:T(8,128)} %all-reduce.5.cloned.1.call-done, f32[320,8,10,128]{3,2,1,0:T(8,128)S(1)} %bitcast.254, f32[2560,512]{1,0:T(8,128)} %param.9, f32[1280]{0:T(1024)S(1)} %copy-done.12, s32[1280]{0:T(1024)S(1)} %iota_add_fusion.1, ...), kind=kOutput, calls=%fused_computation.19 | convolution fusion | flops 20162150400 | bytes 39348480 | tf_op jit(solution)/shard_map/dot_general | solution.py:265
  (221 shorter events, 114.6 us)
Async XLA Ops:
  6.5 13.6 %copy-start.6 = (s32[2,48]{1,0:T(2,128)S(1)}, s32[2,48]{1,0:T(2,128)}, u32[]{:S(2)}) copy-start(s32[2,48]{1,0:T(2,128)} %param.7) | copy-start | bytes 1156
  6.5 70.2 %all-gather.6.cloned.1.call-start = ((), (), s32[]{:S(2)}) async-start(), calls=%async_computation.5 | async-start | bytes 2162688 | tf_op jit(solution)/shard_map/all_gather | solution.py:93
  12.7 60.3 %collective-permute-start = (f32[5,128,128]{2,1,0:T(8,128)S(1)}, f32[5,128,128]{2,1,0:T(8,128)S(1)}, u32[]{:S(2)}, u32[]{:S(2)}) collective-permute-start(f32[5,128,128]{2,1,0:T(8,128)S(1)} %get-tuple-element.83), channel_id=1, source_target_pairs={{0,4},{4,8},{8,12},{12,0},{1,5},{5,9},{9,13},{13,1},{2,6},{6,10},{... | collective-permute-start | bytes 983048 | tf_op jit(solution)/shard_map/ppermute | solution.py:152
  15.7 57.3 %collective-permute-start.1 = (f32[5,128,128]{2,1,0:T(8,128)S(1)}, f32[5,128,128]{2,1,0:T(8,128)S(1)}, u32[]{:S(2)}, u32[]{:S(2)}) collective-permute-start(f32[5,128,128]{2,1,0:T(8,128)S(1)} %get-tuple-element.82), channel_id=1, source_target_pairs={{0,8},{4,12},{8,0},{12,4},{1,9},{5,13},{9,1},{13,5},{2,10},{6,14},... | collective-permute-start | bytes 983048 | tf_op jit(solution)/shard_map/ppermute | solution.py:152
  17.2 55.8 %collective-permute-start.2 = (f32[5,128,128]{2,1,0:T(8,128)S(1)}, f32[5,128,128]{2,1,0:T(8,128)S(1)}, u32[]{:S(2)}, u32[]{:S(2)}) collective-permute-start(f32[5,128,128]{2,1,0:T(8,128)S(1)} %get-tuple-element.84), channel_id=1, source_target_pairs={{0,12},{4,0},{8,4},{12,8},{1,13},{5,1},{9,5},{13,9},{2,14},{6,2},{... | collective-permute-start | bytes 983048 | tf_op jit(solution)/shard_map/ppermute | solution.py:152
  20.1 239.2 %all-gather.4.cloned.1.call-start = ((), (), s32[]{:S(2)}) async-start(), calls=%async_computation.3 | async-start | bytes 6553600 | tf_op jit(solution)/shard_map/all_gather | solution.py:163
  31.6 9.6 %copy-start.7 = (s32[2,48]{1,0:T(2,128)S(1)}, s32[2,48]{1,0:T(2,128)}, u32[]{:S(2)}) copy-start(s32[2,48]{1,0:T(2,128)} %param.6) | copy-start | bytes 1156
  73.0 6.4 copy-start.8
  99.2 291.4 %all-to-all-start = ((f32[4,3,1536,128]{3,2,1,0:T(8,128)}), f32[4,3,1536,128]{3,2,1,0:T(8,128)}, u32[]{:S(2)}, u32[]{:S(2)}) async-start(f32[4,3,1536,128]{3,2,1,0:T(8,128)} %get-tuple-element.72), calls=%async_computation | async-start | bytes 18874368 | tf_op jit(solution)/shard_map/all_to_all | solution.py:194
  110.4 244.5 %copy-start.5 = (f32[512,512]{1,0:T(8,128)S(1)}, f32[512,512]{1,0:T(8,128)}, u32[]{:S(2)}) copy-start(f32[512,512]{1,0:T(8,128)} %fusion.18) | copy-start | bytes 3145732
  259.3 99.4 %collective-permute-start.3 = (f32[4,20,128,128]{3,2,1,0:T(8,128)}, f32[4,20,128,128]{3,2,1,0:T(8,128)}, u32[]{:S(2)}, u32[]{:S(2)}) collective-permute-start(f32[4,20,128,128]{3,2,1,0:T(8,128)} %all-gather.4.cloned.1.call-done), channel_id=1, source_target_pairs={{0,16},{16,0},{1,17},{17,1},{2,18},{18,2},{3,19},{19,3},{4,20},{20... | collective-permute-start | bytes 15728648 | tf_op jit(solution)/shard_map/ppermute | solution.py:164
  353.7 5.1 copy-start.3
  371.5 15.1 %slice-start = ((s8[5242880]{0:T(1024)(128)(4,1)}), s8[1048576]{0:T(1024)(128)(4,1)S(1)}, s32[]{:S(2)}) async-start(s8[5242880]{0:T(1024)(128)(4,1)} %bitcast.258), calls=%async_computation.6 | async-start | bytes 2097152
  377.2 9.3 %slice-start.1 = ((s8[5242880]{0:T(1024)(128)(4,1)}), s8[4194304]{0:T(1024)(128)(4,1)S(1)}, s32[]{:S(2)}) async-start(s8[5242880]{0:T(1024)(128)(4,1)} %bitcast.258), calls=%async_computation.7 | async-start | bytes 8388608
  386.6 4.6 copy-start.11
  386.6 4.6 copy-start.13
  386.6 4.8 copy-start.10
  390.6 15.1 %collective-permute-start.4 = (f32[4,3,1536,128]{3,2,1,0:T(8,128)}, f32[4,3,1536,128]{3,2,1,0:T(8,128)}, u32[]{:S(2)}, u32[]{:S(2)}) collective-permute-start(f32[4,3,1536,128]{3,2,1,0:T(8,128)} %all-to-all-done), channel_id=1, source_target_pairs={{0,16},{16,0},{1,17},{17,1},{2,18},{18,2},{3,19},{19,3},{4,20},{20... | collective-permute-start | bytes 28311560 | tf_op jit(solution)/shard_map/ppermute | solution.py:198
  423.5 222.2 %all-to-all-start.1 = ((f32[4,3,1536,128]{3,2,1,0:T(8,128)}), f32[4,3,1536,128]{3,2,1,0:T(8,128)}, u32[]{:S(2)}, u32[]{:S(2)}) async-start(f32[4,3,1536,128]{3,2,1,0:T(8,128)} %get-tuple-element.26), calls=%async_computation.1 | async-start | bytes 18874368 | tf_op jit(solution)/shard_map/all_to_all | solution.py:241
  429.3 216.4 %all-reduce.5.cloned.1.call-start = ((), (), s32[]{:S(2)}) async-start(), calls=%async_computation.4 | async-start | bytes 5242880 | tf_op jit(solution)/shard_map/psum | solution.py:13
  438.8 89.0 %collective-permute-start.5 = (f32[5,10,128,128]{3,2,1,0:T(8,128)}, f32[5,10,128,128]{3,2,1,0:T(8,128)}, u32[]{:S(2)}, u32[]{:S(2)}) collective-permute-start(f32[5,10,128,128]{3,2,1,0:T(8,128)} %get-tuple-element.76), channel_id=1, source_target_pairs={{0,4},{4,8},{8,12},{12,0},{1,5},{5,9},{9,13},{13,1},{2,6},{6,10},{... | collective-permute-start | bytes 9830408 | tf_op jit(solution)/shard_map/ppermute | solution.py:227
  440.2 164.2 %collective-permute-start.6 = (f32[5,10,128,128]{3,2,1,0:T(8,128)}, f32[5,10,128,128]{3,2,1,0:T(8,128)}, u32[]{:S(2)}, u32[]{:S(2)}) collective-permute-start(f32[5,10,128,128]{3,2,1,0:T(8,128)} %get-tuple-element.75), channel_id=1, source_target_pairs={{0,8},{4,12},{8,0},{12,4},{1,9},{5,13},{9,1},{13,5},{2,10},{6,14},... | collective-permute-start | bytes 9830408 | tf_op jit(solution)/shard_map/ppermute | solution.py:227
  442.0 162.5 %collective-permute-start.7 = (f32[5,10,128,128]{3,2,1,0:T(8,128)}, f32[5,10,128,128]{3,2,1,0:T(8,128)}, u32[]{:S(2)}, u32[]{:S(2)}) collective-permute-start(f32[5,10,128,128]{3,2,1,0:T(8,128)} %get-tuple-element.74), channel_id=1, source_target_pairs={{0,12},{4,0},{8,4},{12,8},{1,13},{5,1},{9,5},{13,9},{2,14},{6,2},{... | collective-permute-start | bytes 9830408 | tf_op jit(solution)/shard_map/ppermute | solution.py:227
  453.8 1.2 copy-start.4
  455.1 2.0 copy-start
  457.1 1.0 copy-start.1
  663.4 6.8 copy-start.9
  663.4 7.0 copy-start.2
  663.4 149.9 %all-to-all-start.2 = ((f32[4,5,10,128,128]{4,3,2,1,0:T(8,128)}), f32[4,5,10,128,128]{4,3,2,1,0:T(8,128)}, u32[]{:S(2)}, u32[]{:S(2)}) async-start(f32[4,5,10,128,128]{4,3,2,1,0:T(8,128)} %bitcast.249), calls=%async_computation.2 | async-start | bytes 26214400 | tf_op jit(solution)/shard_map/all_to_all | solution.py:232
  835.1 26.6 %copy-start.12 = (f32[1280]{0:T(1024)S(1)}, f32[1280]{0:T(1024)}, u32[]{:S(2)}) copy-start(f32[1280]{0:T(1024)} %param.8) | copy-start | bytes 15364
Sparse Core Ops, SparseCore 0:
  20.2 56.4 all-gather.5
  78.3 180.9 all-gather.3
  460.5 185.1 all-reduce.4

commit v14 on v13

--- a/solution.py
+++ b/solution.py
@@ -79,7 +79,7 @@
     return lax.dot_general(rows, inverse, (((1,), (1,)), ((), ())), precision=lax.Precision.HIGHEST)
 
 
-def early_corner(child_piece, row_map, col_map, full_diagonal):
+def early_corner(child_piece, row_map, col_map, own_diagonal):
     n_row = lax.axis_size("row")
     n_col = lax.axis_size("col")
     n_sub = lax.axis_size("sub")
@@ -90,7 +90,10 @@
     first_rows = min(row_blocks, -(-panel_blocks // n_row))
     first_cols = min(col_blocks, -(-panel_blocks // n_col))
     piece = child_piece[: first_rows * BLOCK, : first_cols * BLOCK]
-    pieces = lax.all_gather(piece, ("sub", "row", "col"))
+    extra = own_diagonal[:PANEL].reshape(-1, first_cols * BLOCK)
+    pieces = lax.all_gather(jnp.concatenate([piece, extra], axis=0), ("sub", "row", "col"))
+    full_diagonal = pieces[0, first_rows * BLOCK :].reshape(-1)
+    pieces = pieces[:, : first_rows * BLOCK]
     pieces = pieces.reshape(n_sub, n_row, n_col, first_rows, BLOCK, first_cols, BLOCK)
     pieces = pieces.transpose(0, 1, 3, 2, 5, 4, 6).reshape(
         n_sub, n_row * first_rows, n_col * first_cols, BLOCK, BLOCK
@@ -111,7 +114,7 @@
         cb = jnp.where(cb < panel_blocks, cb, panel_blocks)
         corner = corner.at[rb[:, None], cb[None, :]].add(pieces[which])
     corner = corner[:panel_blocks, :panel_blocks].transpose(0, 2, 1, 3).reshape(PANEL, PANEL)
-    return corner + jnp.diag(full_diagonal[:PANEL])
+    return corner + jnp.diag(full_diagonal[:PANEL]), full_diagonal
 
 
 def shards(child, row_map, col_map, own_diagonal, coupling):
@@ -136,8 +139,7 @@
     my_rows_map = lax.dynamic_index_in_dim(row_map, my_sub, 0, keepdims=False)
     my_cols_map = lax.dynamic_index_in_dim(col_map, my_sub, 0, keepdims=False)
 
-    full_diagonal = from_root(own_diagonal[:PANEL], ("sub", "col"), 0)
-    corner = early_corner(child_piece, row_map, col_map, full_diagonal)
+    corner, full_diagonal = early_corner(child_piece, row_map, col_map, own_diagonal)
     global_row = my_row * front_rows + jnp.arange(front_rows, dtype=jnp.int32)
 
     panel_blocks = PANEL // BLOCK

time: 911 us -> 911 us (level)
  blocking collectives: 15.9 us -> 0 us
  waiting for transfers between devices: 421 us -> 436 us
    all_gather x1, waiting for transfers between devices: 1.66 us -> 18.1 us  [early_corner(): lax.all_gather(jnp.concatenate([piece, extra], axis=0), ('sub', 'row', 'c...]
    psum x1 -> x0, blocking collectives: 15.9 us -> none  [from_root(): return lax.psum(kept, axis)]
where the time goes in v14:
time: 911 us; the launch traced here: 903 us
  waiting for transfers between devices  436 us (48%)
  local copies, waits for them, and re-layouts  186 us (20%)
  other arithmetic  184 us (20%)
  matrix products  50.7 us (6%)
  starting transfers between devices  29.6 us (3%)
  between operations  16.8 us (2%)
    ppermute x3, waiting for transfers between devices, row_receiving(): pieces.append(lax.ppermute(piece, 'row', pairs))  144 us
    all_to_all x1, waiting for transfers between devices, row_receiving(): lax.all_to_all(sending, 'row', split_axis=0, concat_axis=0, tiled=True)  138 us
    all_gather x1, waiting for transfers between devices, shards(): cands = lax.all_gather(cand_rows, 'col')  103 us
    another operation x15, other arithmetic, factor_corner(): lower = jnp.linalg.cholesky(symmetric_of(corner))  82.1 us
    another operation x4, other arithmetic, factor_corner(): jax.scipy.linalg.solve_triangular(lower, jnp.eye(PANEL, dtype=jnp.float32...  43 us
    gather x2, local copies, waits for them, and re-layouts, row_sending(): half.at[col_index[None, None, :], row_index[:, :, None]]  35.4 us
    dot_general x1, matrix products, shards(): lax.dot_general(own_rows, theirs, (((1,), (1,)), ((), ())), precision=lax...  34.2 us
    reshape x1, local copies, waits for them, and re-layouts, shards(): assembled = assembled.transpose(0, 2, 1, 3).reshape(front_rows, front_cols)  26.6 us
  transfers between devices with their start and end apart: 14, of which 7 were waited for; matrix products, arithmetic and copies ran while one was open for 32% of the time, Pallas kernels for 0%

profile of v14, /device:TPU:0, one launch (start us, length us, event | category | flops | bytes accessed | tf_op | source)
XLA Modules:
  0.0 903.0 jit_solution(5828147148546158901)
XLA Ops:
  20.9 9.6 %copy.30 = f32[1,1536,1536]{1,2,0:T(8,128)} copy(f32[1,1536,1536]{2,1,0:T(8,128)} %param.5) | data formatting | bytes 18874368 | tf_op args[0]
  32.3 9.6 %copy.31 = f32[1536,12,128]{2,0,1:T(8,128)} copy(f32[1536,12,128]{0,2,1:T(8,128)} %bitcast.256) | data formatting | bytes 18874368 | tf_op jit(solution)/shard_map/reshape;squeeze | solution.py:188
  43.6 13.3 %gather_fusion = f32[24,1536,128]{2,1,0:T(8,128)} fusion(f32[1536,12,128]{2,0,1:T(8,128)} %copy.31, s32[1024]{0:T(1024)S(1)} %pad_clamp_fusion.7), kind=kCustom, calls=%fused_computation | custom fusion | bytes 37748832 | tf_op jit(solution)/shard_map/gather | solution.py:192
  59.3 18.1 %all-gather.7.cloned.1.call-done = f32[32,132,128]{2,1,0:T(8,128)} async-done(((f32[1,132,128]{2,1,0:T(8,128)}), f32[32,132,128]{2,1,0:T(8,128)}) %all-gather.7.cloned.1.call-update) | async-done | bytes 2162704 | tf_op jit(solution)/shard_map/all_gather | solution.py:94
  86.5 13.9 %slice_bitcast_fusion = (f32[4,3,1536,128]{3,2,1,0:T(8,128)}, f32[4,3,1536,128]{3,2,1,0:T(8,128)}) fusion(f32[2,4,3,1536,128]{4,3,2,1,0:T(8,128)} %bitcast.252), kind=kLoop, calls=%fused_computation.28 | loop fusion | bytes 37748736 | tf_op jit(solution)/shard_map/squeeze | solution.py:241
  111.6 11.7 %cholesky.103 = f32[128,128]{1,0:T(8,128)S(1)} custom-call(f32[128,128]{1,0:T(8,128)S(1)} %cholesky.263), custom_call_target="Cholesky" | custom-call | tf_op jit(solution)/shard_map/jit(cholesky)/cholesky | solution.py:71
  124.1 9.8 %custom-call.31 = f32[1,128,128]{1,2,0:T(8,128)S(1)} custom-call(f32[1,128,128]{2,1,0:T(8,128)S(1)} %get-tuple-element.94), custom_call_target="InvertDiagBlocksLowerTriangular" | custom-call | tf_op jit(solution)/shard_map/jit(cholesky)/cholesky | solution.py:71
  134.5 11.7 %cholesky.215 = f32[128,128]{1,0:T(8,128)S(1)} custom-call(f32[128,128]{1,0:T(8,128)S(1)} %cholesky.267), custom_call_target="Cholesky" | custom-call | tf_op jit(solution)/shard_map/jit(cholesky)/cholesky | solution.py:71
  146.9 10.0 %custom-call.32 = f32[1,128,128]{1,2,0:T(8,128)S(1)} custom-call(f32[1,128,128]{2,1,0:T(8,128)S(1)} %get-tuple-element.91), custom_call_target="InvertDiagBlocksLowerTriangular" | custom-call | tf_op jit(solution)/shard_map/jit(cholesky)/cholesky | solution.py:71
  156.9 102.7 %all-gather.5.cloned.1.call-done = f32[4,20,128,128]{3,2,1,0:T(8,128)} async-done(((f32[1,20,128,128]{3,2,1,0:T(8,128)}), f32[4,20,128,128]{3,2,1,0:T(8,128)}) %all-gather.5.cloned.1.call-update) | async-done | bytes 5242896 | tf_op jit(solution)/shard_map/all_gather | solution.py:165
  260.3 11.7 %cholesky.236 = f32[128,128]{1,0:T(8,128)S(1)} custom-call(f32[128,128]{1,0:T(8,128)S(1)} %cholesky.272), custom_call_target="Cholesky" | custom-call | tf_op jit(solution)/shard_map/jit(cholesky)/cholesky | solution.py:71
  272.0 9.8 %custom-call.33 = f32[1,128,128]{1,2,0:T(8,128)S(1)} custom-call(f32[1,128,128]{2,1,0:T(8,128)S(1)} %get-tuple-element.88), custom_call_target="InvertDiagBlocksLowerTriangular" | custom-call | tf_op jit(solution)/shard_map/jit(cholesky)/cholesky | solution.py:71
  282.4 12.1 %cholesky.253 = f32[128,128]{1,0:T(8,128)S(1)} custom-call(f32[128,128]{1,0:T(8,128)S(1)} %convolution_subtract_fusion.6), custom_call_target="Cholesky" | custom-call | tf_op jit(solution)/shard_map/jit(cholesky)/cholesky | solution.py:71
  303.0 10.8 %while.1 = (s32[]{:T(128)}, f32[512,512]{1,0:T(8,128)S(1)}, s32[4,2]{0,1:T(2,128)S(1)}, f32[4,128,128]{2,1,0:T(8,128)}, s32[]{:T(128)}) while((s32[]{:T(128)}, f32[512,512]{1,0:T(8,128)S(1)}, s32[4,2]{0,1:T(2,128)S(1)}, f32[4,128,128]{2,1,0:T(8,128)}, s32[]{:T(128)}) %tuple.85), condition=%wide.while_cond, body=%wide.while_body.sunk | while | flops 2 | bytes 132705 | solution.py:72
  313.8 40.1 %custom-call.34 = f32[4,128,128]{1,2,0:T(8,128)S(1)} custom-call(f32[4,128,128]{2,1,0:T(8,128)} %get-tuple-element.38), custom_call_target="InvertDiagBlocksLowerTriangular" | custom-call | tf_op jit(solution)/shard_map/jit(_solve_triangular)/triangular_solve | solution.py:72
  359.0 7.0 fusion.6
  392.1 14.0 %collective-permute-done.4 = f32[4,3,1536,128]{3,2,1,0:T(8,128)} collective-permute-done((f32[4,3,1536,128]{3,2,1,0:T(8,128)}, f32[4,3,1536,128]{3,2,1,0:T(8,128)}, u32[]{:S(2)}, u32[]{:S(2)}) %collective-permute-start.4) | collective-permute-done | bytes 9437216 | tf_op jit(solution)/shard_map/ppermute | solution.py:200
  406.0 17.7 %gather_fusion.9 = f32[200,128,128]{2,1,0:T(8,128)} fusion(f32[12,12,128,128]{3,2,1,0:T(8,128)} %bitcast.66, s32[200]{0:T(256)S(1)} %reshape.938), kind=kCustom, calls=%fused_computation.9 | custom fusion | bytes 26216000 | tf_op jit(solution)/shard_map/gather | solution.py:213
  430.0 9.1 %constant_dynamic-slice_fusion.1 = (f32[1,5,10,128,128]{4,3,2,1,0:T(8,128)S(1)}, f32[5,10,128,128]{3,2,1,0:T(8,128)}, f32[5,10,128,128]{3,2,1,0:T(8,128)}, f32[5,10,128,128]{3,2,1,0:T(8,128)}) fusion(f32[4,5,10,128,128]{4,3,2,1,0:T(8,128)} %bitcast.254, s32[]{:T(128)S(6)} %select_n.707, s32[]{:T(128)S(6)} %select_n.713, s32[]{:T(128)S(6)} %select_n.711, ...), kind=kLoop, calls=%fused_computation.166 | loop fusion | bytes 26214416 | tf_op jit(solution)/shard_map/jit(dynamic_index_in_dim)/dynamic_slice | solution.py:225
  443.5 10.7 %fusion.99 = f32[2560,512]{1,0:T(8,128)S(1)} fusion(f32[2560,512]{1,0:T(8,128)} %fusion.7, f32[512,512]{1,0:T(8,128)} %pad_maximum_fusion.3), kind=kOutput, calls=%fused_computation.330 | convolution fusion | flops 8053063680 | bytes 11534336 | tf_op jit(solution)/shard_map/dot_general | solution.py:79
  461.1 67.1 %collective-permute-done.5 = f32[5,10,128,128]{3,2,1,0:T(8,128)} collective-permute-done((f32[5,10,128,128]{3,2,1,0:T(8,128)}, f32[5,10,128,128]{3,2,1,0:T(8,128)}, u32[]{:S(2)}, u32[]{:S(2)}) %collective-permute-start.5) | collective-permute-done | bytes 3276832 | tf_op jit(solution)/shard_map/ppermute | solution.py:229
  528.1 76.9 %collective-permute-done.6 = f32[5,10,128,128]{3,2,1,0:T(8,128)} collective-permute-done((f32[5,10,128,128]{3,2,1,0:T(8,128)}, f32[5,10,128,128]{3,2,1,0:T(8,128)}, u32[]{:S(2)}, u32[]{:S(2)}) %collective-permute-start.6) | collective-permute-done | bytes 3276832 | tf_op jit(solution)/shard_map/ppermute | solution.py:229
  605.0 9.0 pad_maximum_fusion
  614.0 12.6 %gather_fusion.10 = f32[20,10,128,128]{3,2,1,0:T(8,128)} fusion(f32[20,10,128,128]{3,2,1,0:T(8,128)} %bitcast.255, s32[1024]{0:T(1024)S(1)} %pad_clamp_fusion.1), kind=kCustom, calls=%fused_computation.10 | custom fusion | bytes 26214480 | tf_op jit(solution)/shard_map/gather | solution.py:236
  626.6 19.6 %all-reduce.5.cloned.1.call-done = f32[1280,512]{1,0:T(8,128)} async-done(((f32[1280,512]{1,0:T(8,128)}), f32[1280,512]{1,0:T(8,128)}) %all-reduce.5.cloned.1.call-update) | async-done | bytes 2621456 | tf_op jit(solution)/shard_map/psum | solution.py:13
  646.2 17.7 %gather_fusion.11 = f32[200,128,128]{2,1,0:T(8,128)} fusion(f32[12,12,128,128]{3,2,1,0:T(8,128)} %bitcast.84, s32[200]{0:T(256)S(1)} %reshape.952), kind=kCustom, calls=%fused_computation.11 | custom fusion | bytes 26216000 | tf_op jit(solution)/shard_map/gather | solution.py:213
  663.9 6.7 all-to-all-start.2
  675.9 137.9 %all-to-all-done.2 = f32[4,5,10,128,128]{4,3,2,1,0:T(8,128)} async-done(((f32[4,5,10,128,128]{4,3,2,1,0:T(8,128)}), f32[4,5,10,128,128]{4,3,2,1,0:T(8,128)}, u32[]{:S(2)}, u32[]{:S(2)}) %all-to-all-start.2) | async-done | bytes 13107232 | tf_op jit(solution)/shard_map/all_to_all | solution.py:234
  813.8 12.4 %gather_fusion.12 = f32[20,10,128,128]{3,2,1,0:T(8,128)} fusion(f32[20,10,128,128]{3,2,1,0:T(8,128)} %bitcast.86, s32[1024]{0:T(1024)S(1)} %pad_clamp_fusion), kind=kCustom, calls=%fused_computation.12 | custom fusion | bytes 26214480 | tf_op jit(solution)/shard_map/gather | solution.py:236
  826.2 9.3 %add_bitcast_fusion = f32[20,128,10,128]{3,1,2,0:T(8,128)S(1)} fusion(f32[20,10,128,128]{3,2,1,0:T(8,128)} %gather_fusion.12, f32[20,10,128,128]{3,2,1,0:T(8,128)} %gather_fusion.10, pred[20,10]{1,0:T(8,128)(4,1)S(1)} %broadcast_and_fusion, pred[20,10]{1,0:T(8,128)(4,1)S(1)} %broadcast_and_fusion.1), kind=kLoop, calls=%fused_computation.23 | loop fusion | flops 9830400 | bytes 39322000 | tf_op jit(solution)/shard_map/transpose | solution.py:257
  835.5 26.6 %copy.38 = f32[20,128,10,128]{3,2,1,0:T(8,128)S(1)} copy(f32[20,128,10,128]{3,1,2,0:T(8,128)S(1)} %add_bitcast_fusion) | data formatting | bytes 26214400 | tf_op jit(solution)/shard_map/reshape | solution.py:257
  862.1 34.2 %fusion.1 = f32[2560,1280]{1,0:T(8,128)} fusion(f32[2560,512]{1,0:T(8,128)} %pad_maximum_fusion.1, f32[1280,512]{1,0:T(8,128)} %all-reduce.5.cloned.1.call-done, f32[320,8,10,128]{3,2,1,0:T(8,128)S(1)} %bitcast.258, f32[2560,512]{1,0:T(8,128)} %param.9, f32[1280]{0:T(1024)S(1)} %copy-done.12, s32[1280]{0:T(1024)S(1)} %iota_add_fusion.1, ...), kind=kOutput, calls=%fused_computation.19 | convolution fusion | flops 20162150400 | bytes 39348480 | tf_op jit(solution)/shard_map/dot_general | solution.py:267
  (222 shorter events, 113.7 us)
Async XLA Ops:
  6.5 14.3 %copy-start.6 = (s32[2,48]{1,0:T(2,128)S(1)}, s32[2,48]{1,0:T(2,128)}, u32[]{:S(2)}) copy-start(s32[2,48]{1,0:T(2,128)} %param.7) | copy-start | bytes 1156
  6.5 70.9 %all-gather.7.cloned.1.call-start = ((), (), s32[]{:S(2)}) async-start(), calls=%async_computation.5 | async-start | bytes 2297856 | tf_op jit(solution)/shard_map/all_gather | solution.py:94
  12.7 44.5 %collective-permute-start = (f32[5,128,128]{2,1,0:T(8,128)S(1)}, f32[5,128,128]{2,1,0:T(8,128)S(1)}, u32[]{:S(2)}, u32[]{:S(2)}) collective-permute-start(f32[5,128,128]{2,1,0:T(8,128)S(1)} %get-tuple-element.83), channel_id=1, source_target_pairs={{0,4},{4,8},{8,12},{12,0},{1,5},{5,9},{9,13},{13,1},{2,6},{6,10},{... | collective-permute-start | bytes 983048 | tf_op jit(solution)/shard_map/ppermute | solution.py:154
  15.7 41.5 %collective-permute-start.1 = (f32[5,128,128]{2,1,0:T(8,128)S(1)}, f32[5,128,128]{2,1,0:T(8,128)S(1)}, u32[]{:S(2)}, u32[]{:S(2)}) collective-permute-start(f32[5,128,128]{2,1,0:T(8,128)S(1)} %get-tuple-element.82), channel_id=1, source_target_pairs={{0,8},{4,12},{8,0},{12,4},{1,9},{5,13},{9,1},{13,5},{2,10},{6,14},... | collective-permute-start | bytes 983048 | tf_op jit(solution)/shard_map/ppermute | solution.py:154
  17.2 40.0 %collective-permute-start.2 = (f32[5,128,128]{2,1,0:T(8,128)S(1)}, f32[5,128,128]{2,1,0:T(8,128)S(1)}, u32[]{:S(2)}, u32[]{:S(2)}) collective-permute-start(f32[5,128,128]{2,1,0:T(8,128)S(1)} %get-tuple-element.84), channel_id=1, source_target_pairs={{0,12},{4,0},{8,4},{12,8},{1,13},{5,1},{9,5},{13,9},{2,14},{6,2},{... | collective-permute-start | bytes 983048 | tf_op jit(solution)/shard_map/ppermute | solution.py:154
  20.8 238.8 %all-gather.5.cloned.1.call-start = ((), (), s32[]{:S(2)}) async-start(), calls=%async_computation.3 | async-start | bytes 6553600 | tf_op jit(solution)/shard_map/all_gather | solution.py:165
  32.3 9.6 %copy-start.7 = (s32[2,48]{1,0:T(2,128)S(1)}, s32[2,48]{1,0:T(2,128)}, u32[]{:S(2)}) copy-start(s32[2,48]{1,0:T(2,128)} %param.6) | copy-start | bytes 1156
  57.1 23.0 %copy-start.8 = (pred[20]{0:T(512)(128)(4,1)}, pred[20]{0:T(512)(128)(4,1)S(1)}, u32[]{:S(2)}) copy-start(pred[20]{0:T(512)(128)(4,1)S(1)} %broadcast_compare_fusion.5) | copy-start | bytes 64
  100.4 290.5 %all-to-all-start = ((f32[4,3,1536,128]{3,2,1,0:T(8,128)}), f32[4,3,1536,128]{3,2,1,0:T(8,128)}, u32[]{:S(2)}, u32[]{:S(2)}) async-start(f32[4,3,1536,128]{3,2,1,0:T(8,128)} %get-tuple-element.72), calls=%async_computation | async-start | bytes 18874368 | tf_op jit(solution)/shard_map/all_to_all | solution.py:196
  111.6 243.6 %copy-start.5 = (f32[512,512]{1,0:T(8,128)S(1)}, f32[512,512]{1,0:T(8,128)}, u32[]{:S(2)}) copy-start(f32[512,512]{1,0:T(8,128)} %fusion.18) | copy-start | bytes 3145732
  259.6 99.4 %collective-permute-start.3 = (f32[4,20,128,128]{3,2,1,0:T(8,128)}, f32[4,20,128,128]{3,2,1,0:T(8,128)}, u32[]{:S(2)}, u32[]{:S(2)}) collective-permute-start(f32[4,20,128,128]{3,2,1,0:T(8,128)} %all-gather.5.cloned.1.call-done), channel_id=1, source_target_pairs={{0,16},{16,0},{1,17},{17,1},{2,18},{18,2},{3,19},{19,3},{4,20},{20... | collective-permute-start | bytes 15728648 | tf_op jit(solution)/shard_map/ppermute | solution.py:166
  353.9 5.1 copy-start.3
  371.8 15.1 %slice-start = ((s8[5242880]{0:T(1024)(128)(4,1)}), s8[1048576]{0:T(1024)(128)(4,1)S(1)}, s32[]{:S(2)}) async-start(s8[5242880]{0:T(1024)(128)(4,1)} %bitcast.262), calls=%async_computation.6 | async-start | bytes 2097152
  377.5 9.3 %slice-start.1 = ((s8[5242880]{0:T(1024)(128)(4,1)}), s8[4194304]{0:T(1024)(128)(4,1)S(1)}, s32[]{:S(2)}) async-start(s8[5242880]{0:T(1024)(128)(4,1)} %bitcast.262), calls=%async_computation.7 | async-start | bytes 8388608
  386.9 4.6 copy-start.11
  386.9 4.6 copy-start.13
  386.9 4.8 copy-start.10
  390.9 15.1 %collective-permute-start.4 = (f32[4,3,1536,128]{3,2,1,0:T(8,128)}, f32[4,3,1536,128]{3,2,1,0:T(8,128)}, u32[]{:S(2)}, u32[]{:S(2)}) collective-permute-start(f32[4,3,1536,128]{3,2,1,0:T(8,128)} %all-to-all-done), channel_id=1, source_target_pairs={{0,16},{16,0},{1,17},{17,1},{2,18},{18,2},{3,19},{19,3},{4,20},{20... | collective-permute-start | bytes 28311560 | tf_op jit(solution)/shard_map/ppermute | solution.py:200
  423.8 222.5 %all-to-all-start.1 = ((f32[4,3,1536,128]{3,2,1,0:T(8,128)}), f32[4,3,1536,128]{3,2,1,0:T(8,128)}, u32[]{:S(2)}, u32[]{:S(2)}) async-start(f32[4,3,1536,128]{3,2,1,0:T(8,128)} %get-tuple-element.26), calls=%async_computation.1 | async-start | bytes 18874368 | tf_op jit(solution)/shard_map/all_to_all | solution.py:243
  429.6 216.7 %all-reduce.5.cloned.1.call-start = ((), (), s32[]{:S(2)}) async-start(), calls=%async_computation.4 | async-start | bytes 5242880 | tf_op jit(solution)/shard_map/psum | solution.py:13
  439.1 89.0 %collective-permute-start.5 = (f32[5,10,128,128]{3,2,1,0:T(8,128)}, f32[5,10,128,128]{3,2,1,0:T(8,128)}, u32[]{:S(2)}, u32[]{:S(2)}) collective-permute-start(f32[5,10,128,128]{3,2,1,0:T(8,128)} %get-tuple-element.76), channel_id=1, source_target_pairs={{0,4},{4,8},{8,12},{12,0},{1,5},{5,9},{9,13},{13,1},{2,6},{6,10},{... | collective-permute-start | bytes 9830408 | tf_op jit(solution)/shard_map/ppermute | solution.py:229
  440.7 164.3 %collective-permute-start.6 = (f32[5,10,128,128]{3,2,1,0:T(8,128)}, f32[5,10,128,128]{3,2,1,0:T(8,128)}, u32[]{:S(2)}, u32[]{:S(2)}) collective-permute-start(f32[5,10,128,128]{3,2,1,0:T(8,128)} %get-tuple-element.75), channel_id=1, source_target_pairs={{0,8},{4,12},{8,0},{12,4},{1,9},{5,13},{9,1},{13,5},{2,10},{6,14},... | collective-permute-start | bytes 9830408 | tf_op jit(solution)/shard_map/ppermute | solution.py:229
  442.5 162.5 %collective-permute-start.7 = (f32[5,10,128,128]{3,2,1,0:T(8,128)}, f32[5,10,128,128]{3,2,1,0:T(8,128)}, u32[]{:S(2)}, u32[]{:S(2)}) collective-permute-start(f32[5,10,128,128]{3,2,1,0:T(8,128)} %get-tuple-element.74), channel_id=1, source_target_pairs={{0,12},{4,0},{8,4},{12,8},{1,13},{5,1},{9,5},{13,9},{2,14},{6,2},{... | collective-permute-start | bytes 9830408 | tf_op jit(solution)/shard_map/ppermute | solution.py:229
  454.2 1.2 copy-start.4
  455.4 2.0 copy-start
  457.4 1.0 copy-start.1
  663.9 6.8 copy-start.9
  663.9 7.0 copy-start.2
  663.9 149.9 %all-to-all-start.2 = ((f32[4,5,10,128,128]{4,3,2,1,0:T(8,128)}), f32[4,5,10,128,128]{4,3,2,1,0:T(8,128)}, u32[]{:S(2)}, u32[]{:S(2)}) async-start(f32[4,5,10,128,128]{4,3,2,1,0:T(8,128)} %bitcast.253), calls=%async_computation.2 | async-start | bytes 26214400 | tf_op jit(solution)/shard_map/all_to_all | solution.py:234
  835.5 26.6 %copy-start.12 = (f32[1280]{0:T(1024)S(1)}, f32[1280]{0:T(1024)}, u32[]{:S(2)}) copy-start(f32[1280]{0:T(1024)} %param.8) | copy-start | bytes 15364
Sparse Core Ops, SparseCore 0:
  20.9 56.4 all-gather.6
  79.0 180.5 all-gather.4
  460.8 185.3 all-reduce.4
